TPU v7x, 256 devices: a whole 4x4x8 slice. The times are simulated.
256 devices in a mesh: seq: 128 (over x, y, z), head: 2 (over core).
Axes of the slice: x: 4, y: 4, z: 8, core: 2. Of those that a mesh axis runs over, the one named last changes fastest.
Arguments:
- queries: bfloat16 [32768, 4096], P('seq', 'head'), may hold values from -12 to 12
- key_states: bfloat16 [32768, 1024], P('seq', 'head'), may hold values from -12 to 12
- value_states: bfloat16 [32768, 1024], P('seq', 'head'), may hold values from -6 to 6
- positions: int32 [3, 32768], P(None, 'seq'), may hold values from 0 to 4095
- random_blocks: int32 [512, 8, 3], P('seq', 'head'), may hold values from 0 to 511, as said below
- global_blocks: int32 [2], replicated, may hold values from 0 to 511
- out_grad: bfloat16 [32768, 4096], P('seq', 'head'), may hold values from -6 to 6
Outputs:
- attended: bfloat16 [32768, 4096], P('seq', 'head')
- query_grad: bfloat16 [32768, 4096], P('seq', 'head')
- key_grad: bfloat16 [32768, 1024], P('seq', 'head')
- value_grad: bfloat16 [32768, 1024], P('seq', 'head')
Inputs may be any that keep to these rules, and one draw needn't show every extreme that they name: `random_blocks`: for each index of seq and each index of head (its 4 block rows and 4 key-value heads), at most 2 of its random blocks lie in the blocks of any one index of seq, and exactly 2 in one of them.
All inputs are finite; a program needn't handle non-finite values.
Results may differ from a plain program's by a relative error of at most 0.013.
The roundings to bfloat16 on the way count: a program that leaves them out, or rounds other values in their place, can miss the bound.
Values may be sent and summed in bfloat16 or wider, within the bound.
No kernel may reach another device: no remote copies, remote signals or barrier semaphores. Data moves between devices by JAX's collectives and lax.ppermute only.
A program may use at most 128 MiB of HBM per device.

v0:
```python
import math

import jax
import jax.numpy as jnp
from jax import lax
from jax.sharding import PartitionSpec as P

HD = 128
GROUP = 4
BLK = 64
GLOB = 2
RND = 3


NEG_FILL = -1e30
ROPE_BASE = 1000000.0


def extended(array, sides, width):
    for axis, dim in sides:
        devices, length = (lax.axis_size(axis), array.shape[dim])
        up = [(i, (i + 1) % devices) for i in range(devices - 1)]
        down = [(j, i) for i, j in up]
        last = lax.slice_in_dim(array, length - width, length, axis=dim)
        leading = lax.slice_in_dim(array, 0, width, axis=dim)
        before = lax.ppermute(last, axis, up)
        after = lax.ppermute(leading, axis, down)
        array = jnp.concatenate([before, array, after], axis=dim)
    return array


def spread(block, axis, source):
    block = jnp.where(lax.axis_index(axis) == source, block, jnp.zeros_like(block))
    return lax.psum(block, axis)


def shifted(array, axis, by):
    devices = lax.axis_size(axis)
    pairs = [(i, i + by) for i in range(devices) if 0 <= i + by < devices]
    return lax.ppermute(array, axis, pairs)


def tables(positions):
    half_dim = HD // 2
    freq_ids = jnp.arange(half_dim)
    inv_freq = jnp.power(jnp.float32(ROPE_BASE), -2.0 * freq_ids.astype(jnp.float32) / HD)
    pos_float = positions.astype(jnp.float32)
    chosen = jnp.where(
        (freq_ids % 3 == 0)[None, :],
        pos_float[0][:, None],
        jnp.where((freq_ids % 3 == 1)[None, :], pos_float[1][:, None], pos_float[2][:, None]),
    )
    angles = chosen * inv_freq[None, :]
    return (jnp.cos(angles), jnp.sin(angles))


def rotate(states, cosines, sine_vals):
    half_dim = HD // 2
    first_half = states[..., :half_dim]
    second_half = states[..., half_dim:]
    cos_b = cosines[:, None, :]
    sin_b = sine_vals[:, None, :]
    return jnp.concatenate(
        [first_half * cos_b - second_half * sin_b, second_half * cos_b + first_half * sin_b],
        axis=-1,
    )


def unrotate(states, cosines, sine_vals):
    half_dim = HD // 2
    first_half = states[..., :half_dim]
    second_half = states[..., half_dim:]
    cos_b = cosines[:, None, :]
    sin_b = sine_vals[:, None, :]
    return jnp.concatenate(
        [first_half * cos_b + second_half * sin_b, second_half * cos_b - first_half * sin_b],
        axis=-1,
    )


def attend(query_block_view, key_block_view, value_block_view, gradient_block_view, key_mask):
    score_scale = 1.0 / math.sqrt(HD)
    logit_scores = (
        jnp.einsum(
            "mtyp,mop->myto", query_block_view, key_block_view, preferred_element_type=jnp.float32
        )
        * score_scale
    )
    logit_scores = jnp.where(key_mask[:, None, None, :], logit_scores, NEG_FILL)
    row_max = jnp.max(logit_scores, axis=-1, keepdims=True)
    exponent = jnp.exp(logit_scores - row_max)
    probability = exponent / jnp.sum(exponent, axis=-1, keepdims=True)
    attention_weights = probability.astype(jnp.bfloat16)
    attended = jnp.einsum(
        "ywiu,yuz->yiwz", attention_weights, value_block_view, preferred_element_type=jnp.float32
    ).astype(jnp.bfloat16)
    weight_gradient = jnp.einsum(
        "mtyp,mop->myto", gradient_block_view, value_block_view, preferred_element_type=jnp.float32
    )
    row_delta = jnp.sum(
        gradient_block_view.astype(jnp.float32) * attended.astype(jnp.float32), axis=-1
    )
    row_delta = jnp.transpose(row_delta, (0, 2, 1))[..., None]
    score_gradient = (probability * (weight_gradient - row_delta) * score_scale).astype(
        jnp.bfloat16
    )
    value_portion = jnp.einsum(
        "pcht,phca->pta", attention_weights, gradient_block_view, preferred_element_type=jnp.float32
    )
    key_portion = jnp.einsum(
        "pcht,phca->pta", score_gradient, query_block_view, preferred_element_type=jnp.float32
    )
    query_portion = jnp.einsum(
        "ywiu,yuz->yiwz", score_gradient, key_block_view, preferred_element_type=jnp.float32
    )
    return (attended, query_portion, key_portion, value_portion)


def split_slots(portion, block_rows):
    key_slots = 3 + GLOB + RND
    per_slot = portion.reshape(block_rows, key_slots, BLK, HD)
    window_sum = jnp.pad(per_slot[:, 0], ((0, 2), (0, 0), (0, 0)))
    window_sum = window_sum + jnp.pad(per_slot[:, 1], ((1, 1), (0, 0), (0, 0)))
    window_sum = window_sum + jnp.pad(per_slot[:, 2], ((2, 0), (0, 0), (0, 0)))
    glob_sum = jnp.sum(per_slot[:, 3 : 3 + GLOB], axis=0)
    return (window_sum, glob_sum, per_slot[:, 3 + GLOB :])


def local(queries, key_states, value_states, positions, random_blocks, global_blocks, out_grad):
    tok_rows = queries.shape[0]
    block_rows = tok_rows // BLK
    kv_dev = key_states.shape[1] // HD
    q_heads = kv_dev * GROUP
    key_slots = 3 + GLOB + RND
    seq_count = lax.axis_size("seq")
    my_index = lax.axis_index("seq")
    slot_count = block_rows * kv_dev * RND
    capacity = (slot_count + seq_count - 1) // seq_count + 1
    cosines, sine_vals = tables(positions)
    q_rot = rotate(
        queries.reshape(tok_rows, q_heads, HD).astype(jnp.float32), cosines, sine_vals
    ).astype(jnp.bfloat16)
    k_rot = rotate(
        key_states.reshape(tok_rows, kv_dev, HD).astype(jnp.float32), cosines, sine_vals
    ).astype(jnp.bfloat16)
    paired = jnp.stack([k_rot.reshape(tok_rows, kv_dev * HD), value_states])
    own_blocks = paired.reshape(2, block_rows, BLK, kv_dev, HD)
    padded = extended(paired, (("seq", 1),), BLK)
    window_heads = padded.reshape(2, block_rows + 2, BLK, kv_dev, HD).transpose(3, 0, 1, 2, 4)
    glob_owner = global_blocks // block_rows
    glob_local = global_blocks % block_rows
    glob_pieces = []
    for which_glob in range(GLOB):
        glob_piece = lax.dynamic_index_in_dim(own_blocks, glob_local[which_glob], 1, keepdims=False)
        glob_pieces.append(spread(glob_piece, "seq", glob_owner[which_glob]))
    glob_kv = jnp.stack(glob_pieces, axis=1)
    glob_heads = glob_kv.transpose(3, 0, 1, 2, 4)
    flat_ids = random_blocks.reshape(slot_count)
    owners = flat_ids // block_rows
    head_ids = jnp.broadcast_to(
        jnp.arange(kv_dev, dtype=jnp.int32)[None, :, None], (block_rows, kv_dev, RND)
    ).reshape(slot_count)
    req_code = flat_ids % block_rows * kv_dev + head_ids
    slot_ids = jnp.arange(slot_count, dtype=jnp.int32)
    earlier = (owners[:, None] == owners[None, :]) & (slot_ids[None, :] < slot_ids[:, None])
    slot_pos = owners * capacity + jnp.sum(earlier, axis=1)
    kv_table = own_blocks.transpose(1, 3, 0, 2, 4).reshape(block_rows * kv_dev, 2, BLK, HD)
    request = jnp.zeros((seq_count * capacity,), jnp.int32).at[slot_pos].set(req_code)
    request = request.reshape(seq_count, capacity)
    asked_part = lax.all_to_all(request, "seq", split_axis=0, concat_axis=0, tiled=True)
    answers = kv_table[asked_part]
    fetched = lax.all_to_all(answers, "seq", split_axis=0, concat_axis=0, tiled=True)
    random_kv = fetched.reshape(seq_count * capacity, 2, BLK, HD)[slot_pos]
    random_heads = random_kv.reshape(block_rows, kv_dev, RND, 2, BLK, HD).transpose(
        1, 3, 0, 2, 4, 5
    )
    window_ids = (
        my_index * block_rows + jnp.arange(block_rows)[:, None] + jnp.arange(-1, 2)[None, :]
    )
    window_ok = (window_ids >= 0) & (window_ids < seq_count * block_rows)
    block_ok = jnp.concatenate([window_ok, jnp.ones((block_rows, GLOB + RND), dtype=bool)], axis=1)
    key_mask = jnp.repeat(block_ok, BLK, axis=1)
    query_heads = q_rot.reshape(block_rows, BLK, kv_dev, GROUP, HD).transpose(2, 0, 1, 3, 4)
    grad_heads = out_grad.reshape(block_rows, BLK, kv_dev, GROUP, HD).transpose(2, 0, 1, 3, 4)

    def one_head(inputs):
        query_h, grad_h, window_h, glob_h, random_h = inputs
        window_set = jnp.stack(
            [window_h[:, offset : offset + block_rows] for offset in range(3)], axis=2
        )
        glob_set = jnp.broadcast_to(glob_h[:, None], (2, block_rows, GLOB, BLK, HD))
        key_set = jnp.concatenate([window_set, glob_set, random_h], axis=2)
        key_set = key_set.reshape(2, block_rows, key_slots * BLK, HD)
        attended, query_portion, key_portion, value_portion = attend(
            query_h, key_set[0], key_set[1], grad_h, key_mask
        )
        key_window, key_glob, key_random = split_slots(key_portion, block_rows)
        value_window, value_glob, value_random = split_slots(value_portion, block_rows)
        return (
            attended,
            query_portion,
            jnp.stack([key_window, value_window]),
            jnp.stack([key_glob, value_glob]),
            jnp.stack([key_random, value_random], axis=2),
        )

    attended, query_portion, window_acc, glob_local_grad, random_out = lax.map(
        one_head, (query_heads, grad_heads, window_heads, glob_heads, random_heads)
    )
    window_acc = window_acc.transpose(1, 0, 2, 3, 4)
    from_right = shifted(window_acc[:, :, 0].astype(jnp.bfloat16), "seq", -1).astype(jnp.float32)
    from_left = shifted(window_acc[:, :, block_rows + 1].astype(jnp.bfloat16), "seq", 1).astype(
        jnp.float32
    )
    kv_grad = window_acc[:, :, 1 : block_rows + 1]
    kv_grad = kv_grad.at[:, :, block_rows - 1].add(from_right).at[:, :, 0].add(from_left)
    glob_grad = lax.psum(glob_local_grad.transpose(1, 0, 2, 3, 4), "seq")
    glob_mine = jnp.where((glob_owner == my_index)[None, None, :, None, None], glob_grad, 0.0)
    kv_grad = kv_grad.at[:, :, glob_local].add(glob_mine)
    random_grad = random_out.transpose(1, 0, 2, 3, 4, 5).reshape(slot_count, 2, BLK, HD)
    inverse = jnp.full((seq_count * capacity,), slot_count, jnp.int32).at[slot_pos].set(slot_ids)
    filled = inverse < slot_count
    outgoing = jnp.where(
        filled[:, None, None, None], random_grad[jnp.minimum(inverse, slot_count - 1)], 0.0
    )
    outgoing = outgoing.reshape(seq_count, capacity, 2, BLK, HD)
    returned = lax.all_to_all(
        outgoing.astype(jnp.bfloat16), "seq", split_axis=0, concat_axis=0, tiled=True
    ).astype(outgoing.dtype)
    collected = (
        jnp.zeros((block_rows * kv_dev, 2, BLK, HD), jnp.float32)
        .at[asked_part.reshape(-1)]
        .add(returned.reshape(seq_count * capacity, 2, BLK, HD))
    )
    kv_grad = kv_grad + collected.reshape(block_rows, kv_dev, 2, BLK, HD).transpose(2, 1, 0, 3, 4)
    attended = attended.transpose(1, 2, 0, 3, 4).reshape(tok_rows, q_heads * HD)
    query_portion = query_portion.transpose(1, 2, 0, 3, 4).reshape(tok_rows, q_heads, HD)
    query_grad = (
        unrotate(query_portion, cosines, sine_vals)
        .astype(jnp.bfloat16)
        .reshape(tok_rows, q_heads * HD)
    )
    key_acc = kv_grad[0].transpose(1, 2, 0, 3).reshape(tok_rows, kv_dev, HD)
    key_grad = (
        unrotate(key_acc, cosines, sine_vals).astype(jnp.bfloat16).reshape(tok_rows, kv_dev * HD)
    )
    value_grad = (
        kv_grad[1].transpose(1, 2, 0, 3).reshape(tok_rows, kv_dev * HD).astype(jnp.bfloat16)
    )
    return (attended, query_grad, key_grad, value_grad)


def solution(mesh):
    in_specs = (
        P("seq", "head"),
        P("seq", "head"),
        P("seq", "head"),
        P(None, "seq"),
        P("seq", "head", None),
        P(),
        P("seq", "head"),
    )
    out_specs = (P("seq", "head"), P("seq", "head"), P("seq", "head"), P("seq", "head"))
    return jax.shard_map(local, mesh=mesh, in_specs=in_specs, out_specs=out_specs, check_vma=False)
```

profile of v0, /device:TPU:32, one launch (start us, length us, event | category | flops | bytes accessed | tf_op | source)
XLA Modules:
  0.0 668.5 jit_solution(16357737815024441734)
XLA Ops:
  10.0 15.0 %all-to-all-start = ((s32[128,1,2]{2,1,0:T(1,128)}), s32[128,1,2]{2,1,0:T(1,128)S(1)}, u32[]{:S(2)}, u32[]{:S(2)}) async-start(s32[128,1,2]{2,1,0:T(1,128)} %bitcast.18), calls=%async_computation | async-start | bytes 131072 | tf_op jit(solution)/shard_map/all_to_all | solution.py:170
  25.8 1.1 copy.166
  27.8 8.4 %all-to-all-done = s32[128,1,2]{2,1,0:T(1,128)S(1)} async-done(((s32[128,1,2]{2,1,0:T(1,128)}), s32[128,1,2]{2,1,0:T(1,128)S(1)}, u32[]{:S(2)}, u32[]{:S(2)}) %all-to-all-start) | async-done | bytes 1056 | tf_op jit(solution)/shard_map/all_to_all | solution.py:170
  36.3 8.3 %gather_fusion = bf16[256,2,64,128]{3,2,1,0:T(8,128)(2,1)} fusion(bf16[16,2,64,128]{3,2,1,0:T(8,128)(2,1)S(1)} %bitcast.307, s32[1024]{0:T(1024)S(1)} %pad_clamp_fusion.2), kind=kCustom, calls=%fused_computation | custom fusion | bytes 16778240 | tf_op jit(solution)/shard_map/gather | solution.py:171
  44.6 8.0 %all-to-all-start.1 = ((bf16[128,2,2,64,128]{4,3,2,1,0:T(8,128)(2,1)}), bf16[128,2,2,64,128]{4,3,2,1,0:T(8,128)(2,1)}, u32[]{:S(2)}, u32[]{:S(2)}) async-start(bf16[128,2,2,64,128]{4,3,2,1,0:T(8,128)(2,1)} %bitcast.320), calls=%async_computation.1 | async-start | bytes 16777216 | tf_op jit(solution)/shard_map/all_to_all | solution.py:172
  53.8 3.4 collective-permute-start
  57.2 2.5 collective-permute-start.1
  70.4 3.0 maximum_bitcast_fusion.3
  74.3 3.0 copy.179
  77.3 2.6 reshape.596
  79.9 159.8 %collective-permute-done = bf16[2,64,512]{1,2,0:T(8,128)(2,1)S(1)} collective-permute-done((bf16[2,64,512]{1,2,0:T(8,128)(2,1)}, bf16[2,64,512]{1,2,0:T(8,128)(2,1)S(1)}, u32[]{:S(2)}, u32[]{:S(2)}) %collective-permute-start) | collective-permute-done | bytes 131104 | tf_op jit(solution)/shard_map/ppermute | solution.py:26
  239.9 2.3 pad_maximum_fusion.1
  242.2 1.4 copy.168
  243.6 1.1 reshape.589
  244.7 1.3 copy.176
  246.0 45.4 %all-reduce.13.cloned.1.call-done = (bf16[2,1,64,4,128]{4,2,1,3,0:T(8,128)(2,1)}, bf16[2,1,64,4,128]{4,2,1,3,0:T(8,128)(2,1)}) async-done(((bf16[2,1,64,4,128]{4,2,1,3,0:T(8,128)(2,1)}, bf16[2,1,64,4,128]{4,2,1,3,0:T(8,128)(2,1)}), (bf16[2,1,64,4,128]{4,2,1,3,0:T(8,128)(2,1)}, bf16[2,1,64,4,128]{4,2,1,3,0:T(8,128)(2,1)})) %all-reduce.13.cloned.1.call-update) | async-done | bytes 262160 | tf_op jit(solution)/shard_map/psum | solution.py:34
  291.4 1.7 maximum_bitcast_fusion.4
  293.1 5.4 gather_fusion.1
  298.5 44.8 %while.23 = (s32[]{:T(128)}, bf16[4,4,64,4,128]{4,2,3,1,0:T(8,128)(2,1)}, f32[4,4,64,4,128]{4,2,1,3,0:T(8,128)}, f32[4,2,6,64,128]{4,3,0,1,2:T(8,128)}, f32[4,2,...) while((s32[]{:T(128)}, ...), condition=%wide.region_10.11_spmd.clone, body=%wide.region_4.10_spmd.clone.sunk | while | flops 813399552 | bytes 35746000 | solution.py:207
  299.5 1.0 constant_dynamic-slice_fusion.6
  300.7 1.1 fusion.101
  304.1 1.1 bitcast_dynamic-update-slice_fusion.2
  310.7 1.0 constant_dynamic-slice_fusion.6
  311.9 1.1 fusion.101
  315.4 1.1 bitcast_dynamic-update-slice_fusion.2
  323.1 1.1 fusion.101
  326.5 1.1 bitcast_dynamic-update-slice_fusion.2
  334.2 1.1 fusion.101
  337.7 1.1 bitcast_dynamic-update-slice_fusion.2
  343.2 8.3 %gather_fusion.2 = bf16[256,2,64,128]{3,2,1,0:T(8,128)(2,1)} fusion(bf16[48,2,64,128]{3,2,1,0:T(8,128)(2,1)S(1)} %bitcast.318, s32[1024]{0:T(1024)S(1)} %pad_clamp_fusion), kind=kCustom, calls=%fused_computation.2 | custom fusion | bytes 16778240 | tf_op jit(solution)/shard_map/gather | solution.py:224
  351.6 8.4 %select_convert_fusion = bf16[128,2,2,64,128]{4,3,2,1,0:T(8,128)(2,1)} fusion(bf16[128,2,2,64,128]{4,3,2,1,0:T(8,128)(2,1)} %bitcast.319, pred[128,2]{1,0:T(8,128)(4,1)S(1)} %copy-done.8), kind=kLoop, calls=%fused_computation.71 | loop fusion | flops 4194304 | bytes 16777472 | tf_op jit(solution)/shard_map/convert_element_type | solution.py:228
  360.0 11.3 %all-to-all-start.2 = ((bf16[128,2,2,64,128]{4,3,2,1,0:T(8,128)(2,1)}), bf16[128,2,2,64,128]{4,3,2,1,0:T(8,128)(2,1)}, u32[]{:S(2)}, u32[]{:S(2)}) async-start(bf16[128,2,2,64,128]{4,3,2,1,0:T(8,128)(2,1)} %select_convert_fusion), calls=%async_computation.2 | async-start | bytes 16777216 | tf_op jit(solution)/shard_map/all_to_all | solution.py:227
  373.6 1.6 reshape.597
  375.2 1.7 bitcast_convert_fusion.1
  377.6 3.4 collective-permute-start.3
  381.0 2.5 collective-permute-start.2
  383.5 2.7 fusion.53
  386.2 3.3 copy.215
  389.5 1.6 copy.214
  391.1 2.0 add_convert_fusion
  393.1 1.1 pad_maximum_fusion
  394.3 2.3 copy.194
  396.6 156.2 %collective-permute-done.2 = bf16[2,4,64,128]{3,2,1,0:T(8,128)(2,1)S(1)} collective-permute-done((bf16[2,4,64,128]{3,2,1,0:T(8,128)(2,1)S(1)}, bf16[2,4,64,128]{3,2,1,0:T(8,128)(2,1)S(1)}, u32[]{:S(2)}, u32[]{:S(2)}) %collective-permute-start.2) | collective-permute-done | bytes 131104 | tf_op jit(solution)/shard_map/ppermute | solution.py:40
  553.4 56.5 %all-reduce.11.cloned.1.call-done = f32[2,4,2,64,128]{4,3,2,0,1:T(8,128)} async-done(((f32[2,4,2,64,128]{4,3,2,0,1:T(8,128)}), f32[2,4,2,64,128]{4,3,2,0,1:T(8,128)}) %all-reduce.11.cloned.1.call-update) | async-done | bytes 524304 | tf_op jit(solution)/shard_map/psum | solution.py:217
  609.9 1.2 select_bitcast_fusion
  612.0 11.4 %bitcast_convert_fusion = f32[256,2,64,128]{3,2,1,0:T(8,128)} fusion(bf16[128,2,2,64,128]{4,3,2,1,0:T(8,128)(2,1)} %all-to-all-done.2), kind=kLoop, calls=%fused_computation.72 | loop fusion | flops 4194304 | bytes 25165824 | tf_op jit(solution)/shard_map/reshape | solution.py:233
  623.5 33.1 %scatter_fusion = f32[16,2,64,128]{3,2,1,0:T(8,128)S(1)} fusion(f32[16,2,64,128]{3,2,1,0:T(8,128)S(1)} %broadcast_in_dim.219, s32[256]{0:T(256)S(1)} %bitcast.346, f32[256,2,64,128]{3,2,1,0:T(8,128)} %bitcast_convert_fusion), kind=kCustom, calls=%fused_computation.5 | custom fusion | flops 4194304 | bytes 50332672 | tf_op jit(solution)/shard_map/scatter-add | solution.py:233
  657.2 1.8 scatter_fusion.1
  (219 shorter events, 53.4 us)
Async XLA Ops:
  7.2 20.4 %copy-start.5 = (bf16[256,512]{1,0:T(8,128)(2,1)S(1)}, bf16[256,512]{1,0:T(8,128)(2,1)}, u32[]{:S(2)}) copy-start(bf16[256,512]{1,0:T(8,128)(2,1)} %param.15) | copy-start | bytes 786436
  10.0 26.1 %all-to-all-start = ((s32[128,1,2]{2,1,0:T(1,128)}), s32[128,1,2]{2,1,0:T(1,128)S(1)}, u32[]{:S(2)}, u32[]{:S(2)}) async-start(s32[128,1,2]{2,1,0:T(1,128)} %bitcast.18), calls=%async_computation | async-start | bytes 131072 | tf_op jit(solution)/shard_map/all_to_all | solution.py:170
  36.1 8.5 %copy-start.6 = (s32[128,1,2]{2,1,0:T(1,128)}, s32[128,1,2]{2,1,0:T(1,128)S(1)}, u32[]{:S(2)}) copy-start(s32[128,1,2]{2,1,0:T(1,128)S(1)} %all-to-all-done) | copy-start | bytes 3076
  44.6 15.0 %copy-start.11 = (s32[2]{0:T(128)S(1)}, s32[2]{0:T(128)}, u32[]{:S(2)}) copy-start(s32[2]{0:T(128)} %param.18) | copy-start | bytes 28
  44.6 248.4 %all-to-all-start.1 = ((bf16[128,2,2,64,128]{4,3,2,1,0:T(8,128)(2,1)}), bf16[128,2,2,64,128]{4,3,2,1,0:T(8,128)(2,1)}, u32[]{:S(2)}, u32[]{:S(2)}) async-start(bf16[128,2,2,64,128]{4,3,2,1,0:T(8,128)(2,1)} %bitcast.320), calls=%async_computation.1 | async-start | bytes 16777216 | tf_op jit(solution)/shard_map/all_to_all | solution.py:172
  52.7 15.0 %copy-start.3 = (bf16[256,2048]{1,0:T(8,128)(2,1)S(1)}, bf16[256,2048]{1,0:T(8,128)(2,1)}, u32[]{:S(2)}) copy-start(bf16[256,2048]{1,0:T(8,128)(2,1)} %param.13) | copy-start | bytes 3145732
  52.7 238.7 %all-reduce.13.cloned.1.call-start = ((), (), s32[]{:S(2)}) async-start(), calls=%async_computation.4 | async-start | bytes 524288 | tf_op jit(solution)/shard_map/psum | solution.py:34
  53.8 185.9 %collective-permute-start = (bf16[2,64,512]{1,2,0:T(8,128)(2,1)}, bf16[2,64,512]{1,2,0:T(8,128)(2,1)S(1)}, u32[]{:S(2)}, u32[]{:S(2)}) collective-permute-start(bf16[2,64,512]{1,2,0:T(8,128)(2,1)} %get-tuple-element.351), channel_id=1, source_target_pairs={{0,2},{2,4},{4,6},{6,8},{8,10},{10,12},{12,14},{14,16},{16,18},{18... | collective-permute-start | bytes 393224 | tf_op jit(solution)/shard_map/ppermute | solution.py:26
  57.2 182.7 %collective-permute-start.1 = (bf16[2,64,512]{1,2,0:T(8,128)(2,1)}, bf16[2,64,512]{1,2,0:T(8,128)(2,1)}, u32[]{:S(2)}, u32[]{:S(2)}) collective-permute-start(bf16[2,64,512]{1,2,0:T(8,128)(2,1)} %get-tuple-element.352), channel_id=1, source_target_pairs={{2,0},{4,2},{6,4},{8,6},{10,8},{12,10},{14,12},{16,14},{18,16},{20... | collective-permute-start | bytes 393224 | tf_op jit(solution)/shard_map/ppermute | solution.py:27
  343.2 8.4 %copy-start.8 = (pred[128,2]{1,0:T(8,128)(4,1)S(1)}, pred[128,2]{1,0:T(8,128)(4,1)}, u32[]{:S(2)}) copy-start(pred[128,2]{1,0:T(8,128)(4,1)} %broadcast_in_dim.220) | copy-start | bytes 772
  360.0 11.8 %copy-start.7 = (s32[128,1,2]{2,1,0:T(1,128)S(1)}, s32[128,1,2]{2,1,0:T(1,128)}, u32[]{:S(2)}) copy-start(s32[128,1,2]{2,1,0:T(1,128)} %copy-done.6) | copy-start | bytes 3076
  360.0 12.8 %copy-start.4 = (bf16[4,4,64,4,128]{4,2,3,1,0:T(8,128)(2,1)S(1)}, bf16[4,4,64,4,128]{4,2,3,1,0:T(8,128)(2,1)}, u32[]{:S(2)}) copy-start(bf16[4,4,64,4,128]{4,2,3,1,0:T(8,128)(2,1)} %get-tuple-element.181) | copy-start | bytes 3145732
  360.0 252.0 %all-to-all-start.2 = ((bf16[128,2,2,64,128]{4,3,2,1,0:T(8,128)(2,1)}), bf16[128,2,2,64,128]{4,3,2,1,0:T(8,128)(2,1)}, u32[]{:S(2)}, u32[]{:S(2)}) async-start(bf16[128,2,2,64,128]{4,3,2,1,0:T(8,128)(2,1)} %select_convert_fusion), calls=%async_computation.2 | async-start | bytes 16777216 | tf_op jit(solution)/shard_map/all_to_all | solution.py:227
  371.2 238.7 %all-reduce.11.cloned.1.call-start = ((), (), s32[]{:S(2)}) async-start(), calls=%async_computation.3 | async-start | bytes 1048576 | tf_op jit(solution)/shard_map/psum | solution.py:217
  375.2 8.2 %copy-start = (f32[4,4,64,4,128]{4,2,1,3,0:T(8,128)S(1)}, f32[4,4,64,4,128]{4,2,1,3,0:T(8,128)}, u32[]{:S(2)}) copy-start(f32[4,4,64,4,128]{4,2,1,3,0:T(8,128)} %get-tuple-element.182) | copy-start | bytes 6291460
  377.6 175.8 %collective-permute-start.3 = (bf16[2,4,64,128]{3,2,1,0:T(8,128)(2,1)}, bf16[2,4,64,128]{3,2,1,0:T(8,128)(2,1)S(1)}, u32[]{:S(2)}, u32[]{:S(2)}) collective-permute-start(bf16[2,4,64,128]{3,2,1,0:T(8,128)(2,1)} %get-tuple-element.341), channel_id=1, source_target_pairs={{0,2},{2,4},{4,6},{6,8},{8,10},{10,12},{12,14},{14,16},{16,18},{18... | collective-permute-start | bytes 393224 | tf_op jit(solution)/shard_map/ppermute | solution.py:40
  381.0 171.9 %collective-permute-start.2 = (bf16[2,4,64,128]{3,2,1,0:T(8,128)(2,1)S(1)}, bf16[2,4,64,128]{3,2,1,0:T(8,128)(2,1)S(1)}, u32[]{:S(2)}, u32[]{:S(2)}) collective-permute-start(bf16[2,4,64,128]{3,2,1,0:T(8,128)(2,1)S(1)} %get-tuple-element.342), channel_id=1, source_target_pairs={{2,0},{4,2},{6,4},{8,6},{10,8},{12,10},{14,12},{16,14},{18,16},{20... | collective-permute-start | bytes 393224 | tf_op jit(solution)/shard_map/ppermute | solution.py:40
  386.2 3.3 copy-start.1
  391.1 3.1 copy-start.2
  396.6 213.3 %copy-start.9 = (pred[2]{0:T(512)(128)(4,1)S(1)}, pred[2]{0:T(512)(128)(4,1)}, u32[]{:S(2)}) copy-start(pred[2]{0:T(512)(128)(4,1)} %get-tuple-element.315) | copy-start | bytes 10
  656.6 0.6 copy-start.10
Sparse Core Ops, SparseCore 0:
  67.8 223.5 all-reduce.12
  377.5 232.4 all-reduce.10
where the time goes:
time: 672 us; the launch traced here: 668 us
  waiting for transfers between devices  427 us (64%)
  other arithmetic  86.1 us (13%)
  local copies, waits for them, and re-layouts  74.8 us (11%)
  starting transfers between devices  46.1 us (7%)
  between operations  19.6 us (3%)
  matrix products  14.4 us (2%)
    ppermute x1, waiting for transfers between devices, extended(): before = lax.ppermute(last, axis, up)  160 us
    ppermute x2, waiting for transfers between devices, shifted(): return lax.ppermute(array, axis, pairs)  157 us
    psum x1, waiting for transfers between devices, local(): glob_grad = lax.psum(glob_local_grad.transpose(1, 0, 2, 3, 4), 'seq')  56.5 us
    psum x1, waiting for transfers between devices, spread(): return lax.psum(block, axis)  45.4 us
    scatter-add x1, other arithmetic, local(): collected = jnp.zeros((block_rows * kv_dev, 2, BLK, HD), jnp.float32).at[...  33.1 us
    unnamed x37, local copies, waits for them, and re-layouts  16.5 us
    all_to_all x1, starting transfers between devices, local(): lax.all_to_all(request, 'seq', split_axis=0, concat_axis=0, tiled=True)  15 us
  transfers between devices with their start and end apart: 9, of which 7 were waited for; matrix products, arithmetic and copies ran while one was open for 7% of the time, Pallas kernels for 0%

commit v1 on v0

v1 whole, which is shorter than its diff:
```python
import math

import jax
import jax.numpy as jnp
from jax import lax
from jax.sharding import PartitionSpec as P

HD = 128
GROUP = 4
BLK = 64
GLOB = 2
RND = 3


NEG_FILL = -1e30
ROPE_BASE = 1000000.0


def extended(array, sides, width):
    for axis, dim in sides:
        devices, length = (lax.axis_size(axis), array.shape[dim])
        up = [(i, (i + 1) % devices) for i in range(devices - 1)]
        down = [(j, i) for i, j in up]
        last = lax.slice_in_dim(array, length - width, length, axis=dim)
        leading = lax.slice_in_dim(array, 0, width, axis=dim)
        before = lax.ppermute(last, axis, up)
        after = lax.ppermute(leading, axis, down)
        array = jnp.concatenate([before, array, after], axis=dim)
    return array


def spread(block, axis, source):
    block = jnp.where(lax.axis_index(axis) == source, block, jnp.zeros_like(block))
    return lax.psum(block, axis)


def shifted(array, axis, by):
    devices = lax.axis_size(axis)
    pairs = [(i, i + by) for i in range(devices) if 0 <= i + by < devices]
    return lax.ppermute(array, axis, pairs)


def tables(positions):
    half_dim = HD // 2
    freq_ids = jnp.arange(half_dim)
    inv_freq = jnp.power(jnp.float32(ROPE_BASE), -2.0 * freq_ids.astype(jnp.float32) / HD)
    pos_float = positions.astype(jnp.float32)
    chosen = jnp.where(
        (freq_ids % 3 == 0)[None, :],
        pos_float[0][:, None],
        jnp.where((freq_ids % 3 == 1)[None, :], pos_float[1][:, None], pos_float[2][:, None]),
    )
    angles = chosen * inv_freq[None, :]
    return (jnp.cos(angles), jnp.sin(angles))


def rotate(states, cosines, sine_vals):
    half_dim = HD // 2
    first_half = states[..., :half_dim]
    second_half = states[..., half_dim:]
    cos_b = cosines[:, None, :]
    sin_b = sine_vals[:, None, :]
    return jnp.concatenate(
        [first_half * cos_b - second_half * sin_b, second_half * cos_b + first_half * sin_b],
        axis=-1,
    )


def unrotate(states, cosines, sine_vals):
    half_dim = HD // 2
    first_half = states[..., :half_dim]
    second_half = states[..., half_dim:]
    cos_b = cosines[:, None, :]
    sin_b = sine_vals[:, None, :]
    return jnp.concatenate(
        [first_half * cos_b + second_half * sin_b, second_half * cos_b - first_half * sin_b],
        axis=-1,
    )


def attend(query_block_view, key_block_view, value_block_view, gradient_block_view, key_mask):
    score_scale = 1.0 / math.sqrt(HD)
    logit_scores = (
        jnp.einsum(
            "mtyp,mop->myto", query_block_view, key_block_view, preferred_element_type=jnp.float32
        )
        * score_scale
    )
    logit_scores = jnp.where(key_mask[:, None, None, :], logit_scores, NEG_FILL)
    row_max = jnp.max(logit_scores, axis=-1, keepdims=True)
    exponent = jnp.exp(logit_scores - row_max)
    probability = exponent / jnp.sum(exponent, axis=-1, keepdims=True)
    attention_weights = probability.astype(jnp.bfloat16)
    attended = jnp.einsum(
        "ywiu,yuz->yiwz", attention_weights, value_block_view, preferred_element_type=jnp.float32
    ).astype(jnp.bfloat16)
    weight_gradient = jnp.einsum(
        "mtyp,mop->myto", gradient_block_view, value_block_view, preferred_element_type=jnp.float32
    )
    row_delta = jnp.sum(
        gradient_block_view.astype(jnp.float32) * attended.astype(jnp.float32), axis=-1
    )
    row_delta = jnp.transpose(row_delta, (0, 2, 1))[..., None]
    score_gradient = (probability * (weight_gradient - row_delta) * score_scale).astype(
        jnp.bfloat16
    )
    value_portion = jnp.einsum(
        "pcht,phca->pta", attention_weights, gradient_block_view, preferred_element_type=jnp.float32
    )
    key_portion = jnp.einsum(
        "pcht,phca->pta", score_gradient, query_block_view, preferred_element_type=jnp.float32
    )
    query_portion = jnp.einsum(
        "ywiu,yuz->yiwz", score_gradient, key_block_view, preferred_element_type=jnp.float32
    )
    return (attended, query_portion, key_portion, value_portion)


def onehot(ids, count):
    return (ids[:, None] == jnp.arange(count, dtype=jnp.int32)[None, :]).astype(jnp.bfloat16)


def local(queries, key_states, value_states, positions, random_blocks, global_blocks, out_grad):
    tok_rows = queries.shape[0]
    block_rows = tok_rows // BLK
    kv_dev = key_states.shape[1] // HD
    seq_count = lax.axis_size("seq")
    my_index = lax.axis_index("seq")
    slot_count = block_rows * kv_dev * RND
    capacity = (slot_count + seq_count - 1) // seq_count + 1
    score_scale = 1.0 / math.sqrt(HD)
    table_rows = block_rows * kv_dev

    all_blocks = lax.all_gather(random_blocks, "seq").reshape(seq_count, slot_count)
    head_ids = jnp.broadcast_to(
        jnp.arange(kv_dev, dtype=jnp.int32)[None, :, None], (block_rows, kv_dev, RND)
    ).reshape(slot_count)
    slot_ids = jnp.arange(slot_count, dtype=jnp.int32)
    all_owners = all_blocks // block_rows
    earlier = (all_owners[:, :, None] == all_owners[:, None, :]) & (
        slot_ids[None, None, :] < slot_ids[None, :, None]
    )
    all_rank = jnp.sum(earlier, axis=2)
    all_code = all_blocks % block_rows * kv_dev + head_ids[None, :]
    mine = all_owners == my_index
    asked_part = jnp.stack(
        [jnp.sum(jnp.where(mine & (all_rank == c), all_code, 0), axis=1) for c in range(capacity)],
        axis=1,
    )
    flat_ids = random_blocks.reshape(slot_count)
    owners = flat_ids // block_rows
    my_rank = lax.dynamic_index_in_dim(all_rank, my_index, 0, keepdims=False)
    slot_pos = owners * capacity + my_rank

    cosines, sine_vals = tables(positions)
    q_rot = rotate(
        queries.reshape(tok_rows, kv_dev * GROUP, HD).astype(jnp.float32), cosines, sine_vals
    ).astype(jnp.bfloat16)
    k_rot = rotate(
        key_states.reshape(tok_rows, kv_dev, HD).astype(jnp.float32), cosines, sine_vals
    ).astype(jnp.bfloat16)
    paired = jnp.stack([k_rot.reshape(tok_rows, kv_dev * HD), value_states])
    own_blocks = paired.reshape(2, block_rows, BLK, kv_dev, HD)

    kv_table = own_blocks.transpose(1, 3, 0, 2, 4).reshape(table_rows, 2 * BLK * HD)
    asked_flat = asked_part.reshape(seq_count * capacity)
    answers = jnp.dot(
        onehot(asked_flat, table_rows), kv_table, preferred_element_type=jnp.float32
    ).astype(jnp.bfloat16)
    padded = extended(paired, (("seq", 1),), BLK)
    window_blocks = padded.reshape(2, block_rows + 2, BLK, kv_dev, HD)
    glob_owner = global_blocks // block_rows
    glob_local = global_blocks % block_rows
    glob_pieces = []
    for which_glob in range(GLOB):
        glob_piece = lax.dynamic_index_in_dim(own_blocks, glob_local[which_glob], 1, keepdims=False)
        glob_pieces.append(spread(glob_piece, "seq", glob_owner[which_glob]))
    glob_kv = jnp.stack(glob_pieces, axis=1)
    answers, padded, glob_kv = lax.optimization_barrier((answers, padded, glob_kv))
    window_blocks = padded.reshape(2, block_rows + 2, BLK, kv_dev, HD)
    fetched = lax.all_to_all(
        answers.reshape(seq_count, capacity, 2 * BLK * HD), "seq", 0, 0, tiled=True
    ).reshape(seq_count * capacity, 2 * BLK * HD)

    window_set = jnp.stack([window_blocks[:, offset : offset + block_rows] for offset in range(3)], axis=2)
    glob_set = jnp.broadcast_to(glob_kv[:, None], (2, block_rows, GLOB, BLK, kv_dev, HD))
    near_set = jnp.concatenate([window_set, glob_set], axis=2).reshape(
        2, block_rows, (3 + GLOB) * BLK, kv_dev, HD
    )
    window_ids = (
        my_index * block_rows + jnp.arange(block_rows)[:, None] + jnp.arange(-1, 2)[None, :]
    )
    window_ok = (window_ids >= 0) & (window_ids < seq_count * block_rows)
    near_ok = jnp.concatenate([window_ok, jnp.ones((block_rows, GLOB), dtype=bool)], axis=1)
    near_mask = jnp.repeat(near_ok, BLK, axis=1)

    query_nat = q_rot.reshape(block_rows, BLK, kv_dev, GROUP, HD)
    grad_nat = out_grad.reshape(block_rows, BLK, kv_dev, GROUP, HD)
    near_k = near_set[0]
    near_v = near_set[1]
    near_scores = (
        jnp.einsum("rthgd,rkhd->rhgtk", query_nat, near_k, preferred_element_type=jnp.float32)
        * score_scale
    )
    near_scores = jnp.where(near_mask[:, None, None, None, :], near_scores, NEG_FILL)
    near_wgrad = jnp.einsum("rthgd,rkhd->rhgtk", grad_nat, near_v, preferred_element_type=jnp.float32)

    random_kv = fetched[slot_pos].reshape(block_rows, kv_dev, RND, 2, BLK, HD)
    far_k = random_kv[:, :, :, 0].reshape(block_rows, kv_dev, RND * BLK, HD)
    far_v = random_kv[:, :, :, 1].reshape(block_rows, kv_dev, RND * BLK, HD)
    far_scores = (
        jnp.einsum("rthgd,rhkd->rhgtk", query_nat, far_k, preferred_element_type=jnp.float32)
        * score_scale
    )
    far_wgrad = jnp.einsum("rthgd,rhkd->rhgtk", grad_nat, far_v, preferred_element_type=jnp.float32)
    row_max = jnp.maximum(
        jnp.max(near_scores, axis=-1, keepdims=True), jnp.max(far_scores, axis=-1, keepdims=True)
    )
    near_exp = jnp.exp(near_scores - row_max)
    far_exp = jnp.exp(far_scores - row_max)
    total = jnp.sum(near_exp, axis=-1, keepdims=True) + jnp.sum(far_exp, axis=-1, keepdims=True)
    near_prob = near_exp / total
    far_prob = far_exp / total
    near_w = near_prob.astype(jnp.bfloat16)
    far_w = far_prob.astype(jnp.bfloat16)
    attended = (
        jnp.einsum("rhgtk,rkhd->rthgd", near_w, near_v, preferred_element_type=jnp.float32)
        + jnp.einsum("rhgtk,rhkd->rthgd", far_w, far_v, preferred_element_type=jnp.float32)
    ).astype(jnp.bfloat16)
    row_delta = jnp.sum(grad_nat.astype(jnp.float32) * attended.astype(jnp.float32), axis=-1)
    row_delta = row_delta.transpose(0, 2, 3, 1)[..., None]
    near_sgrad = (near_prob * (near_wgrad - row_delta) * score_scale).astype(jnp.bfloat16)
    far_sgrad = (far_prob * (far_wgrad - row_delta) * score_scale).astype(jnp.bfloat16)

    far_kgrad = jnp.einsum("rhgtk,rthgd->rhkd", far_sgrad, query_nat, preferred_element_type=jnp.float32)
    far_vgrad = jnp.einsum("rhgtk,rthgd->rhkd", far_w, grad_nat, preferred_element_type=jnp.float32)
    random_grad = jnp.stack(
        [
            far_kgrad.reshape(block_rows, kv_dev, RND, BLK, HD),
            far_vgrad.reshape(block_rows, kv_dev, RND, BLK, HD),
        ],
        axis=3,
    ).reshape(slot_count, 2 * BLK * HD).astype(jnp.bfloat16)
    outgoing = jnp.dot(
        onehot(slot_pos, seq_count * capacity).T, random_grad, preferred_element_type=jnp.float32
    ).astype(jnp.bfloat16)
    query_portion = jnp.einsum(
        "rhgtk,rkhd->rthgd", near_sgrad, near_k, preferred_element_type=jnp.float32
    ) + jnp.einsum("rhgtk,rhkd->rthgd", far_sgrad, far_k, preferred_element_type=jnp.float32)
    near_kgrad = jnp.einsum("rhgtk,rthgd->rkhd", near_sgrad, query_nat, preferred_element_type=jnp.float32)
    near_vgrad = jnp.einsum("rhgtk,rthgd->rkhd", near_w, grad_nat, preferred_element_type=jnp.float32)
    near_grad = jnp.stack([near_kgrad, near_vgrad]).reshape(2, block_rows, 3 + GLOB, BLK, kv_dev, HD)
    window_acc = jnp.pad(near_grad[:, :, 0], ((0, 0), (0, 2), (0, 0), (0, 0), (0, 0)))
    window_acc = window_acc + jnp.pad(near_grad[:, :, 1], ((0, 0), (1, 1), (0, 0), (0, 0), (0, 0)))
    window_acc = window_acc + jnp.pad(near_grad[:, :, 2], ((0, 0), (2, 0), (0, 0), (0, 0), (0, 0)))
    glob_local_grad = jnp.sum(near_grad[:, :, 3:], axis=1)
    from_right = shifted(window_acc[:, 0].astype(jnp.bfloat16), "seq", -1).astype(jnp.float32)
    from_left = shifted(window_acc[:, block_rows + 1].astype(jnp.bfloat16), "seq", 1).astype(jnp.float32)
    glob_grad = lax.psum(glob_local_grad, "seq")
    outgoing, from_right, from_left, glob_grad = lax.optimization_barrier(
        (outgoing, from_right, from_left, glob_grad)
    )
    returned = lax.all_to_all(
        outgoing.reshape(seq_count, capacity, 2 * BLK * HD), "seq", 0, 0, tiled=True
    ).reshape(seq_count * capacity, 2 * BLK * HD)

    kv_grad = window_acc[:, 1 : block_rows + 1]
    kv_grad = kv_grad.at[:, block_rows - 1].add(from_right).at[:, 0].add(from_left)
    glob_mine = jnp.where((glob_owner == my_index)[None, :, None, None, None], glob_grad, 0.0)
    kv_grad = kv_grad.at[:, glob_local].add(glob_mine)
    collected = jnp.dot(
        onehot(asked_flat, table_rows).T, returned, preferred_element_type=jnp.float32
    ).reshape(block_rows, kv_dev, 2, BLK, HD)
    kv_grad = kv_grad + collected.transpose(2, 0, 3, 1, 4)

    attended = attended.reshape(tok_rows, kv_dev * GROUP * HD)
    query_grad = (
        unrotate(query_portion.reshape(tok_rows, kv_dev * GROUP, HD), cosines, sine_vals)
        .astype(jnp.bfloat16)
        .reshape(tok_rows, kv_dev * GROUP * HD)
    )
    key_acc = kv_grad[0].reshape(tok_rows, kv_dev, HD)
    key_grad = (
        unrotate(key_acc, cosines, sine_vals).astype(jnp.bfloat16).reshape(tok_rows, kv_dev * HD)
    )
    value_grad = kv_grad[1].reshape(tok_rows, kv_dev * HD).astype(jnp.bfloat16)
    return (attended, query_grad, key_grad, value_grad)


def solution(mesh):
    in_specs = (
        P("seq", "head"),
        P("seq", "head"),
        P("seq", "head"),
        P(None, "seq"),
        P("seq", "head", None),
        P(),
        P("seq", "head"),
    )
    out_specs = (P("seq", "head"), P("seq", "head"), P("seq", "head"), P("seq", "head"))
    return jax.shard_map(local, mesh=mesh, in_specs=in_specs, out_specs=out_specs, check_vma=False)
```

time: 672 us -> 1080 us (1.61)
  blocking collectives: 0 us -> 348 us
  other arithmetic: 86.1 us -> 23.6 us
  local copies, waits for them, and re-layouts: 74.8 us -> 123 us
  waiting for transfers between devices: 427 us -> 462 us
  matrix products: 14.4 us -> 45.1 us
    all_gather x0 -> x1, blocking collectives: none -> 348 us  [local(): lax.all_gather(random_blocks, 'seq').reshape(seq_count, slot_count)]
    all_to_all x3 -> x2, waiting for transfers between devices: 8.39 us -> 265 us  [the longest x1 164 us: local(): lax.all_to_all(outgoing.reshape(seq_count, capacity, 2 * BLK * HD), 'seq'...]
    ppermute x1, waiting for transfers between devices: 160 us -> 0.01 us  [extended(): before = lax.ppermute(last, axis, up)]
    ppermute x2, waiting for transfers between devices: 157 us -> 0.01 us  [shifted(): return lax.ppermute(array, axis, pairs)]
    psum x1, waiting for transfers between devices: 56.5 us -> 198 us  [local(): glob_grad = lax.psum(glob_local_grad, 'seq')]
    reshape x5 -> x11, local copies, waits for them, and re-layouts: 5.47 us -> 72.3 us  [the longest x2 25.1 us: local(): returned = lax.all_to_all(outgoing.reshape(seq_count, capacity, 2 * BLK *...]
    psum x1, waiting for transfers between devices: 45.4 us -> 0.01 us  [spread(): return lax.psum(block, axis)]
    scatter-add x4 -> x3, other arithmetic: 35 us -> 0.97 us  [the longest x1 0.8 us: local(): kv_grad = kv_grad.at[:, glob_local].add(glob_mine)]
  transfers between devices with their start and end apart: 9 -> 8, of which waited for: 7 -> 3; matrix products, arithmetic and copies ran while one was open for 7% -> 6% of each run, Pallas kernels for 0% -> 0%
where the time goes in v1:
time: 1080 us; the launch traced here: 1070 us
  waiting for transfers between devices  462 us (43%)
  blocking collectives  348 us (32%)
  local copies, waits for them, and re-layouts  123 us (11%)
  starting transfers between devices  49.3 us (5%)
  matrix products  45.1 us (4%)
  other arithmetic  23.6 us (2%)
  between operations  20.4 us (2%)
    all_gather x1, blocking collectives, local(): lax.all_gather(random_blocks, 'seq').reshape(seq_count, slot_count)  348 us
    psum x1, waiting for transfers between devices, local(): glob_grad = lax.psum(glob_local_grad, 'seq')  198 us
    all_to_all x1, waiting for transfers between devices, local(): lax.all_to_all(outgoing.reshape(seq_count, capacity, 2 * BLK * HD), 'seq'...  164 us
    all_to_all x1, waiting for transfers between devices, local(): lax.all_to_all(answers.reshape(seq_count, capacity, 2 * BLK * HD), 'seq',...  101 us
    reshape x2, local copies, waits for them, and re-layouts, local(): returned = lax.all_to_all(outgoing.reshape(seq_count, capacity, 2 * BLK *...  25.1 us
  transfers between devices with their start and end apart: 8, of which 3 were waited for; matrix products, arithmetic and copies ran while one was open for 6% of the time, Pallas kernels for 0%

profile of v1, /device:TPU:32, one launch (start us, length us, event | category | flops | bytes accessed | tf_op | source)
XLA Modules:
  0.0 1072.5 jit_solution(8341888297970544012)
XLA Ops:
  11.5 3.8 collective-permute-start
  15.4 2.7 collective-permute-start.1
  27.1 348.5 %all-gather = s32[512,4,3]{2,1,0:T(4,128)S(1)} all-gather(s32[4,4,3]{2,1,0:T(4,128)S(1)} %copy.280), channel_id=2, replica_groups=mesh['seq'=128,'head'=2] {'seq'}, dimensions={0}, use_global_device_ids=true | all-gather | bytes 24768 | tf_op jit(solution)/shard_map/all_gather | solution.py:134
  378.6 3.4 copy.336
  383.5 5.7 convolution_convert_fusion.1
  389.2 2.4 pad_maximum_fusion.4
  392.5 14.2 %reshape.604 = bf16[128,2,16384]{2,1,0:T(2,128)(2,1)} reshape(bf16[256,16384]{1,0:T(8,128)(2,1)} %convolution_convert_fusion.1) | data formatting | bytes 16777216 | tf_op jit(solution)/shard_map/reshape | solution.py:182
  406.7 14.0 %all-to-all-start = ((bf16[128,2,16384]{2,1,0:T(2,128)(2,1)}), bf16[128,2,16384]{2,1,0:T(2,128)(2,1)}, u32[]{:S(2)}, u32[]{:S(2)}) async-start(bf16[128,2,16384]{2,1,0:T(2,128)(2,1)} %reshape.604), calls=%async_computation | async-start | bytes 16777216 | tf_op jit(solution)/shard_map/all_to_all | solution.py:181
  420.7 11.7 %all-reduce.8.cloned.1.call-start = ((), (), s32[]{:S(2)}) async-start(), calls=%async_computation.2 | async-start | bytes 1048576 | tf_op jit(solution)/shard_map/psum | solution.py:259
  433.4 1.5 reshape.609
  440.7 1.4 copy.294
  444.0 1.7 fusion.54
  446.8 3.7 bitcast_reduce_fusion
  450.5 101.1 %all-to-all-done = bf16[128,2,16384]{2,1,0:T(2,128)(2,1)} async-done(((bf16[128,2,16384]{2,1,0:T(2,128)(2,1)}), bf16[128,2,16384]{2,1,0:T(2,128)(2,1)}, u32[]{:S(2)}, u32[]{:S(2)}) %all-to-all-start) | async-done | bytes 8388640 | tf_op jit(solution)/shard_map/all_to_all | solution.py:181
  551.5 13.1 %reshape.605 = bf16[256,16384]{1,0:T(8,128)(2,1)} reshape(bf16[128,2,16384]{2,1,0:T(2,128)(2,1)} %all-to-all-done) | data formatting | bytes 16777216 | tf_op jit(solution)/shard_map/reshape | solution.py:183
  564.7 7.4 gather_fusion
  573.5 1.5 fusion.11
  575.6 1.9 fusion.5
  577.6 3.6 bitcast_convert_fusion
  581.2 2.1 fusion.14
  583.3 3.0 multiply_reduce_fusion
  586.3 2.1 fusion.8
  588.4 2.8 fusion.2
  591.3 4.0 fusion.12
  596.3 2.0 copy_dynamic-update-slice_fusion.1
  598.3 2.1 copy_dynamic-update-slice_fusion
  600.4 2.3 copy-done.2
  603.9 2.1 slice_bitcast_fusion.2
  606.0 1.8 bitcast_convert_fusion.1
  607.8 1.8 fusion.53
  612.4 1.9 collective-permute-start.3
  614.3 3.9 collective-permute-start.2
  618.2 5.7 convolution_convert_fusion
  624.7 197.6 %all-reduce.8.cloned.1.call-done = f32[2,2,64,4,128]{4,3,2,0,1:T(4,128)} async-done(((f32[2,2,64,4,128]{4,3,2,0,1:T(4,128)}), f32[2,2,64,4,128]{4,3,2,0,1:T(4,128)}) %all-reduce.8.cloned.1.call-update) | async-done | bytes 524304 | tf_op jit(solution)/shard_map/psum | solution.py:259
  822.3 14.2 %reshape.614 = bf16[128,2,16384]{2,1,0:T(2,128)(2,1)} reshape(bf16[256,16384]{1,0:T(8,128)(2,1)} %convolution_convert_fusion) | data formatting | bytes 16777216 | tf_op jit(solution)/shard_map/reshape | solution.py:264
  836.5 11.2 %all-to-all-start.1 = ((bf16[128,2,16384]{2,1,0:T(2,128)(2,1)}), bf16[128,2,16384]{2,1,0:T(2,128)(2,1)}, u32[]{:S(2)}, u32[]{:S(2)}) async-start(bf16[128,2,16384]{2,1,0:T(2,128)(2,1)} %reshape.614), calls=%async_computation.1 | async-start | bytes 16777216 | tf_op jit(solution)/shard_map/all_to_all | solution.py:263
  847.7 3.2 copy.304
  851.0 2.6 reshape.608
  853.6 2.4 fusion.61
  857.0 2.1 fusion.55
  859.1 2.2 copy.340
  861.3 1.6 copy.339
  862.8 1.6 add_convert_fusion.1
  864.6 1.4 copy.325
  867.6 163.5 %all-to-all-done.1 = bf16[128,2,16384]{2,1,0:T(2,128)(2,1)} async-done(((bf16[128,2,16384]{2,1,0:T(2,128)(2,1)}), bf16[128,2,16384]{2,1,0:T(2,128)(2,1)}, u32[]{:S(2)}, u32[]{:S(2)}) %all-to-all-start.1) | async-done | bytes 8388640 | tf_op jit(solution)/shard_map/all_to_all | solution.py:263
  1031.1 13.1 %reshape.615 = bf16[256,16384]{1,0:T(8,128)(2,1)} reshape(bf16[128,2,16384]{2,1,0:T(2,128)(2,1)} %all-to-all-done.1) | data formatting | bytes 16777216 | tf_op jit(solution)/shard_map/reshape | solution.py:265
  1044.2 12.0 %copy.318 = bf16[256,16384]{0,1:T(8,128)(2,1)} copy(bf16[256,16384]{1,0:T(8,128)(2,1)} %reshape.615) | data formatting | bytes 16777216 | tf_op jit(solution)/shard_map/reshape | solution.py:265
  1056.2 5.7 fusion.17
  (153 shorter events, 36.8 us)
Async XLA Ops:
  7.2 14.8 %copy-start.15 = (bf16[256,512]{1,0:T(8,128)(2,1)S(1)}, bf16[256,512]{1,0:T(8,128)(2,1)}, u32[]{:S(2)}) copy-start(bf16[256,512]{1,0:T(8,128)(2,1)} %param.13) | copy-start | bytes 786436
  7.2 10.9 %copy-start.20 = (s32[2]{0:T(128)S(1)}, s32[2]{0:T(128)}, u32[]{:S(2)}) copy-start(s32[2]{0:T(128)} %param.16) | copy-start | bytes 28
  7.2 384.4 %all-reduce.10.cloned.1.call-start = ((), (), s32[]{:S(2)}) async-start(), calls=%async_computation.3 | async-start | bytes 524288 | tf_op jit(solution)/shard_map/psum | solution.py:34
  10.5 16.2 %copy-start.17 = (s32[4,4,3]{1,0,2:T(4,128)S(1)}, s32[4,4,3]{1,0,2:T(4,128)}, u32[]{:S(2)}) copy-start(s32[4,4,3]{1,0,2:T(4,128)} %param.15) | copy-start | bytes 580
  11.5 377.6 %collective-permute-start = (bf16[2,64,512]{1,2,0:T(8,128)(2,1)}, bf16[2,64,512]{1,2,0:T(8,128)(2,1)}, u32[]{:S(2)}, u32[]{:S(2)}) collective-permute-start(bf16[2,64,512]{1,2,0:T(8,128)(2,1)} %get-tuple-element.102), channel_id=1, source_target_pairs={{0,2},{2,4},{4,6},{6,8},{8,10},{10,12},{12,14},{14,16},{16,18},{18... | collective-permute-start | bytes 393224 | tf_op jit(solution)/shard_map/ppermute | solution.py:26
  15.4 373.8 %collective-permute-start.1 = (bf16[2,64,512]{1,2,0:T(8,128)(2,1)}, bf16[2,64,512]{1,2,0:T(8,128)(2,1)}, u32[]{:S(2)}, u32[]{:S(2)}) collective-permute-start(bf16[2,64,512]{1,2,0:T(8,128)(2,1)} %get-tuple-element.103), channel_id=1, source_target_pairs={{2,0},{4,2},{6,4},{8,6},{10,8},{12,10},{14,12},{16,14},{18,16},{20... | collective-permute-start | bytes 393224 | tf_op jit(solution)/shard_map/ppermute | solution.py:27
  377.2 0.6 copy-start.16
  406.7 26.7 %copy-start.12 = (bf16[256,2048]{1,0:T(8,128)(2,1)S(1)}, bf16[256,2048]{1,0:T(8,128)(2,1)}, u32[]{:S(2)}) copy-start(bf16[256,2048]{1,0:T(8,128)(2,1)} %param.17) | copy-start | bytes 3145732
  406.7 28.2 %copy-start.13 = (bf16[256,2048]{1,0:T(8,128)(2,1)S(1)}, bf16[256,2048]{1,0:T(8,128)(2,1)}, u32[]{:S(2)}) copy-start(bf16[256,2048]{1,0:T(8,128)(2,1)} %param.11) | copy-start | bytes 3145732
  406.7 144.8 %all-to-all-start = ((bf16[128,2,16384]{2,1,0:T(2,128)(2,1)}), bf16[128,2,16384]{2,1,0:T(2,128)(2,1)}, u32[]{:S(2)}, u32[]{:S(2)}) async-start(bf16[128,2,16384]{2,1,0:T(2,128)(2,1)} %reshape.604), calls=%async_computation | async-start | bytes 16777216 | tf_op jit(solution)/shard_map/all_to_all | solution.py:181
  420.7 401.6 %all-reduce.8.cloned.1.call-start = ((), (), s32[]{:S(2)}) async-start(), calls=%async_computation.2 | async-start | bytes 1048576 | tf_op jit(solution)/shard_map/psum | solution.py:259
  445.7 1.1 copy-start.3
  572.4 2.5 slice-start
  572.6 2.4 copy-start.6
  572.6 3.0 slice-start.1
  575.6 2.0 copy-start.14
  577.6 3.6 copy-start.10
  588.4 17.6 %copy-start.4 = (bf16[4,4,4,64,192]{4,3,2,1,0:T(8,128)(2,1)}, bf16[4,4,4,64,192]{4,3,2,1,0:T(8,128)(2,1)S(1)}, u32[]{:S(2)}) copy-start(bf16[4,4,4,64,192]{4,3,2,1,0:T(8,128)(2,1)S(1)} %fusion.8) | copy-start | bytes 4718596
  591.3 4.0 copy-start
  600.4 2.3 copy-start.2
  607.8 2.5 copy-start.9
  612.4 11.6 %collective-permute-start.3 = (bf16[2,64,4,128]{3,2,1,0:T(4,128)(2,1)S(1)}, bf16[2,64,4,128]{3,2,1,0:T(4,128)(2,1)S(1)}, u32[]{:S(2)}, u32[]{:S(2)}) collective-permute-start(bf16[2,64,4,128]{3,2,1,0:T(4,128)(2,1)S(1)} %get-tuple-element.89), channel_id=1, source_target_pairs={{0,2},{2,4},{4,6},{6,8},{8,10},{10,12},{12,14},{14,16},{16,18},{18... | collective-permute-start | bytes 393224 | tf_op jit(solution)/shard_map/ppermute | solution.py:40
  614.3 9.7 collective-permute-start.2
  836.5 194.6 %all-to-all-start.1 = ((bf16[128,2,16384]{2,1,0:T(2,128)(2,1)}), bf16[128,2,16384]{2,1,0:T(2,128)(2,1)}, u32[]{:S(2)}, u32[]{:S(2)}) async-start(bf16[128,2,16384]{2,1,0:T(2,128)(2,1)} %reshape.614), calls=%async_computation.1 | async-start | bytes 16777216 | tf_op jit(solution)/shard_map/all_to_all | solution.py:263
  847.7 5.9 copy-start.1
  853.6 2.4 copy-start.5
  853.6 2.4 copy-start.7
  862.8 3.2 copy-start.8
  864.5 1.6 copy-start.18
  866.0 1.4 copy-start.11
  1056.2 5.8 copy-start.19
Sparse Core Ops, SparseCore 0:
  26.8 218.4 all-reduce.9
  610.4 211.8 all-reduce.7

commit v2 on v1

--- a/solution.py
+++ b/solution.py
@@ -120,6 +120,10 @@
     return (ids[:, None] == jnp.arange(count, dtype=jnp.int32)[None, :]).astype(jnp.bfloat16)
 
 
+def exchange(array):
+    return lax.all_to_all(array, "seq", 0, 0, tiled=True)
+
+
 def local(queries, key_states, value_states, positions, random_blocks, global_blocks, out_grad):
     tok_rows = queries.shape[0]
     block_rows = tok_rows // BLK
@@ -130,57 +134,64 @@
     capacity = (slot_count + seq_count - 1) // seq_count + 1
     score_scale = 1.0 / math.sqrt(HD)
     table_rows = block_rows * kv_dev
-
-    all_blocks = lax.all_gather(random_blocks, "seq").reshape(seq_count, slot_count)
+    piece = 2 * BLK * kv_dev * HD // seq_count
+    code_cols = 128
+
+    cosines, sine_vals = tables(positions)
+    q_rot = rotate(
+        queries.reshape(tok_rows, kv_dev * GROUP, HD).astype(jnp.float32), cosines, sine_vals
+    ).astype(jnp.bfloat16)
+    k_rot = rotate(
+        key_states.reshape(tok_rows, kv_dev, HD).astype(jnp.float32), cosines, sine_vals
+    ).astype(jnp.bfloat16)
+    paired = jnp.stack([k_rot.reshape(tok_rows, kv_dev * HD), value_states])
+    own_blocks = paired.reshape(2, block_rows, BLK, kv_dev, HD)
+
+    flat_ids = random_blocks.reshape(slot_count)
+    owners = flat_ids // block_rows
     head_ids = jnp.broadcast_to(
         jnp.arange(kv_dev, dtype=jnp.int32)[None, :, None], (block_rows, kv_dev, RND)
     ).reshape(slot_count)
+    req_code = flat_ids % block_rows * kv_dev + head_ids
     slot_ids = jnp.arange(slot_count, dtype=jnp.int32)
-    all_owners = all_blocks // block_rows
-    earlier = (all_owners[:, :, None] == all_owners[:, None, :]) & (
-        slot_ids[None, None, :] < slot_ids[None, :, None]
-    )
-    all_rank = jnp.sum(earlier, axis=2)
-    all_code = all_blocks % block_rows * kv_dev + head_ids[None, :]
-    mine = all_owners == my_index
-    asked_part = jnp.stack(
-        [jnp.sum(jnp.where(mine & (all_rank == c), all_code, 0), axis=1) for c in range(capacity)],
-        axis=1,
-    )
-    flat_ids = random_blocks.reshape(slot_count)
-    owners = flat_ids // block_rows
-    my_rank = lax.dynamic_index_in_dim(all_rank, my_index, 0, keepdims=False)
-    slot_pos = owners * capacity + my_rank
-
-    cosines, sine_vals = tables(positions)
-    q_rot = rotate(
-        queries.reshape(tok_rows, kv_dev * GROUP, HD).astype(jnp.float32), cosines, sine_vals
-    ).astype(jnp.bfloat16)
-    k_rot = rotate(
-        key_states.reshape(tok_rows, kv_dev, HD).astype(jnp.float32), cosines, sine_vals
-    ).astype(jnp.bfloat16)
-    paired = jnp.stack([k_rot.reshape(tok_rows, kv_dev * HD), value_states])
-    own_blocks = paired.reshape(2, block_rows, BLK, kv_dev, HD)
-
-    kv_table = own_blocks.transpose(1, 3, 0, 2, 4).reshape(table_rows, 2 * BLK * HD)
-    asked_flat = asked_part.reshape(seq_count * capacity)
-    answers = jnp.dot(
-        onehot(asked_flat, table_rows), kv_table, preferred_element_type=jnp.float32
-    ).astype(jnp.bfloat16)
-    padded = extended(paired, (("seq", 1),), BLK)
-    window_blocks = padded.reshape(2, block_rows + 2, BLK, kv_dev, HD)
+    earlier = (owners[:, None] == owners[None, :]) & (slot_ids[None, :] < slot_ids[:, None])
+    slot_pos = owners * capacity + jnp.sum(earlier, axis=1)
+    request = jnp.zeros((seq_count * capacity,), jnp.int32).at[slot_pos].set(req_code)
+    request = request.reshape(seq_count, capacity)
     glob_owner = global_blocks // block_rows
     glob_local = global_blocks % block_rows
-    glob_pieces = []
+    glob_scatter = []
     for which_glob in range(GLOB):
         glob_piece = lax.dynamic_index_in_dim(own_blocks, glob_local[which_glob], 1, keepdims=False)
-        glob_pieces.append(spread(glob_piece, "seq", glob_owner[which_glob]))
-    glob_kv = jnp.stack(glob_pieces, axis=1)
+        glob_piece = jnp.where(my_index == glob_owner[which_glob], glob_piece, jnp.zeros_like(glob_piece))
+        glob_scatter.append(glob_piece.reshape(seq_count, piece))
+    first_out = jnp.concatenate(
+        glob_scatter
+        + [request.astype(jnp.bfloat16), jnp.zeros((seq_count, code_cols - capacity), jnp.bfloat16)],
+        axis=1,
+    )
+    first_in = exchange(first_out)
+    asked_part = first_in[:, GLOB * piece : GLOB * piece + capacity].astype(jnp.int32)
+    my_pieces = jnp.stack(
+        [
+            lax.dynamic_index_in_dim(first_in, glob_owner[g], 0, keepdims=False)[g * piece : (g + 1) * piece]
+            for g in range(GLOB)
+        ]
+    )
+    glob_in = exchange(jnp.broadcast_to(my_pieces[None], (seq_count, GLOB, piece)))
+    glob_kv = glob_in.transpose(1, 0, 2).reshape(GLOB, 2, BLK, kv_dev, HD).transpose(1, 0, 2, 3, 4)
+
+    kv_table = own_blocks.transpose(1, 3, 0, 2, 4).reshape(table_rows, 2, BLK, HD)
+    asked_flat = asked_part.reshape(seq_count * capacity)
+    answers = jnp.einsum(
+        "sq,qkte->skte", onehot(asked_flat, table_rows), kv_table, preferred_element_type=jnp.float32
+    ).astype(jnp.bfloat16)
+    padded = extended(paired, (("seq", 1),), BLK)
     answers, padded, glob_kv = lax.optimization_barrier((answers, padded, glob_kv))
     window_blocks = padded.reshape(2, block_rows + 2, BLK, kv_dev, HD)
-    fetched = lax.all_to_all(
-        answers.reshape(seq_count, capacity, 2 * BLK * HD), "seq", 0, 0, tiled=True
-    ).reshape(seq_count * capacity, 2 * BLK * HD)
+    fetched = exchange(answers.reshape(seq_count, capacity, 2, BLK, HD)).reshape(
+        seq_count * capacity, 2, BLK, HD
+    )
 
     window_set = jnp.stack([window_blocks[:, offset : offset + block_rows] for offset in range(3)], axis=2)
     glob_set = jnp.broadcast_to(glob_kv[:, None], (2, block_rows, GLOB, BLK, kv_dev, HD))
@@ -240,9 +251,12 @@
             far_vgrad.reshape(block_rows, kv_dev, RND, BLK, HD),
         ],
         axis=3,
-    ).reshape(slot_count, 2 * BLK * HD).astype(jnp.bfloat16)
-    outgoing = jnp.dot(
-        onehot(slot_pos, seq_count * capacity).T, random_grad, preferred_element_type=jnp.float32
+    ).reshape(slot_count, 2, BLK, HD).astype(jnp.bfloat16)
+    outgoing = jnp.einsum(
+        "ps,pkte->skte",
+        onehot(slot_pos, seq_count * capacity),
+        random_grad,
+        preferred_element_type=jnp.float32,
     ).astype(jnp.bfloat16)
     query_portion = jnp.einsum(
         "rhgtk,rkhd->rthgd", near_sgrad, near_k, preferred_element_type=jnp.float32
@@ -253,23 +267,28 @@
     window_acc = jnp.pad(near_grad[:, :, 0], ((0, 0), (0, 2), (0, 0), (0, 0), (0, 0)))
     window_acc = window_acc + jnp.pad(near_grad[:, :, 1], ((0, 0), (1, 1), (0, 0), (0, 0), (0, 0)))
     window_acc = window_acc + jnp.pad(near_grad[:, :, 2], ((0, 0), (2, 0), (0, 0), (0, 0), (0, 0)))
-    glob_local_grad = jnp.sum(near_grad[:, :, 3:], axis=1)
     from_right = shifted(window_acc[:, 0].astype(jnp.bfloat16), "seq", -1).astype(jnp.float32)
     from_left = shifted(window_acc[:, block_rows + 1].astype(jnp.bfloat16), "seq", 1).astype(jnp.float32)
-    glob_grad = lax.psum(glob_local_grad, "seq")
+    glob_local_grad = jnp.sum(near_grad[:, :, 3:], axis=1)
+    glob_split = glob_local_grad.transpose(1, 0, 2, 3, 4).reshape(GLOB, seq_count, piece)
+    piece_sum = jnp.sum(exchange(glob_split.transpose(1, 0, 2)), axis=0)
+    to_owner = jnp.where(
+        jnp.arange(seq_count)[:, None, None] == glob_owner[None, :, None], piece_sum[None], 0.0
+    )
+    glob_grad = exchange(to_owner).transpose(1, 0, 2).reshape(GLOB, 2, BLK, kv_dev, HD)
     outgoing, from_right, from_left, glob_grad = lax.optimization_barrier(
         (outgoing, from_right, from_left, glob_grad)
     )
-    returned = lax.all_to_all(
-        outgoing.reshape(seq_count, capacity, 2 * BLK * HD), "seq", 0, 0, tiled=True
-    ).reshape(seq_count * capacity, 2 * BLK * HD)
+    returned = exchange(outgoing.reshape(seq_count, capacity, 2, BLK, HD)).reshape(
+        seq_count * capacity, 2, BLK, HD
+    )
 
     kv_grad = window_acc[:, 1 : block_rows + 1]
     kv_grad = kv_grad.at[:, block_rows - 1].add(from_right).at[:, 0].add(from_left)
-    glob_mine = jnp.where((glob_owner == my_index)[None, :, None, None, None], glob_grad, 0.0)
-    kv_grad = kv_grad.at[:, glob_local].add(glob_mine)
-    collected = jnp.dot(
-        onehot(asked_flat, table_rows).T, returned, preferred_element_type=jnp.float32
+    glob_mine = jnp.where((glob_owner == my_index)[:, None, None, None, None], glob_grad, 0.0)
+    kv_grad = kv_grad.at[:, glob_local].add(glob_mine.transpose(1, 0, 2, 3, 4))
+    collected = jnp.einsum(
+        "sq,skte->qkte", onehot(asked_flat, table_rows), returned, preferred_element_type=jnp.float32
     ).reshape(block_rows, kv_dev, 2, BLK, HD)
     kv_grad = kv_grad + collected.transpose(2, 0, 3, 1, 4)
 

time: 1080 us -> 611 us (0.57)
  blocking collectives: 348 us -> 0 us
  waiting for transfers between devices: 462 us -> 356 us
  local copies, waits for them, and re-layouts: 123 us -> 93.6 us
  starting transfers between devices: 49.3 us -> 73.7 us
    all_gather x1 -> x0, blocking collectives: 348 us -> none  [local(): lax.all_gather(random_blocks, 'seq').reshape(seq_count, slot_count)]
    psum x2 -> x0, waiting for transfers between devices: 198 us -> none  [the longest x1 198 us: local(): glob_grad = lax.psum(glob_local_grad, 'seq')]
    all_to_all x2 -> x6, waiting for transfers between devices: 265 us -> 353 us  [exchange(): return lax.all_to_all(array, 'seq', 0, 0, tiled=True)]
    reshape x8, local copies, waits for them, and re-layouts: 67.9 us -> 21.9 us  [the longest x1 9.99 us: local(): outgoing.reshape(seq_count, capacity, 2, BLK, HD)]
    all_to_all x2 -> x6, starting transfers between devices: 25.2 us -> 62 us  [exchange(): return lax.all_to_all(array, 'seq', 0, 0, tiled=True)]
    all_to_all x0 -> x3, local copies, waits for them, and re-layouts: none -> 17.1 us  [exchange(): return lax.all_to_all(array, 'seq', 0, 0, tiled=True)]
    psum x2 -> x0, starting transfers between devices: 11.8 us -> none  [the longest x1 11.7 us: local(): glob_grad = lax.psum(glob_local_grad, 'seq')]
  transfers between devices with their start and end apart: 8 -> 10, of which waited for: 3 -> 7; matrix products, arithmetic and copies ran while one was open for 6% -> 10% of each run, Pallas kernels for 0% -> 0%
where the time goes in v2:
time: 611 us; the launch traced here: 602 us
  waiting for transfers between devices  356 us (58%)
  local copies, waits for them, and re-layouts  93.6 us (15%)
  starting transfers between devices  73.7 us (12%)
  matrix products  42 us (7%)
  other arithmetic  25.4 us (4%)
  between operations  11.1 us (2%)
    all_to_all x6, waiting for transfers between devices, exchange(): return lax.all_to_all(array, 'seq', 0, 0, tiled=True)  353 us
    all_to_all x6, starting transfers between devices, exchange(): return lax.all_to_all(array, 'seq', 0, 0, tiled=True)  62 us
    unnamed x71, local copies, waits for them, and re-layouts  19.9 us
    all_to_all x3, local copies, waits for them, and re-layouts, exchange(): return lax.all_to_all(array, 'seq', 0, 0, tiled=True)  17.1 us
  transfers between devices with their start and end apart: 10, of which 7 were waited for; matrix products, arithmetic and copies ran while one was open for 10% of the time, Pallas kernels for 0%

profile of v2, /device:TPU:32, one launch (start us, length us, event | category | flops | bytes accessed | tf_op | source)
XLA Modules:
  0.0 601.6 jit_solution(6933492390591966453)
XLA Ops:
  18.4 15.0 %all-to-all-start = ((bf16[128,2,576]{2,1,0:T(2,128)(2,1)}), bf16[128,2,576]{2,1,0:T(2,128)(2,1)S(1)}, u32[]{:S(2)}, u32[]{:S(2)}) async-start(bf16[128,2,576]{2,1,0:T(2,128)(2,1)} %reshape.659), calls=%async_computation | async-start | bytes 655360 | tf_op jit(solution)/shard_map/all_to_all | solution.py:124
  33.7 2.8 collective-permute-start.1
  36.5 3.0 collective-permute-start
  43.9 3.1 collective-permute-done.1
  48.3 1.8 all-to-all-done
  51.6 11.6 %all-to-all-start.1 = ((bf16[128,2,512]{2,1,0:T(2,128)(2,1)}), bf16[128,2,512]{2,1,0:T(2,128)(2,1)S(1)}, u32[]{:S(2)}, u32[]{:S(2)}) async-start(bf16[128,2,512]{2,1,0:T(2,128)(2,1)} %broadcast_in_dim.165), calls=%async_computation.1 | async-start | bytes 524288 | tf_op jit(solution)/shard_map/all_to_all | solution.py:124
  63.4 5.7 convolution_convert_fusion.1
  69.0 7.9 %all-to-all-done.1 = bf16[128,2,512]{2,1,0:T(2,128)(2,1)S(1)} async-done(((bf16[128,2,512]{2,1,0:T(2,128)(2,1)}), bf16[128,2,512]{2,1,0:T(2,128)(2,1)S(1)}, u32[]{:S(2)}, u32[]{:S(2)}) %all-to-all-start.1) | async-done | bytes 262176 | tf_op jit(solution)/shard_map/all_to_all | solution.py:124
  77.2 10.0 %copy.248 = bf16[128,2,2,64,128]{4,1,3,2,0:T(2,128)(2,1)} copy(bf16[128,2,2,64,128]{4,1,0,3,2:T(2,128)(2,1)} %bitcast.233) | data formatting | bytes 16777216 | tf_op jit(solution)/shard_map/reshape | solution.py:192
  87.2 8.5 %all-to-all-start.2 = ((bf16[128,2,2,64,128]{4,1,3,2,0:T(2,128)(2,1)}), bf16[128,2,2,64,128]{4,1,3,2,0:T(2,128)(2,1)}, u32[]{:S(2)}, u32[]{:S(2)}) async-start(bf16[128,2,2,64,128]{4,1,3,2,0:T(2,128)(2,1)} %copy.248), calls=%async_computation.2 | async-start | bytes 16777216 | tf_op jit(solution)/shard_map/all_to_all | solution.py:124
  95.7 1.5 reshape.607
  106.8 1.6 fusion.60
  109.5 3.7 bitcast_reduce_fusion
  113.2 168.9 %all-to-all-done.2 = bf16[128,2,2,64,128]{4,1,3,2,0:T(2,128)(2,1)} async-done(((bf16[128,2,2,64,128]{4,1,3,2,0:T(2,128)(2,1)}), bf16[128,2,2,64,128]{4,1,3,2,0:T(2,128)(2,1)}, u32[]{:S(2)}, u32[]{:S(2)}) %all-to-all-start.2) | async-done | bytes 8388640 | tf_op jit(solution)/shard_map/all_to_all | solution.py:124
  282.1 9.2 %copy.249 = bf16[128,2,2,64,128]{4,3,2,1,0:T(8,128)(2,1)} copy(bf16[128,2,2,64,128]{4,1,3,2,0:T(2,128)(2,1)} %all-to-all-done.2) | data formatting | bytes 16777216 | tf_op jit(solution)/shard_map/all_to_all | solution.py:124
  291.2 4.2 gather_fusion
  297.4 5.7 fusion.5
  303.1 1.5 fusion.11
  304.7 3.6 fusion.15
  308.3 3.1 bitcast_convert_fusion
  311.4 2.1 fusion.17
  313.5 2.9 multiply_reduce_fusion
  316.5 2.8 fusion.2
  321.0 1.9 copy_dynamic-update-slice_fusion.1
  323.4 2.1 copy_dynamic-update-slice_fusion
  325.6 2.4 copy-done.3
  329.7 5.6 all-to-all-start.3
  335.3 4.0 fusion.8
  341.2 11.5 %all-to-all-done.3 = f32[128,2,512]{2,1,0:T(2,128)S(1)} async-done(((f32[128,2,512]{2,1,0:T(2,128)}), f32[128,2,512]{2,1,0:T(2,128)S(1)}, u32[]{:S(2)}, u32[]{:S(2)}) %all-to-all-start.3) | async-done | bytes 524320 | tf_op jit(solution)/shard_map/all_to_all | solution.py:124
  354.0 6.6 %all-to-all-start.4 = ((f32[128,2,512]{2,1,0:T(2,128)}), f32[128,2,512]{2,1,0:T(2,128)S(1)}, u32[]{:S(2)}, u32[]{:S(2)}) async-start(f32[128,2,512]{2,1,0:T(2,128)} %broadcast_select_fusion), calls=%async_computation.4 | async-start | bytes 1048576 | tf_op jit(solution)/shard_map/all_to_all | solution.py:124
  360.6 2.2 slice_bitcast_fusion.2
  362.8 1.7 fusion.59
  364.6 2.9 collective-permute-start.2
  367.5 2.9 collective-permute-start.3
  370.5 5.7 convolution_convert_fusion
  379.8 10.0 %copy.267 = bf16[128,2,2,64,128]{4,1,3,2,0:T(2,128)(2,1)} copy(bf16[128,2,2,64,128]{4,1,0,3,2:T(2,128)(2,1)} %bitcast.232) | data formatting | bytes 16777216 | tf_op jit(solution)/shard_map/reshape | solution.py:282
  389.8 14.7 %all-to-all-start.5 = ((bf16[128,2,2,64,128]{4,1,3,2,0:T(2,128)(2,1)}), bf16[128,2,2,64,128]{4,1,3,2,0:T(2,128)(2,1)}, u32[]{:S(2)}, u32[]{:S(2)}) async-start(bf16[128,2,2,64,128]{4,1,3,2,0:T(2,128)(2,1)} %copy.267), calls=%async_computation.5 | async-start | bytes 16777216 | tf_op jit(solution)/shard_map/all_to_all | solution.py:124
  404.5 3.2 copy.252
  407.7 2.6 reshape.606
  410.3 2.4 fusion.67
  413.7 2.1 fusion.61
  415.8 2.2 copy.294
  418.0 1.6 copy.293
  419.5 1.6 add_convert_fusion.1
  424.8 1.7 fusion.29
  426.5 161.2 %all-to-all-done.5 = bf16[128,2,2,64,128]{4,1,3,2,0:T(2,128)(2,1)} async-done(((bf16[128,2,2,64,128]{4,1,3,2,0:T(2,128)(2,1)}), bf16[128,2,2,64,128]{4,1,3,2,0:T(2,128)(2,1)}, u32[]{:S(2)}, u32[]{:S(2)}) %all-to-all-start.5) | async-done | bytes 8388640 | tf_op jit(solution)/shard_map/all_to_all | solution.py:124
  587.6 7.4 %copy.268 = bf16[128,2,2,64,128]{4,1,0,3,2:T(2,128)(2,1)S(1)} copy(bf16[128,2,2,64,128]{4,1,3,2,0:T(2,128)(2,1)} %all-to-all-done.5) | data formatting | bytes 16777216 | tf_op jit(solution)/shard_map/all_to_all | solution.py:124
  595.1 2.5 fusion.20
  (177 shorter events, 47.5 us)
Async XLA Ops:
  0.6 9.0 %copy-start.22 = (s32[2]{0:T(128)S(1)}, s32[2]{0:T(128)}, u32[]{:S(2)}) copy-start(s32[2]{0:T(128)} %param.16) | copy-start | bytes 28
  9.3 24.1 %copy-start.16 = (bf16[256,512]{1,0:T(8,128)(2,1)S(1)}, bf16[256,512]{1,0:T(8,128)(2,1)}, u32[]{:S(2)}) copy-start(bf16[256,512]{1,0:T(8,128)(2,1)} %param.13) | copy-start | bytes 786436
  13.7 34.6 %copy-start.23 = (s32[48]{0:T(128)}, s32[48]{0:T(128)S(1)}, u32[]{:S(2)}) copy-start(s32[48]{0:T(128)S(1)} %get-tuple-element.104) | copy-start | bytes 580
  13.9 0.6 copy-start.24
  14.5 0.5 copy-start.21
  18.4 31.7 %all-to-all-start = ((bf16[128,2,576]{2,1,0:T(2,128)(2,1)}), bf16[128,2,576]{2,1,0:T(2,128)(2,1)S(1)}, u32[]{:S(2)}, u32[]{:S(2)}) async-start(bf16[128,2,576]{2,1,0:T(2,128)(2,1)} %reshape.659), calls=%async_computation | async-start | bytes 655360 | tf_op jit(solution)/shard_map/all_to_all | solution.py:124
  33.7 13.3 %collective-permute-start.1 = (bf16[2,64,512]{1,2,0:T(8,128)(2,1)S(1)}, bf16[2,64,512]{1,2,0:T(8,128)(2,1)S(1)}, u32[]{:S(2)}, u32[]{:S(2)}) collective-permute-start(bf16[2,64,512]{1,2,0:T(8,128)(2,1)S(1)} %get-tuple-element.95), channel_id=1, source_target_pairs={{2,0},{4,2},{6,4},{8,6},{10,8},{12,10},{14,12},{16,14},{18,16},{20... | collective-permute-start | bytes 393224 | tf_op jit(solution)/shard_map/ppermute | solution.py:27
  36.5 10.5 %collective-permute-start = (bf16[2,64,512]{1,2,0:T(8,128)(2,1)S(1)}, bf16[2,64,512]{1,2,0:T(8,128)(2,1)S(1)}, u32[]{:S(2)}, u32[]{:S(2)}) collective-permute-start(bf16[2,64,512]{1,2,0:T(8,128)(2,1)S(1)} %get-tuple-element.94), channel_id=1, source_target_pairs={{0,2},{2,4},{4,6},{6,8},{8,10},{10,12},{12,14},{14,16},{16,18},{18... | collective-permute-start | bytes 393224 | tf_op jit(solution)/shard_map/ppermute | solution.py:26
  51.6 25.4 %all-to-all-start.1 = ((bf16[128,2,512]{2,1,0:T(2,128)(2,1)}), bf16[128,2,512]{2,1,0:T(2,128)(2,1)S(1)}, u32[]{:S(2)}, u32[]{:S(2)}) async-start(bf16[128,2,512]{2,1,0:T(2,128)(2,1)} %broadcast_in_dim.165), calls=%async_computation.1 | async-start | bytes 524288 | tf_op jit(solution)/shard_map/all_to_all | solution.py:124
  87.2 8.5 %copy-start.13 = (bf16[256,2048]{1,0:T(8,128)(2,1)S(1)}, bf16[256,2048]{1,0:T(8,128)(2,1)}, u32[]{:S(2)}) copy-start(bf16[256,2048]{1,0:T(8,128)(2,1)} %param.17) | copy-start | bytes 3145732
  87.2 10.3 %copy-start.14 = (bf16[256,2048]{1,0:T(8,128)(2,1)S(1)}, bf16[256,2048]{1,0:T(8,128)(2,1)}, u32[]{:S(2)}) copy-start(bf16[256,2048]{1,0:T(8,128)(2,1)} %param.11) | copy-start | bytes 3145732
  87.2 194.9 %all-to-all-start.2 = ((bf16[128,2,2,64,128]{4,1,3,2,0:T(2,128)(2,1)}), bf16[128,2,2,64,128]{4,1,3,2,0:T(2,128)(2,1)}, u32[]{:S(2)}, u32[]{:S(2)}) async-start(bf16[128,2,2,64,128]{4,1,3,2,0:T(2,128)(2,1)} %copy.248), calls=%async_computation.2 | async-start | bytes 16777216 | tf_op jit(solution)/shard_map/all_to_all | solution.py:124
  108.4 1.1 copy-start.4
  295.6 0.9 copy-start.7
  295.6 17.9 %copy-start.17 = (bf16[4,4,3,1,64,128]{5,4,3,2,1,0:T(8,128)(2,1)}, bf16[4,4,3,1,64,128]{5,4,3,2,1,0:T(8,128)(2,1)S(1)}, u32[]{:S(2)}) copy-start(bf16[4,4,3,1,64,128]{5,4,3,2,1,0:T(8,128)(2,1)S(1)} %get-tuple-element.79) | copy-start | bytes 2359300
  296.5 8.1 %slice-start = ((s8[6291456]{0:T(1024)(128)(4,1)}), s8[4194304]{0:T(1024)(128)(4,1)S(1)}, s32[]{:S(2)}) async-start(s8[6291456]{0:T(1024)(128)(4,1)} %bitcast.234), calls=%async_computation.6 | async-start | bytes 8388608
  297.4 16.2 %copy-start = (f32[4,4,192,64,4]{2,3,4,1,0:T(8,128)}, f32[4,4,192,64,4]{2,3,4,1,0:T(8,128)S(1)}, u32[]{:S(2)}) copy-start(f32[4,4,192,64,4]{2,3,4,1,0:T(8,128)S(1)} %get-tuple-element.112) | copy-start | bytes 9437188
  297.4 7.2 %slice-start.1 = ((s8[6291456]{0:T(1024)(128)(4,1)}), s8[2097152]{0:T(1024)(128)(4,1)S(1)}, s32[]{:S(2)}) async-start(s8[6291456]{0:T(1024)(128)(4,1)} %bitcast.234), calls=%async_computation.7 | async-start | bytes 4194304
  303.1 1.5 copy-start.15
  308.2 3.1 copy-start.11
  319.3 1.7 copy-start.1
  325.6 2.4 copy-start.3
  329.7 23.0 %all-to-all-start.3 = ((f32[128,2,512]{2,1,0:T(2,128)}), f32[128,2,512]{2,1,0:T(2,128)S(1)}, u32[]{:S(2)}, u32[]{:S(2)}) async-start(f32[128,2,512]{2,1,0:T(2,128)} %copy.265), calls=%async_computation.3 | async-start | bytes 1048576 | tf_op jit(solution)/shard_map/all_to_all | solution.py:124
  339.3 1.4 copy-start.5
  354.0 24.5 %all-to-all-start.4 = ((f32[128,2,512]{2,1,0:T(2,128)}), f32[128,2,512]{2,1,0:T(2,128)S(1)}, u32[]{:S(2)}, u32[]{:S(2)}) async-start(f32[128,2,512]{2,1,0:T(2,128)} %broadcast_select_fusion), calls=%async_computation.4 | async-start | bytes 1048576 | tf_op jit(solution)/shard_map/all_to_all | solution.py:124
  362.8 7.7 %copy-start.20 = (s32[48]{0:T(128)S(1)}, s32[48]{0:T(128)}, u32[]{:S(2)}) copy-start(s32[48]{0:T(128)} %multiply_add_fusion.2) | copy-start | bytes 580
  364.6 11.6 %collective-permute-start.2 = (bf16[2,64,4,128]{3,2,1,0:T(4,128)(2,1)S(1)}, bf16[2,64,4,128]{3,2,1,0:T(4,128)(2,1)S(1)}, u32[]{:S(2)}, u32[]{:S(2)}) collective-permute-start(bf16[2,64,4,128]{3,2,1,0:T(4,128)(2,1)S(1)} %get-tuple-element.82), channel_id=1, source_target_pairs={{2,0},{4,2},{6,4},{8,6},{10,8},{12,10},{14,12},{16,14},{18,16},{20... | collective-permute-start | bytes 393224 | tf_op jit(solution)/shard_map/ppermute | solution.py:40
  367.5 8.7 %collective-permute-start.3 = (bf16[2,64,4,128]{3,2,1,0:T(4,128)(2,1)S(1)}, bf16[2,64,4,128]{3,2,1,0:T(4,128)(2,1)S(1)}, u32[]{:S(2)}, u32[]{:S(2)}) collective-permute-start(bf16[2,64,4,128]{3,2,1,0:T(4,128)(2,1)S(1)} %get-tuple-element.81), channel_id=1, source_target_pairs={{0,2},{2,4},{4,6},{6,8},{8,10},{10,12},{12,14},{14,16},{16,18},{18... | collective-permute-start | bytes 393224 | tf_op jit(solution)/shard_map/ppermute | solution.py:40
  389.8 197.8 %all-to-all-start.5 = ((bf16[128,2,2,64,128]{4,1,3,2,0:T(2,128)(2,1)}), bf16[128,2,2,64,128]{4,1,3,2,0:T(2,128)(2,1)}, u32[]{:S(2)}, u32[]{:S(2)}) async-start(bf16[128,2,2,64,128]{4,1,3,2,0:T(2,128)(2,1)} %copy.267), calls=%async_computation.5 | async-start | bytes 16777216 | tf_op jit(solution)/shard_map/all_to_all | solution.py:124
  404.5 5.8 copy-start.2
  410.3 2.4 copy-start.6
  410.3 2.4 copy-start.8
  419.5 3.2 copy-start.9
  421.2 2.6 copy-start.10
  421.2 2.6 copy-start.18
  422.7 2.1 copy-start.12
  595.0 2.7 copy-start.19

commit v3 on v2

--- a/solution.py
+++ b/solution.py
@@ -124,6 +124,12 @@
     return lax.all_to_all(array, "seq", 0, 0, tiled=True)
 
 
+def pick(ids, table):
+    return jnp.einsum(
+        "sq,qte->ste", onehot(ids, table.shape[0]), table, preferred_element_type=jnp.float32
+    )
+
+
 def local(queries, key_states, value_states, positions, random_blocks, global_blocks, out_grad):
     tok_rows = queries.shape[0]
     block_rows = tok_rows // BLK
@@ -135,6 +141,7 @@
     score_scale = 1.0 / math.sqrt(HD)
     table_rows = block_rows * kv_dev
     piece = 2 * BLK * kv_dev * HD // seq_count
+    glob_rows = GLOB * piece // HD
     code_cols = 128
 
     cosines, sine_vals = tables(positions)
@@ -172,27 +179,32 @@
     )
     first_in = exchange(first_out)
     asked_part = first_in[:, GLOB * piece : GLOB * piece + capacity].astype(jnp.int32)
-    my_pieces = jnp.stack(
+    my_pieces = jnp.concatenate(
         [
             lax.dynamic_index_in_dim(first_in, glob_owner[g], 0, keepdims=False)[g * piece : (g + 1) * piece]
             for g in range(GLOB)
         ]
     )
-    glob_in = exchange(jnp.broadcast_to(my_pieces[None], (seq_count, GLOB, piece)))
+    asked_flat = asked_part.reshape(seq_count * capacity)
+
+    k_table = own_blocks[0].transpose(0, 2, 1, 3).reshape(table_rows, BLK, HD)
+    v_table = own_blocks[1].transpose(0, 2, 1, 3).reshape(table_rows, BLK, HD)
+    answers_k = pick(asked_flat, k_table).astype(jnp.bfloat16).reshape(seq_count, capacity * BLK, HD)
+    answers_k = jnp.concatenate(
+        [answers_k, jnp.broadcast_to(my_pieces.reshape(1, glob_rows, HD), (seq_count, glob_rows, HD))],
+        axis=1,
+    )
+    answers_v = pick(asked_flat, v_table).astype(jnp.bfloat16).reshape(seq_count, capacity * BLK, HD)
+    padded = extended(paired, (("seq", 1),), BLK)
+    answers_k, padded = lax.optimization_barrier((answers_k, padded))
+    fetched_k = exchange(answers_k)
+    answers_v, fetched_k = lax.optimization_barrier((answers_v, fetched_k))
+    fetched_v = exchange(answers_v).reshape(seq_count * capacity, BLK, HD)
+    glob_in = fetched_k[:, capacity * BLK :].reshape(seq_count, GLOB, piece)
+    fetched_k = fetched_k[:, : capacity * BLK].reshape(seq_count * capacity, BLK, HD)
     glob_kv = glob_in.transpose(1, 0, 2).reshape(GLOB, 2, BLK, kv_dev, HD).transpose(1, 0, 2, 3, 4)
 
-    kv_table = own_blocks.transpose(1, 3, 0, 2, 4).reshape(table_rows, 2, BLK, HD)
-    asked_flat = asked_part.reshape(seq_count * capacity)
-    answers = jnp.einsum(
-        "sq,qkte->skte", onehot(asked_flat, table_rows), kv_table, preferred_element_type=jnp.float32
-    ).astype(jnp.bfloat16)
-    padded = extended(paired, (("seq", 1),), BLK)
-    answers, padded, glob_kv = lax.optimization_barrier((answers, padded, glob_kv))
     window_blocks = padded.reshape(2, block_rows + 2, BLK, kv_dev, HD)
-    fetched = exchange(answers.reshape(seq_count, capacity, 2, BLK, HD)).reshape(
-        seq_count * capacity, 2, BLK, HD
-    )
-
     window_set = jnp.stack([window_blocks[:, offset : offset + block_rows] for offset in range(3)], axis=2)
     glob_set = jnp.broadcast_to(glob_kv[:, None], (2, block_rows, GLOB, BLK, kv_dev, HD))
     near_set = jnp.concatenate([window_set, glob_set], axis=2).reshape(
@@ -209,21 +221,17 @@
     grad_nat = out_grad.reshape(block_rows, BLK, kv_dev, GROUP, HD)
     near_k = near_set[0]
     near_v = near_set[1]
+    far_k = fetched_k[slot_pos].reshape(block_rows, kv_dev, RND * BLK, HD)
+    far_v = fetched_v[slot_pos].reshape(block_rows, kv_dev, RND * BLK, HD)
     near_scores = (
         jnp.einsum("rthgd,rkhd->rhgtk", query_nat, near_k, preferred_element_type=jnp.float32)
         * score_scale
     )
     near_scores = jnp.where(near_mask[:, None, None, None, :], near_scores, NEG_FILL)
-    near_wgrad = jnp.einsum("rthgd,rkhd->rhgtk", grad_nat, near_v, preferred_element_type=jnp.float32)
-
-    random_kv = fetched[slot_pos].reshape(block_rows, kv_dev, RND, 2, BLK, HD)
-    far_k = random_kv[:, :, :, 0].reshape(block_rows, kv_dev, RND * BLK, HD)
-    far_v = random_kv[:, :, :, 1].reshape(block_rows, kv_dev, RND * BLK, HD)
     far_scores = (
         jnp.einsum("rthgd,rhkd->rhgtk", query_nat, far_k, preferred_element_type=jnp.float32)
         * score_scale
     )
-    far_wgrad = jnp.einsum("rthgd,rhkd->rhgtk", grad_nat, far_v, preferred_element_type=jnp.float32)
     row_max = jnp.maximum(
         jnp.max(near_scores, axis=-1, keepdims=True), jnp.max(far_scores, axis=-1, keepdims=True)
     )
@@ -234,6 +242,20 @@
     far_prob = far_exp / total
     near_w = near_prob.astype(jnp.bfloat16)
     far_w = far_prob.astype(jnp.bfloat16)
+
+    far_vgrad = jnp.einsum("rhgtk,rthgd->rhkd", far_w, grad_nat, preferred_element_type=jnp.float32)
+    out_v = jnp.einsum(
+        "ps,pte->ste",
+        onehot(slot_pos, seq_count * capacity),
+        far_vgrad.astype(jnp.bfloat16).reshape(slot_count, BLK, HD),
+        preferred_element_type=jnp.float32,
+    ).astype(jnp.bfloat16)
+    returned_v = exchange(out_v.reshape(seq_count, capacity * BLK, HD)).reshape(
+        seq_count * capacity, BLK, HD
+    )
+
+    near_wgrad = jnp.einsum("rthgd,rkhd->rhgtk", grad_nat, near_v, preferred_element_type=jnp.float32)
+    far_wgrad = jnp.einsum("rthgd,rhkd->rhgtk", grad_nat, far_v, preferred_element_type=jnp.float32)
     attended = (
         jnp.einsum("rhgtk,rkhd->rthgd", near_w, near_v, preferred_element_type=jnp.float32)
         + jnp.einsum("rhgtk,rhkd->rthgd", far_w, far_v, preferred_element_type=jnp.float32)
@@ -244,53 +266,50 @@
     far_sgrad = (far_prob * (far_wgrad - row_delta) * score_scale).astype(jnp.bfloat16)
 
     far_kgrad = jnp.einsum("rhgtk,rthgd->rhkd", far_sgrad, query_nat, preferred_element_type=jnp.float32)
-    far_vgrad = jnp.einsum("rhgtk,rthgd->rhkd", far_w, grad_nat, preferred_element_type=jnp.float32)
-    random_grad = jnp.stack(
-        [
-            far_kgrad.reshape(block_rows, kv_dev, RND, BLK, HD),
-            far_vgrad.reshape(block_rows, kv_dev, RND, BLK, HD),
-        ],
-        axis=3,
-    ).reshape(slot_count, 2, BLK, HD).astype(jnp.bfloat16)
-    outgoing = jnp.einsum(
-        "ps,pkte->skte",
+    out_k = jnp.einsum(
+        "ps,pte->ste",
         onehot(slot_pos, seq_count * capacity),
-        random_grad,
+        far_kgrad.astype(jnp.bfloat16).reshape(slot_count, BLK, HD),
         preferred_element_type=jnp.float32,
-    ).astype(jnp.bfloat16)
+    ).astype(jnp.bfloat16).reshape(seq_count, capacity * BLK, HD)
+    near_kgrad = jnp.einsum("rhgtk,rthgd->rkhd", near_sgrad, query_nat, preferred_element_type=jnp.float32)
+    near_vgrad = jnp.einsum("rhgtk,rthgd->rkhd", near_w, grad_nat, preferred_element_type=jnp.float32)
+    near_grad = jnp.stack([near_kgrad, near_vgrad]).reshape(2, block_rows, 3 + GLOB, BLK, kv_dev, HD)
+    glob_local_grad = jnp.sum(near_grad[:, :, 3:], axis=1)
+    glob_split = glob_local_grad.transpose(1, 0, 2, 3, 4).reshape(GLOB, seq_count, piece)
+    glob_split = glob_split.transpose(1, 0, 2).reshape(seq_count, glob_rows, HD)
+    glob_high = glob_split.astype(jnp.bfloat16)
+    glob_low = (glob_split - glob_high.astype(jnp.float32)).astype(jnp.bfloat16)
+    returned_k = exchange(jnp.concatenate([out_k, glob_high, glob_low], axis=1))
+    glob_back = returned_k[:, capacity * BLK :].astype(jnp.float32)
+    piece_sum = jnp.sum(glob_back[:, :glob_rows] + glob_back[:, glob_rows:], axis=0).reshape(GLOB, piece)
+    returned_k = returned_k[:, : capacity * BLK].reshape(seq_count * capacity, BLK, HD)
+    to_owner = jnp.where(
+        jnp.arange(seq_count)[:, None, None] == glob_owner[None, :, None], piece_sum[None], 0.0
+    )
+    glob_grad = exchange(to_owner).transpose(1, 0, 2).reshape(GLOB, 2, BLK, kv_dev, HD)
+
     query_portion = jnp.einsum(
         "rhgtk,rkhd->rthgd", near_sgrad, near_k, preferred_element_type=jnp.float32
     ) + jnp.einsum("rhgtk,rhkd->rthgd", far_sgrad, far_k, preferred_element_type=jnp.float32)
-    near_kgrad = jnp.einsum("rhgtk,rthgd->rkhd", near_sgrad, query_nat, preferred_element_type=jnp.float32)
-    near_vgrad = jnp.einsum("rhgtk,rthgd->rkhd", near_w, grad_nat, preferred_element_type=jnp.float32)
-    near_grad = jnp.stack([near_kgrad, near_vgrad]).reshape(2, block_rows, 3 + GLOB, BLK, kv_dev, HD)
     window_acc = jnp.pad(near_grad[:, :, 0], ((0, 0), (0, 2), (0, 0), (0, 0), (0, 0)))
     window_acc = window_acc + jnp.pad(near_grad[:, :, 1], ((0, 0), (1, 1), (0, 0), (0, 0), (0, 0)))
     window_acc = window_acc + jnp.pad(near_grad[:, :, 2], ((0, 0), (2, 0), (0, 0), (0, 0), (0, 0)))
     from_right = shifted(window_acc[:, 0].astype(jnp.bfloat16), "seq", -1).astype(jnp.float32)
     from_left = shifted(window_acc[:, block_rows + 1].astype(jnp.bfloat16), "seq", 1).astype(jnp.float32)
-    glob_local_grad = jnp.sum(near_grad[:, :, 3:], axis=1)
-    glob_split = glob_local_grad.transpose(1, 0, 2, 3, 4).reshape(GLOB, seq_count, piece)
-    piece_sum = jnp.sum(exchange(glob_split.transpose(1, 0, 2)), axis=0)
-    to_owner = jnp.where(
-        jnp.arange(seq_count)[:, None, None] == glob_owner[None, :, None], piece_sum[None], 0.0
-    )
-    glob_grad = exchange(to_owner).transpose(1, 0, 2).reshape(GLOB, 2, BLK, kv_dev, HD)
-    outgoing, from_right, from_left, glob_grad = lax.optimization_barrier(
-        (outgoing, from_right, from_left, glob_grad)
-    )
-    returned = exchange(outgoing.reshape(seq_count, capacity, 2, BLK, HD)).reshape(
-        seq_count * capacity, 2, BLK, HD
-    )
 
     kv_grad = window_acc[:, 1 : block_rows + 1]
     kv_grad = kv_grad.at[:, block_rows - 1].add(from_right).at[:, 0].add(from_left)
     glob_mine = jnp.where((glob_owner == my_index)[:, None, None, None, None], glob_grad, 0.0)
     kv_grad = kv_grad.at[:, glob_local].add(glob_mine.transpose(1, 0, 2, 3, 4))
-    collected = jnp.einsum(
-        "sq,skte->qkte", onehot(asked_flat, table_rows), returned, preferred_element_type=jnp.float32
-    ).reshape(block_rows, kv_dev, 2, BLK, HD)
-    kv_grad = kv_grad + collected.transpose(2, 0, 3, 1, 4)
+    oh_back = onehot(asked_flat, table_rows).T
+    collected = jnp.stack(
+        [
+            jnp.einsum("qs,ste->qte", oh_back, returned_k, preferred_element_type=jnp.float32),
+            jnp.einsum("qs,ste->qte", oh_back, returned_v, preferred_element_type=jnp.float32),
+        ]
+    ).reshape(2, block_rows, kv_dev, BLK, HD)
+    kv_grad = kv_grad + collected.transpose(0, 1, 3, 2, 4)
 
     attended = attended.reshape(tok_rows, kv_dev * GROUP * HD)
     query_grad = (

time: 611 us -> 532 us (0.87)
  waiting for transfers between devices: 356 us -> 289 us
  local copies, waits for them, and re-layouts: 93.6 us -> 78.1 us
    all_to_all x6, waiting for transfers between devices: 353 us -> 285 us  [exchange(): return lax.all_to_all(array, 'seq', 0, 0, tiled=True)]
    reshape x2 -> x3, local copies, waits for them, and re-layouts: 20 us -> 0.55 us  [the longest x1 0.42 us: local(): glob_split = glob_split.transpose(1, 0, 2).reshape(seq_count, glob_rows, HD)]
    all_to_all x3 -> x1, local copies, waits for them, and re-layouts: 17.1 us -> 0.51 us  [exchange(): return lax.all_to_all(array, 'seq', 0, 0, tiled=True)]
    convert_element_type x0 -> x4, local copies, waits for them, and re-layouts: none -> 14.8 us  [the longest x1 4.7 us: local(): out_v = jnp.einsum('ps,pte->ste', onehot(slot_pos, seq_count * capacity),...]
    slice x1 -> x3, local copies, waits for them, and re-layouts: 0.15 us -> 8.26 us  [the longest x1 4.79 us: local(): fetched_k[:, :capacity * BLK].reshape(seq_count * capacity, BLK, HD)]
    unnamed x71 -> x79, local copies, waits for them, and re-layouts: 19.9 us -> 16.7 us
    dot_general x3 -> x6, matrix products: 13.9 us -> 12.3 us  [the longest x1 4.55 us: local(): jnp.einsum('qs,ste->qte', oh_back, returned_v, preferred_element_type=jnp...]
  transfers between devices with their start and end apart: 10 -> 10, of which waited for: 7 -> 8; matrix products, arithmetic and copies ran while one was open for 10% -> 23% of each run, Pallas kernels for 0% -> 0%
where the time goes in v3:
time: 532 us; the launch traced here: 523 us
  waiting for transfers between devices  289 us (54%)
  local copies, waits for them, and re-layouts  78.1 us (15%)
  starting transfers between devices  72.5 us (14%)
  matrix products  47.5 us (9%)
  other arithmetic  24.6 us (5%)
  between operations  11.2 us (2%)
    all_to_all x6, waiting for transfers between devices, exchange(): return lax.all_to_all(array, 'seq', 0, 0, tiled=True)  285 us
    all_to_all x6, starting transfers between devices, exchange(): return lax.all_to_all(array, 'seq', 0, 0, tiled=True)  60.9 us
    unnamed x79, local copies, waits for them, and re-layouts  16.7 us
  transfers between devices with their start and end apart: 10, of which 8 were waited for; matrix products, arithmetic and copies ran while one was open for 23% of the time, Pallas kernels for 0%

profile of v3, /device:TPU:32, one launch (start us, length us, event | category | flops | bytes accessed | tf_op | source)
XLA Modules:
  0.0 522.5 jit_solution(7864724409353690820)
XLA Ops:
  18.5 15.0 %all-to-all-start = ((bf16[128,2,576]{2,1,0:T(2,128)(2,1)}), bf16[128,2,576]{2,1,0:T(2,128)(2,1)S(1)}, u32[]{:S(2)}, u32[]{:S(2)}) async-start(bf16[128,2,576]{2,1,0:T(2,128)(2,1)} %reshape.728), calls=%async_computation | async-start | bytes 655360 | tf_op jit(solution)/shard_map/all_to_all | solution.py:124
  33.8 3.4 collective-permute-start
  37.2 2.5 collective-permute-start.1
  43.5 3.2 collective-permute-done
  52.0 2.7 copy.319
  54.7 2.6 pad_maximum_fusion.1
  57.3 13.0 %all-to-all-start.1 = ((bf16[128,136,128]{2,1,0:T(8,128)(2,1)}), bf16[128,136,128]{2,1,0:T(8,128)(2,1)}, u32[]{:S(2)}, u32[]{:S(2)}) async-start(bf16[128,136,128]{2,1,0:T(8,128)(2,1)} %pad_maximum_fusion.1), calls=%async_computation.1 | async-start | bytes 8912896 | tf_op jit(solution)/shard_map/all_to_all | solution.py:124
  71.8 4.7 copy.323
  76.5 96.5 %all-to-all-done.1 = bf16[128,136,128]{2,1,0:T(8,128)(2,1)} async-done(((bf16[128,136,128]{2,1,0:T(8,128)(2,1)}), bf16[128,136,128]{2,1,0:T(8,128)(2,1)}, u32[]{:S(2)}, u32[]{:S(2)}) %all-to-all-start.1) | async-done | bytes 4456480 | tf_op jit(solution)/shard_map/all_to_all | solution.py:124
  173.0 8.3 %all-to-all-start.2 = ((bf16[128,128,128]{2,1,0:T(8,128)(2,1)}), bf16[128,128,128]{2,1,0:T(8,128)(2,1)}, u32[]{:S(2)}, u32[]{:S(2)}) async-start(bf16[128,128,128]{2,1,0:T(8,128)(2,1)} %bitcast.256), calls=%async_computation.2 | async-start | bytes 8388608 | tf_op jit(solution)/shard_map/all_to_all | solution.py:124
  181.6 1.5 reshape.659
  191.0 4.8 slice.220
  196.7 2.9 gather_fusion
  205.5 2.0 fusion.5
  207.5 3.4 bitcast_convert_fusion
  212.3 4.7 copy.350
  217.0 59.2 %all-to-all-done.2 = bf16[128,128,128]{2,1,0:T(8,128)(2,1)} async-done(((bf16[128,128,128]{2,1,0:T(8,128)(2,1)}), bf16[128,128,128]{2,1,0:T(8,128)(2,1)}, u32[]{:S(2)}, u32[]{:S(2)}) %all-to-all-start.2) | async-done | bytes 4194336 | tf_op jit(solution)/shard_map/all_to_all | solution.py:124
  276.1 8.1 %all-to-all-start.4 = ((bf16[128,128,128]{2,1,0:T(8,128)(2,1)}), bf16[128,128,128]{2,1,0:T(8,128)(2,1)}, u32[]{:S(2)}, u32[]{:S(2)}) async-start(bf16[128,128,128]{2,1,0:T(8,128)(2,1)} %bitcast.257), calls=%async_computation.4 | async-start | bytes 8388608 | tf_op jit(solution)/shard_map/all_to_all | solution.py:124
  284.3 4.9 fusion.20
  289.2 6.0 %fusion.18 = f32[4,4,320,128,1]{3,2,4,1,0:T(8,128)} fusion(bf16[4,64,4,4,128]{4,3,2,1,0:T(4,128)(2,1)S(1)} %copy-done.15, f32[4,4,320,64,4]{2,3,4,1,0:T(8,128)} %copy-done, f32[4,4,4,64]{3,2,1,0:T(4,128)S(1)} %add.213, f32[4,4,4,64]{3,2,1,0:T(4,128)S(1)} %max.8, pred[4,320]{1,0:T(4,128)(4,1)S(1)} %broadcast_in_dim.172), kind=kOutput, calls=%fused_computation.45 | convolution fusion | flops 342097920 | bytes 8946944 | tf_op jit(solution)/shard_map/rhgtk,rthgd->rkhd/dot_general | solution.py:276
  295.2 2.9 gather_fusion.1
  298.1 5.0 multiply_reduce_fusion
  303.2 5.0 fusion.2
  309.3 1.9 copy_dynamic-update-slice_fusion.1
  311.3 2.1 copy_dynamic-update-slice_fusion
  313.4 2.3 copy-done.4
  317.1 4.0 fusion.12
  323.8 2.7 copy.345
  326.6 2.5 pad_maximum_fusion
  329.1 47.5 %all-to-all-done.4 = bf16[128,128,128]{2,1,0:T(8,128)(2,1)} async-done(((bf16[128,128,128]{2,1,0:T(8,128)(2,1)}), bf16[128,128,128]{2,1,0:T(8,128)(2,1)}, u32[]{:S(2)}, u32[]{:S(2)}) %all-to-all-start.4) | async-done | bytes 4194336 | tf_op jit(solution)/shard_map/all_to_all | solution.py:124
  376.6 8.2 %all-to-all-start.3 = ((bf16[128,144,128]{2,1,0:T(8,128)(2,1)}), bf16[128,144,128]{2,1,0:T(8,128)(2,1)}, u32[]{:S(2)}, u32[]{:S(2)}) async-start(bf16[128,144,128]{2,1,0:T(8,128)(2,1)} %pad_maximum_fusion), calls=%async_computation.3 | async-start | bytes 9437184 | tf_op jit(solution)/shard_map/all_to_all | solution.py:124
  385.4 3.3 copy.332
  388.7 2.6 reshape.658
  391.3 2.4 fusion.85
  394.7 2.1 fusion.80
  396.8 2.2 copy.373
  398.9 1.6 copy.372
  403.5 2.1 slice_bitcast_fusion.2
  407.1 3.4 collective-permute-start.3
  410.5 2.5 collective-permute-start.2
  413.0 4.6 fusion.26
  417.6 70.7 %all-to-all-done.3 = bf16[128,144,128]{2,1,0:T(8,128)(2,1)} async-done(((bf16[128,144,128]{2,1,0:T(8,128)(2,1)}), bf16[128,144,128]{2,1,0:T(8,128)(2,1)}, u32[]{:S(2)}, u32[]{:S(2)}) %all-to-all-start.3) | async-done | bytes 4718624 | tf_op jit(solution)/shard_map/all_to_all | solution.py:124
  491.4 1.7 broadcast_select_fusion
  493.1 8.2 %all-to-all-start.5 = ((f32[128,2,512]{2,1,0:T(2,128)}), f32[128,2,512]{2,1,0:T(2,128)}, u32[]{:S(2)}, u32[]{:S(2)}) async-start(f32[128,2,512]{2,1,0:T(2,128)} %broadcast_select_fusion), calls=%async_computation.5 | async-start | bytes 1048576 | tf_op jit(solution)/shard_map/all_to_all | solution.py:124
  501.6 2.5 slice.272
  504.1 2.4 fusion.23
  507.0 9.8 %all-to-all-done.5 = f32[128,2,512]{2,1,0:T(2,128)} async-done(((f32[128,2,512]{2,1,0:T(2,128)}), f32[128,2,512]{2,1,0:T(2,128)}, u32[]{:S(2)}, u32[]{:S(2)}) %all-to-all-start.5) | async-done | bytes 524320 | tf_op jit(solution)/shard_map/all_to_all | solution.py:124
  516.7 1.6 reshape.723
  (195 shorter events, 54.6 us)
Async XLA Ops:
  7.3 0.5 copy-start.26
  12.7 20.9 %copy-start.11 = (bf16[256,512]{1,0:T(8,128)(2,1)S(1)}, bf16[256,512]{1,0:T(8,128)(2,1)}, u32[]{:S(2)}) copy-start(bf16[256,512]{1,0:T(8,128)(2,1)} %param.13) | copy-start | bytes 786436
  18.5 31.3 %all-to-all-start = ((bf16[128,2,576]{2,1,0:T(2,128)(2,1)}), bf16[128,2,576]{2,1,0:T(2,128)(2,1)S(1)}, u32[]{:S(2)}, u32[]{:S(2)}) async-start(bf16[128,2,576]{2,1,0:T(2,128)(2,1)} %reshape.728), calls=%async_computation | async-start | bytes 655360 | tf_op jit(solution)/shard_map/all_to_all | solution.py:124
  33.8 12.9 %collective-permute-start = (bf16[2,64,512]{1,2,0:T(8,128)(2,1)S(1)}, bf16[2,64,512]{1,2,0:T(8,128)(2,1)S(1)}, u32[]{:S(2)}, u32[]{:S(2)}) collective-permute-start(bf16[2,64,512]{1,2,0:T(8,128)(2,1)S(1)} %get-tuple-element.92), channel_id=1, source_target_pairs={{0,2},{2,4},{4,6},{6,8},{8,10},{10,12},{12,14},{14,16},{16,18},{18... | collective-permute-start | bytes 393224 | tf_op jit(solution)/shard_map/ppermute | solution.py:26
  37.2 10.1 %collective-permute-start.1 = (bf16[2,64,512]{1,2,0:T(8,128)(2,1)S(1)}, bf16[2,64,512]{1,2,0:T(8,128)(2,1)S(1)}, u32[]{:S(2)}, u32[]{:S(2)}) collective-permute-start(bf16[2,64,512]{1,2,0:T(8,128)(2,1)S(1)} %get-tuple-element.93), channel_id=1, source_target_pairs={{2,0},{4,2},{6,4},{8,6},{10,8},{12,10},{14,12},{16,14},{18,16},{20... | collective-permute-start | bytes 393224 | tf_op jit(solution)/shard_map/ppermute | solution.py:27
  50.6 19.9 %copy-start.21 = (s32[256]{0:T(256)}, s32[256]{0:T(256)S(1)}, u32[]{:S(2)}) copy-start(s32[256]{0:T(256)S(1)} %reshape.673) | copy-start | bytes 3076
  57.3 115.7 %all-to-all-start.1 = ((bf16[128,136,128]{2,1,0:T(8,128)(2,1)}), bf16[128,136,128]{2,1,0:T(8,128)(2,1)}, u32[]{:S(2)}, u32[]{:S(2)}) async-start(bf16[128,136,128]{2,1,0:T(8,128)(2,1)} %pad_maximum_fusion.1), calls=%async_computation.1 | async-start | bytes 8912896 | tf_op jit(solution)/shard_map/all_to_all | solution.py:124
  173.0 8.6 %copy-start.12 = (bf16[256,2048]{1,0:T(8,128)(2,1)S(1)}, bf16[256,2048]{1,0:T(8,128)(2,1)}, u32[]{:S(2)}) copy-start(bf16[256,2048]{1,0:T(8,128)(2,1)} %param.17) | copy-start | bytes 3145732
  173.0 10.2 %copy-start.13 = (bf16[256,2048]{1,0:T(8,128)(2,1)S(1)}, bf16[256,2048]{1,0:T(8,128)(2,1)}, u32[]{:S(2)}) copy-start(bf16[256,2048]{1,0:T(8,128)(2,1)} %param.11) | copy-start | bytes 3145732
  173.0 103.1 %all-to-all-start.2 = ((bf16[128,128,128]{2,1,0:T(8,128)(2,1)}), bf16[128,128,128]{2,1,0:T(8,128)(2,1)}, u32[]{:S(2)}, u32[]{:S(2)}) async-start(bf16[128,128,128]{2,1,0:T(8,128)(2,1)} %bitcast.256), calls=%async_computation.2 | async-start | bytes 8388608 | tf_op jit(solution)/shard_map/all_to_all | solution.py:124
  199.6 2.3 copy-start.8
  201.9 2.0 copy-start.5
  202.8 4.7 copy-start.1
  203.9 3.5 copy-start
  203.9 99.2 %copy-start.19 = (f32[4,4,4,64]{3,2,1,0:T(4,128)}, f32[4,4,4,64]{3,2,1,0:T(4,128)S(1)}, u32[]{:S(2)}) copy-start(f32[4,4,4,64]{3,2,1,0:T(4,128)S(1)} %max.8) | copy-start | bytes 49156
  205.4 2.0 copy-start.14
  207.5 95.7 %copy-start.20 = (f32[4,4,4,64]{3,2,1,0:T(4,128)}, f32[4,4,4,64]{3,2,1,0:T(4,128)S(1)}, u32[]{:S(2)}) copy-start(f32[4,4,4,64]{3,2,1,0:T(4,128)S(1)} %add.213) | copy-start | bytes 49156
  276.1 100.4 %all-to-all-start.4 = ((bf16[128,128,128]{2,1,0:T(8,128)(2,1)}), bf16[128,128,128]{2,1,0:T(8,128)(2,1)}, u32[]{:S(2)}, u32[]{:S(2)}) async-start(bf16[128,128,128]{2,1,0:T(8,128)(2,1)} %bitcast.257), calls=%async_computation.4 | async-start | bytes 8388608 | tf_op jit(solution)/shard_map/all_to_all | solution.py:124
  284.3 4.9 copy-start.15
  298.1 5.1 copy-start.17
  298.1 5.1 copy-start.16
  303.1 5.0 copy-start.30
  308.2 3.0 copy-start.2
  309.3 2.0 copy-start.10
  313.4 2.3 copy-start.4
  315.7 1.4 copy-start.18
  321.1 1.3 copy-start.6
  329.1 56.3 %copy-start.27 = (s32[2]{0:T(128)S(1)}, s32[2]{0:T(128)}, u32[]{:S(2)}) copy-start(s32[2]{0:T(128)} %copy-done.26) | copy-start | bytes 28
  376.6 111.7 %all-to-all-start.3 = ((bf16[128,144,128]{2,1,0:T(8,128)(2,1)}), bf16[128,144,128]{2,1,0:T(8,128)(2,1)}, u32[]{:S(2)}, u32[]{:S(2)}) async-start(bf16[128,144,128]{2,1,0:T(8,128)(2,1)} %pad_maximum_fusion), calls=%async_computation.3 | async-start | bytes 9437184 | tf_op jit(solution)/shard_map/all_to_all | solution.py:124
  384.8 6.5 %copy-start.3 = (bf16[4,4,4,64,320]{4,3,2,1,0:T(8,128)(2,1)S(1)}, bf16[4,4,4,64,320]{4,3,2,1,0:T(8,128)(2,1)}, u32[]{:S(2)}) copy-start(bf16[4,4,4,64,320]{4,3,2,1,0:T(8,128)(2,1)} %copy-done.2) | copy-start | bytes 7864324
  391.3 2.4 copy-start.7
  391.3 2.4 copy-start.9
  405.7 7.3 %copy-start.22 = (s32[256]{0:T(256)S(1)}, s32[256]{0:T(256)}, u32[]{:S(2)}) copy-start(s32[256]{0:T(256)} %copy-done.21) | copy-start | bytes 3076
  405.7 7.3 %copy-start.24 = (s32[4,4]{1,0:T(4,128)S(1)}, s32[4,4]{1,0:T(4,128)}, u32[]{:S(2)}) copy-start(s32[4,4]{1,0:T(4,128)} %multiply_add_fusion.1) | copy-start | bytes 196
  407.1 94.4 %collective-permute-start.3 = (bf16[2,64,4,128]{3,2,1,0:T(4,128)(2,1)}, bf16[2,64,4,128]{3,2,1,0:T(4,128)(2,1)S(1)}, u32[]{:S(2)}, u32[]{:S(2)}) collective-permute-start(bf16[2,64,4,128]{3,2,1,0:T(4,128)(2,1)} %get-tuple-element.79), channel_id=1, source_target_pairs={{0,2},{2,4},{4,6},{6,8},{8,10},{10,12},{12,14},{14,16},{16,18},{18... | collective-permute-start | bytes 393224 | tf_op jit(solution)/shard_map/ppermute | solution.py:40
  410.5 90.8 %collective-permute-start.2 = (bf16[2,64,4,128]{3,2,1,0:T(4,128)(2,1)}, bf16[2,64,4,128]{3,2,1,0:T(4,128)(2,1)S(1)}, u32[]{:S(2)}, u32[]{:S(2)}) collective-permute-start(bf16[2,64,4,128]{3,2,1,0:T(4,128)(2,1)} %get-tuple-element.80), channel_id=1, source_target_pairs={{2,0},{4,2},{6,4},{8,6},{10,8},{12,10},{14,12},{16,14},{18,16},{20... | collective-permute-start | bytes 393224 | tf_op jit(solution)/shard_map/ppermute | solution.py:40
  493.1 23.7 %all-to-all-start.5 = ((f32[128,2,512]{2,1,0:T(2,128)}), f32[128,2,512]{2,1,0:T(2,128)}, u32[]{:S(2)}, u32[]{:S(2)}) async-start(f32[128,2,512]{2,1,0:T(2,128)} %broadcast_select_fusion), calls=%async_computation.5 | async-start | bytes 1048576 | tf_op jit(solution)/shard_map/all_to_all | solution.py:124
  501.6 2.5 copy-start.23
  501.6 2.5 copy-start.25
  506.5 11.8 %copy-start.28 = (pred[2]{0:T(512)(128)(4,1)S(1)}, pred[2]{0:T(512)(128)(4,1)}, u32[]{:S(2)}) copy-start(pred[2]{0:T(512)(128)(4,1)} %get-tuple-element.60) | copy-start | bytes 10
  506.5 12.1 %copy-start.29 = (s32[2]{0:T(128)S(1)}, s32[2]{0:T(128)}, u32[]{:S(2)}) copy-start(s32[2]{0:T(128)} %get-tuple-element.62) | copy-start | bytes 28

commit v4 on v3

--- a/solution.py
+++ b/solution.py
@@ -168,8 +168,18 @@
     glob_owner = global_blocks // block_rows
     glob_local = global_blocks % block_rows
     glob_scatter = []
+    glob_cos, glob_sin = [], []
     for which_glob in range(GLOB):
-        glob_piece = lax.dynamic_index_in_dim(own_blocks, glob_local[which_glob], 1, keepdims=False)
+        start = glob_local[which_glob] * BLK
+        block_cos, block_sin = tables(lax.dynamic_slice_in_dim(positions, start, BLK, 1))
+        glob_cos.append(block_cos)
+        glob_sin.append(block_sin)
+        block_keys = lax.dynamic_slice_in_dim(key_states, start, BLK, 0)
+        block_keys = rotate(
+            block_keys.reshape(BLK, kv_dev, HD).astype(jnp.float32), block_cos, block_sin
+        ).astype(jnp.bfloat16)
+        block_values = lax.dynamic_slice_in_dim(value_states, start, BLK, 0).reshape(BLK, kv_dev, HD)
+        glob_piece = jnp.stack([block_keys, block_values])
         glob_piece = jnp.where(my_index == glob_owner[which_glob], glob_piece, jnp.zeros_like(glob_piece))
         glob_scatter.append(glob_piece.reshape(seq_count, piece))
     first_out = jnp.concatenate(
@@ -280,7 +290,17 @@
     glob_split = glob_split.transpose(1, 0, 2).reshape(seq_count, glob_rows, HD)
     glob_high = glob_split.astype(jnp.bfloat16)
     glob_low = (glob_split - glob_high.astype(jnp.float32)).astype(jnp.bfloat16)
-    returned_k = exchange(jnp.concatenate([out_k, glob_high, glob_low], axis=1))
+    query_portion = jnp.einsum(
+        "rhgtk,rkhd->rthgd", near_sgrad, near_k, preferred_element_type=jnp.float32
+    ) + jnp.einsum("rhgtk,rhkd->rthgd", far_sgrad, far_k, preferred_element_type=jnp.float32)
+    query_grad = (
+        unrotate(query_portion.reshape(tok_rows, kv_dev * GROUP, HD), cosines, sine_vals)
+        .astype(jnp.bfloat16)
+        .reshape(tok_rows, kv_dev * GROUP * HD)
+    )
+    payload_k = jnp.concatenate([out_k, glob_high, glob_low], axis=1)
+    payload_k, query_grad = lax.optimization_barrier((payload_k, query_grad))
+    returned_k = exchange(payload_k)
     glob_back = returned_k[:, capacity * BLK :].astype(jnp.float32)
     piece_sum = jnp.sum(glob_back[:, :glob_rows] + glob_back[:, glob_rows:], axis=0).reshape(GLOB, piece)
     returned_k = returned_k[:, : capacity * BLK].reshape(seq_count * capacity, BLK, HD)
@@ -289,9 +309,6 @@
     )
     glob_grad = exchange(to_owner).transpose(1, 0, 2).reshape(GLOB, 2, BLK, kv_dev, HD)
 
-    query_portion = jnp.einsum(
-        "rhgtk,rkhd->rthgd", near_sgrad, near_k, preferred_element_type=jnp.float32
-    ) + jnp.einsum("rhgtk,rhkd->rthgd", far_sgrad, far_k, preferred_element_type=jnp.float32)
     window_acc = jnp.pad(near_grad[:, :, 0], ((0, 0), (0, 2), (0, 0), (0, 0), (0, 0)))
     window_acc = window_acc + jnp.pad(near_grad[:, :, 1], ((0, 0), (1, 1), (0, 0), (0, 0), (0, 0)))
     window_acc = window_acc + jnp.pad(near_grad[:, :, 2], ((0, 0), (2, 0), (0, 0), (0, 0), (0, 0)))
@@ -300,8 +317,6 @@
 
     kv_grad = window_acc[:, 1 : block_rows + 1]
     kv_grad = kv_grad.at[:, block_rows - 1].add(from_right).at[:, 0].add(from_left)
-    glob_mine = jnp.where((glob_owner == my_index)[:, None, None, None, None], glob_grad, 0.0)
-    kv_grad = kv_grad.at[:, glob_local].add(glob_mine.transpose(1, 0, 2, 3, 4))
     oh_back = onehot(asked_flat, table_rows).T
     collected = jnp.stack(
         [
@@ -310,18 +325,18 @@
         ]
     ).reshape(2, block_rows, kv_dev, BLK, HD)
     kv_grad = kv_grad + collected.transpose(0, 1, 3, 2, 4)
+    key_rest = unrotate(kv_grad[0].reshape(tok_rows, kv_dev, HD), cosines, sine_vals)
+    key_rest = key_rest.reshape(block_rows, BLK, kv_dev, HD)
+    value_rest = kv_grad[1]
+    glob_mine = jnp.where((glob_owner == my_index)[:, None, None, None, None], glob_grad, 0.0)
+    for which_glob in range(GLOB):
+        glob_keys = unrotate(glob_mine[which_glob, 0], glob_cos[which_glob], glob_sin[which_glob])
+        key_rest = key_rest.at[glob_local[which_glob]].add(glob_keys)
+        value_rest = value_rest.at[glob_local[which_glob]].add(glob_mine[which_glob, 1])
 
     attended = attended.reshape(tok_rows, kv_dev * GROUP * HD)
-    query_grad = (
-        unrotate(query_portion.reshape(tok_rows, kv_dev * GROUP, HD), cosines, sine_vals)
-        .astype(jnp.bfloat16)
-        .reshape(tok_rows, kv_dev * GROUP * HD)
-    )
-    key_acc = kv_grad[0].reshape(tok_rows, kv_dev, HD)
-    key_grad = (
-        unrotate(key_acc, cosines, sine_vals).astype(jnp.bfloat16).reshape(tok_rows, kv_dev * HD)
-    )
-    value_grad = kv_grad[1].reshape(tok_rows, kv_dev * HD).astype(jnp.bfloat16)
+    key_grad = key_rest.astype(jnp.bfloat16).reshape(tok_rows, kv_dev * HD)
+    value_grad = value_rest.reshape(tok_rows, kv_dev * HD).astype(jnp.bfloat16)
     return (attended, query_grad, key_grad, value_grad)
 
 

time: 532 us -> 532 us (level)
  waiting for transfers between devices: 289 us -> 274 us
  other arithmetic: 24.6 us -> 31.7 us
  local copies, waits for them, and re-layouts: 78.1 us -> 84.3 us
    all_to_all x6, waiting for transfers between devices: 285 us -> 198 us  [exchange(): return lax.all_to_all(array, 'seq', 0, 0, tiled=True)]
    ppermute x2, waiting for transfers between devices: 0.01 us -> 72.7 us  [shifted(): return lax.ppermute(array, axis, pairs)]
    unnamed x79 -> x65, local copies, waits for them, and re-layouts: 16.7 us -> 20.9 us
  transfers between devices with their start and end apart: 10 -> 10, of which waited for: 8 -> 9; matrix products, arithmetic and copies ran while one was open for 23% -> 24% of each run, Pallas kernels for 0% -> 0%
where the time goes in v4:
time: 532 us; the launch traced here: 522 us
  waiting for transfers between devices  274 us (52%)
  local copies, waits for them, and re-layouts  84.3 us (16%)
  starting transfers between devices  73.1 us (14%)
  matrix products  46.6 us (9%)
  other arithmetic  31.7 us (6%)
  between operations  12.5 us (2%)
    all_to_all x6, waiting for transfers between devices, exchange(): return lax.all_to_all(array, 'seq', 0, 0, tiled=True)  198 us
    ppermute x2, waiting for transfers between devices, shifted(): return lax.ppermute(array, axis, pairs)  72.7 us
    all_to_all x6, starting transfers between devices, exchange(): return lax.all_to_all(array, 'seq', 0, 0, tiled=True)  61.4 us
    unnamed x65, local copies, waits for them, and re-layouts  20.9 us
  transfers between devices with their start and end apart: 10, of which 9 were waited for; matrix products, arithmetic and copies ran while one was open for 24% of the time, Pallas kernels for 0%

profile of v4, /device:TPU:32, one launch (start us, length us, event | category | flops | bytes accessed | tf_op | source)
XLA Modules:
  0.0 521.8 jit_solution(931592102496020281)
XLA Ops:
  13.6 15.0 %all-to-all-start = ((bf16[128,2,576]{2,1,0:T(2,128)(2,1)}), bf16[128,2,576]{2,1,0:T(2,128)(2,1)S(1)}, u32[]{:S(2)}, u32[]{:S(2)}) async-start(bf16[128,2,576]{2,1,0:T(2,128)(2,1)} %reshape.1258), calls=%async_computation | async-start | bytes 655360 | tf_op jit(solution)/shard_map/all_to_all | solution.py:124
  29.6 3.4 collective-permute-start
  32.9 2.5 collective-permute-start.1
  39.6 2.2 collective-permute-done
  46.7 2.7 copy.232
  49.5 2.6 pad_maximum_fusion.1
  52.1 14.2 %all-to-all-start.1 = ((bf16[128,136,128]{2,1,0:T(8,128)(2,1)}), bf16[128,136,128]{2,1,0:T(8,128)(2,1)}, u32[]{:S(2)}, u32[]{:S(2)}) async-start(bf16[128,136,128]{2,1,0:T(8,128)(2,1)} %pad_maximum_fusion.1), calls=%async_computation.1 | async-start | bytes 8912896 | tf_op jit(solution)/shard_map/all_to_all | solution.py:124
  67.7 4.7 copy.236
  72.4 96.3 %all-to-all-done.1 = bf16[128,136,128]{2,1,0:T(8,128)(2,1)} async-done(((bf16[128,136,128]{2,1,0:T(8,128)(2,1)}), bf16[128,136,128]{2,1,0:T(8,128)(2,1)}, u32[]{:S(2)}, u32[]{:S(2)}) %all-to-all-start.1) | async-done | bytes 4456480 | tf_op jit(solution)/shard_map/all_to_all | solution.py:124
  168.7 8.3 %all-to-all-start.2 = ((bf16[128,128,128]{2,1,0:T(8,128)(2,1)}), bf16[128,128,128]{2,1,0:T(8,128)(2,1)}, u32[]{:S(2)}, u32[]{:S(2)}) async-start(bf16[128,128,128]{2,1,0:T(8,128)(2,1)} %bitcast.304), calls=%async_computation.2 | async-start | bytes 8388608 | tf_op jit(solution)/shard_map/all_to_all | solution.py:124
  189.0 4.7 slice.383
  194.0 2.9 gather_fusion
  203.8 2.0 fusion.5
  205.8 3.3 bitcast_convert_fusion
  210.6 4.7 copy.263
  215.3 56.3 %all-to-all-done.2 = bf16[128,128,128]{2,1,0:T(8,128)(2,1)} async-done(((bf16[128,128,128]{2,1,0:T(8,128)(2,1)}), bf16[128,128,128]{2,1,0:T(8,128)(2,1)}, u32[]{:S(2)}, u32[]{:S(2)}) %all-to-all-start.2) | async-done | bytes 4194336 | tf_op jit(solution)/shard_map/all_to_all | solution.py:124
  271.6 7.8 %all-to-all-start.4 = ((bf16[128,128,128]{2,1,0:T(8,128)(2,1)}), bf16[128,128,128]{2,1,0:T(8,128)(2,1)}, u32[]{:S(2)}, u32[]{:S(2)}) async-start(bf16[128,128,128]{2,1,0:T(8,128)(2,1)} %bitcast.305), calls=%async_computation.4 | async-start | bytes 8388608 | tf_op jit(solution)/shard_map/all_to_all | solution.py:124
  279.4 5.3 %fusion.20 = f32[4,4,128,4,64]{2,4,3,1,0:T(8,128)} fusion(bf16[4,320,4,128,1]{3,1,4,2,0:T(8,128)(2,1)} %bitcast.328, f32[4,4,320,64,4]{2,3,4,1,0:T(8,128)} %copy-done, f32[4,4,4,64]{3,2,1,0:T(4,128)S(1)} %add.282, f32[4,4,4,64]{3,2,1,0:T(4,128)S(1)} %max.8, pred[4,320]{1,0:T(4,128)(4,1)S(1)} %broadcast_in_dim.278), kind=kOutput, calls=%fused_computation.46 | convolution fusion | flops 342097920 | bytes 8684800 | tf_op jit(solution)/shard_map/rhgtk,rkhd->rthgd/dot_general | solution.py:270
  284.7 6.0 %fusion.18 = f32[4,4,320,128,1]{3,2,4,1,0:T(8,128)} fusion(bf16[4,64,4,4,128]{4,3,2,1,0:T(4,128)(2,1)S(1)} %copy-done.17, f32[4,4,320,64,4]{2,3,4,1,0:T(8,128)} %copy-done, f32[4,4,4,64]{3,2,1,0:T(4,128)S(1)} %add.282, f32[4,4,4,64]{3,2,1,0:T(4,128)S(1)} %max.8, pred[4,320]{1,0:T(4,128)(4,1)S(1)} %broadcast_in_dim.278), kind=kOutput, calls=%fused_computation.44 | convolution fusion | flops 342097920 | bytes 8946944 | tf_op jit(solution)/shard_map/rhgtk,rthgd->rkhd/dot_general | solution.py:286
  290.7 2.9 gather_fusion.1
  293.7 5.0 multiply_reduce_fusion
  298.7 5.0 fusion.2
  304.7 2.3 copy-done.2
  307.3 2.3 fusion.12
  310.6 2.8 fusion.90
  313.3 3.1 copy.282
  316.5 3.2 copy.281
  319.7 2.9 fusion.96
  324.6 2.1 copy_dynamic-update-slice_fusion
  326.7 2.4 copy-done.4
  330.2 2.0 reshape.1192
  332.2 2.3 copy.254
  334.5 2.2 reshape.1193
  339.0 2.9 copy.249
  343.4 2.4 pad_maximum_fusion
  345.8 25.9 %all-to-all-done.4 = bf16[128,128,128]{2,1,0:T(8,128)(2,1)} async-done(((bf16[128,128,128]{2,1,0:T(8,128)(2,1)}), bf16[128,128,128]{2,1,0:T(8,128)(2,1)}, u32[]{:S(2)}, u32[]{:S(2)}) %all-to-all-start.4) | async-done | bytes 4194336 | tf_op jit(solution)/shard_map/all_to_all | solution.py:124
  371.7 7.7 %all-to-all-start.3 = ((bf16[128,144,128]{2,1,0:T(8,128)(2,1)}), bf16[128,144,128]{2,1,0:T(8,128)(2,1)}, u32[]{:S(2)}, u32[]{:S(2)}) async-start(bf16[128,144,128]{2,1,0:T(8,128)(2,1)} %pad_maximum_fusion), calls=%async_computation.3 | async-start | bytes 9437184 | tf_op jit(solution)/shard_map/all_to_all | solution.py:124
  384.1 2.2 slice_bitcast_fusion.2
  387.6 3.0 collective-permute-start.2
  390.6 4.6 fusion.26
  397.6 2.9 collective-permute-start.3
  400.5 2.5 copy.269
  403.1 72.7 %collective-permute-done.2 = bf16[2,64,4,128]{3,2,1,0:T(4,128)(2,1)} collective-permute-done((bf16[2,64,4,128]{3,2,1,0:T(4,128)(2,1)}, bf16[2,64,4,128]{3,2,1,0:T(4,128)(2,1)}, u32[]{:S(2)}, u32[]{:S(2)}) %collective-permute-start.2) | collective-permute-done | bytes 131104 | tf_op jit(solution)/shard_map/ppermute | solution.py:40
  477.8 5.3 %all-to-all-done.3 = bf16[128,144,128]{2,1,0:T(8,128)(2,1)} async-done(((bf16[128,144,128]{2,1,0:T(8,128)(2,1)}), bf16[128,144,128]{2,1,0:T(8,128)(2,1)}, u32[]{:S(2)}, u32[]{:S(2)}) %all-to-all-start.3) | async-done | bytes 4718624 | tf_op jit(solution)/shard_map/all_to_all | solution.py:124
  484.4 2.5 slice.447
  486.9 2.4 fusion.23
  490.3 8.4 %all-to-all-start.5 = ((f32[128,2,512]{2,1,0:T(2,128)}), f32[128,2,512]{2,1,0:T(2,128)S(1)}, u32[]{:S(2)}, u32[]{:S(2)}) async-start(f32[128,2,512]{2,1,0:T(2,128)} %broadcast_select_fusion), calls=%async_computation.5 | async-start | bytes 1048576 | tf_op jit(solution)/shard_map/all_to_all | solution.py:124
  501.2 13.4 %all-to-all-done.5 = f32[128,2,512]{2,1,0:T(2,128)S(1)} async-done(((f32[128,2,512]{2,1,0:T(2,128)}), f32[128,2,512]{2,1,0:T(2,128)S(1)}, u32[]{:S(2)}, u32[]{:S(2)}) %all-to-all-start.5) | async-done | bytes 524320 | tf_op jit(solution)/shard_map/all_to_all | solution.py:124
  (193 shorter events, 65.2 us)
Async XLA Ops:
  0.6 28.0 %copy-start.22 = (s32[3,256]{1,0:T(4,128)S(1)}, s32[3,256]{1,0:T(4,128)}, u32[]{:S(2)}) copy-start(s32[3,256]{1,0:T(4,128)} %param.22) | copy-start | bytes 9220
  0.6 28.0 %copy-start.21 = (bf16[256,512]{1,0:T(8,128)(2,1)S(1)}, bf16[256,512]{1,0:T(8,128)(2,1)}, u32[]{:S(2)}) copy-start(bf16[256,512]{1,0:T(8,128)(2,1)} %param.20) | copy-start | bytes 786436
  8.9 20.4 %copy-start.11 = (bf16[256,512]{1,0:T(8,128)(2,1)S(1)}, bf16[256,512]{1,0:T(8,128)(2,1)}, u32[]{:S(2)}) copy-start(bf16[256,512]{1,0:T(8,128)(2,1)} %param.21) | copy-start | bytes 786436
  13.6 31.0 %all-to-all-start = ((bf16[128,2,576]{2,1,0:T(2,128)(2,1)}), bf16[128,2,576]{2,1,0:T(2,128)(2,1)S(1)}, u32[]{:S(2)}, u32[]{:S(2)}) async-start(bf16[128,2,576]{2,1,0:T(2,128)(2,1)} %reshape.1258), calls=%async_computation | async-start | bytes 655360 | tf_op jit(solution)/shard_map/all_to_all | solution.py:124
  29.6 12.2 %collective-permute-start = (bf16[2,64,512]{1,2,0:T(8,128)(2,1)S(1)}, bf16[2,64,512]{1,2,0:T(8,128)(2,1)S(1)}, u32[]{:S(2)}, u32[]{:S(2)}) collective-permute-start(bf16[2,64,512]{1,2,0:T(8,128)(2,1)S(1)} %get-tuple-element.145), channel_id=1, source_target_pairs={{0,2},{2,4},{4,6},{6,8},{8,10},{10,12},{12,14},{14,16},{16,18},{18... | collective-permute-start | bytes 393224 | tf_op jit(solution)/shard_map/ppermute | solution.py:26
  32.9 9.9 %collective-permute-start.1 = (bf16[2,64,512]{1,2,0:T(8,128)(2,1)S(1)}, bf16[2,64,512]{1,2,0:T(8,128)(2,1)S(1)}, u32[]{:S(2)}, u32[]{:S(2)}) collective-permute-start(bf16[2,64,512]{1,2,0:T(8,128)(2,1)S(1)} %get-tuple-element.146), channel_id=1, source_target_pairs={{2,0},{4,2},{6,4},{8,6},{10,8},{12,10},{14,12},{16,14},{18,16},{20... | collective-permute-start | bytes 393224 | tf_op jit(solution)/shard_map/ppermute | solution.py:27
  52.1 116.6 %all-to-all-start.1 = ((bf16[128,136,128]{2,1,0:T(8,128)(2,1)}), bf16[128,136,128]{2,1,0:T(8,128)(2,1)}, u32[]{:S(2)}, u32[]{:S(2)}) async-start(bf16[128,136,128]{2,1,0:T(8,128)(2,1)} %pad_maximum_fusion.1), calls=%async_computation.1 | async-start | bytes 8912896 | tf_op jit(solution)/shard_map/all_to_all | solution.py:124
  168.6 8.6 %copy-start.13 = (bf16[256,2048]{1,0:T(8,128)(2,1)S(1)}, bf16[256,2048]{1,0:T(8,128)(2,1)}, u32[]{:S(2)}) copy-start(bf16[256,2048]{1,0:T(8,128)(2,1)} %param.25) | copy-start | bytes 3145732
  168.7 10.1 %copy-start.14 = (bf16[256,2048]{1,0:T(8,128)(2,1)S(1)}, bf16[256,2048]{1,0:T(8,128)(2,1)}, u32[]{:S(2)}) copy-start(bf16[256,2048]{1,0:T(8,128)(2,1)} %param.19) | copy-start | bytes 3145732
  168.7 102.9 %all-to-all-start.2 = ((bf16[128,128,128]{2,1,0:T(8,128)(2,1)}), bf16[128,128,128]{2,1,0:T(8,128)(2,1)}, u32[]{:S(2)}, u32[]{:S(2)}) async-start(bf16[128,128,128]{2,1,0:T(8,128)(2,1)} %bitcast.304), calls=%async_computation.2 | async-start | bytes 8388608 | tf_op jit(solution)/shard_map/all_to_all | solution.py:124
  196.9 3.4 copy-start.5
  201.2 4.7 copy-start.1
  202.3 3.5 copy-start
  203.8 2.0 copy-start.16
  271.6 100.1 %all-to-all-start.4 = ((bf16[128,128,128]{2,1,0:T(8,128)(2,1)}), bf16[128,128,128]{2,1,0:T(8,128)(2,1)}, u32[]{:S(2)}, u32[]{:S(2)}) async-start(bf16[128,128,128]{2,1,0:T(8,128)(2,1)} %bitcast.305), calls=%async_computation.4 | async-start | bytes 8388608 | tf_op jit(solution)/shard_map/all_to_all | solution.py:124
  279.4 5.3 %copy-start.17 = (bf16[4,64,4,4,128]{4,3,2,1,0:T(4,128)(2,1)S(1)}, bf16[4,64,4,4,128]{4,3,2,1,0:T(4,128)(2,1)}, u32[]{:S(2)}) copy-start(bf16[4,64,4,4,128]{4,3,2,1,0:T(4,128)(2,1)} %reshape.1189) | copy-start | bytes 3145732
  293.6 5.1 copy-start.19
  293.6 5.1 copy-start.12
  293.6 5.1 copy-start.18
  303.7 5.8 %copy-start.3 = (bf16[4,4,4,64,320]{4,3,2,1,0:T(8,128)(2,1)}, bf16[4,4,4,64,320]{4,3,2,1,0:T(8,128)(2,1)S(1)}, u32[]{:S(2)}) copy-start(bf16[4,4,4,64,320]{4,3,2,1,0:T(8,128)(2,1)S(1)} %fusion.2) | copy-start | bytes 7864324
  303.7 3.3 copy-start.2
  303.7 3.5 copy-start.20
  307.3 2.3 copy-start.6
  322.6 2.0 copy-start.9
  326.7 2.4 copy-start.4
  339.0 2.9 copy-start.7
  339.0 2.9 copy-start.8
  341.9 1.4 copy-start.10
  345.8 37.6 %copy-start.23 = (s32[4]{0:T(128)S(1)}, s32[4]{0:T(128)}, u32[]{:S(2)}) copy-start(s32[4]{0:T(128)} %constant.259.clone.1) | copy-start | bytes 52
  371.7 111.4 %all-to-all-start.3 = ((bf16[128,144,128]{2,1,0:T(8,128)(2,1)}), bf16[128,144,128]{2,1,0:T(8,128)(2,1)}, u32[]{:S(2)}, u32[]{:S(2)}) async-start(bf16[128,144,128]{2,1,0:T(8,128)(2,1)} %pad_maximum_fusion), calls=%async_computation.3 | async-start | bytes 9437184 | tf_op jit(solution)/shard_map/all_to_all | solution.py:124
  386.3 8.9 %copy-start.15 = (bf16[4,64,4,4,128]{4,1,3,2,0:T(8,128)(2,1)S(1)}, bf16[4,64,4,4,128]{4,1,3,2,0:T(8,128)(2,1)}, u32[]{:S(2)}) copy-start(bf16[4,64,4,4,128]{4,1,3,2,0:T(8,128)(2,1)} %get-tuple-element.189) | copy-start | bytes 3145732
  387.6 88.1 %collective-permute-start.2 = (bf16[2,64,4,128]{3,2,1,0:T(4,128)(2,1)}, bf16[2,64,4,128]{3,2,1,0:T(4,128)(2,1)}, u32[]{:S(2)}, u32[]{:S(2)}) collective-permute-start(bf16[2,64,4,128]{3,2,1,0:T(4,128)(2,1)} %get-tuple-element.131), channel_id=1, source_target_pairs={{2,0},{4,2},{6,4},{8,6},{10,8},{12,10},{14,12},{16,14},{18,16},{20... | collective-permute-start | bytes 393224 | tf_op jit(solution)/shard_map/ppermute | solution.py:40
  397.6 79.2 %collective-permute-start.3 = (bf16[2,64,4,128]{3,2,1,0:T(4,128)(2,1)}, bf16[2,64,4,128]{3,2,1,0:T(4,128)(2,1)}, u32[]{:S(2)}, u32[]{:S(2)}) collective-permute-start(bf16[2,64,4,128]{3,2,1,0:T(4,128)(2,1)} %get-tuple-element.130), channel_id=1, source_target_pairs={{0,2},{2,4},{4,6},{6,8},{8,10},{10,12},{12,14},{14,16},{16,18},{18... | collective-permute-start | bytes 393224 | tf_op jit(solution)/shard_map/ppermute | solution.py:40
  490.3 24.4 %all-to-all-start.5 = ((f32[128,2,512]{2,1,0:T(2,128)}), f32[128,2,512]{2,1,0:T(2,128)S(1)}, u32[]{:S(2)}, u32[]{:S(2)}) async-start(f32[128,2,512]{2,1,0:T(2,128)} %broadcast_select_fusion), calls=%async_computation.5 | async-start | bytes 1048576 | tf_op jit(solution)/shard_map/all_to_all | solution.py:124

commit v5 on v4

--- a/solution.py
+++ b/solution.py
@@ -122,12 +122,6 @@
 
 def exchange(array):
     return lax.all_to_all(array, "seq", 0, 0, tiled=True)
-
-
-def pick(ids, table):
-    return jnp.einsum(
-        "sq,qte->ste", onehot(ids, table.shape[0]), table, preferred_element_type=jnp.float32
-    )
 
 
 def local(queries, key_states, value_states, positions, random_blocks, global_blocks, out_grad):
@@ -199,12 +193,19 @@
 
     k_table = own_blocks[0].transpose(0, 2, 1, 3).reshape(table_rows, BLK, HD)
     v_table = own_blocks[1].transpose(0, 2, 1, 3).reshape(table_rows, BLK, HD)
-    answers_k = pick(asked_flat, k_table).astype(jnp.bfloat16).reshape(seq_count, capacity * BLK, HD)
-    answers_k = jnp.concatenate(
-        [answers_k, jnp.broadcast_to(my_pieces.reshape(1, glob_rows, HD), (seq_count, glob_rows, HD))],
+    slab_table = jnp.concatenate(
+        [k_table.reshape(table_rows * BLK // glob_rows, glob_rows, HD), my_pieces.reshape(1, glob_rows, HD)]
+    )
+    slab_ids = (asked_part[:, :, None] * (BLK // glob_rows) + jnp.arange(BLK // glob_rows)[None, None, :])
+    slab_ids = jnp.concatenate(
+        [
+            slab_ids.reshape(seq_count, capacity * BLK // glob_rows),
+            jnp.full((seq_count, 1), table_rows * BLK // glob_rows, jnp.int32),
+        ],
         axis=1,
     )
-    answers_v = pick(asked_flat, v_table).astype(jnp.bfloat16).reshape(seq_count, capacity * BLK, HD)
+    answers_k = slab_table[slab_ids].reshape(seq_count, capacity * BLK + glob_rows, HD)
+    answers_v = v_table[asked_flat].reshape(seq_count, capacity * BLK, HD)
     padded = extended(paired, (("seq", 1),), BLK)
     answers_k, padded = lax.optimization_barrier((answers_k, padded))
     fetched_k = exchange(answers_k)

time: 532 us -> 533 us (level)
  local copies, waits for them, and re-layouts: 84.3 us -> 94.4 us
    gather x0 -> x2, local copies, waits for them, and re-layouts: none -> 10.1 us  [the longest x1 7.01 us: local(): slab_table[slab_ids].reshape(seq_count, capacity * BLK + glob_rows, HD)]
    convert_element_type x2 -> x0, local copies, waits for them, and re-layouts: 7.36 us -> none  [the longest x1 4.66 us: local(): pick(asked_flat, v_table).astype(jnp.bfloat16)]
    optimization_barrier x0 -> x1, local copies, waits for them, and re-layouts: none -> 7.02 us  [local(): answers_v, fetched_k = lax.optimization_barrier((answers_v, fetched_k))]
    unnamed x65 -> x67, local copies, waits for them, and re-layouts: 20.9 us -> 20.9 us
  transfers between devices with their start and end apart: 10 -> 10, of which waited for: 9 -> 9; matrix products, arithmetic and copies ran while one was open for 24% -> 25% of each run, Pallas kernels for 0% -> 0%
where the time goes in v5:
time: 533 us; the launch traced here: 523 us
  waiting for transfers between devices  269 us (50%)
  local copies, waits for them, and re-layouts  94.4 us (18%)
  starting transfers between devices  72.9 us (14%)
  matrix products  44 us (8%)
  other arithmetic  29.8 us (6%)
  between operations  12.8 us (2%)
    all_to_all x6, waiting for transfers between devices, exchange(): return lax.all_to_all(array, 'seq', 0, 0, tiled=True)  193 us
    ppermute x2, waiting for transfers between devices, shifted(): return lax.ppermute(array, axis, pairs)  72.5 us
    all_to_all x6, starting transfers between devices, exchange(): return lax.all_to_all(array, 'seq', 0, 0, tiled=True)  61.3 us
    unnamed x67, local copies, waits for them, and re-layouts  20.9 us
  transfers between devices with their start and end apart: 10, of which 9 were waited for; matrix products, arithmetic and copies ran while one was open for 25% of the time, Pallas kernels for 0%

profile of v5, /device:TPU:32, one launch (start us, length us, event | category | flops | bytes accessed | tf_op | source)
XLA Modules:
  0.0 523.0 jit_solution(7011196927799711941)
XLA Ops:
  14.1 15.0 %all-to-all-start = ((bf16[128,2,576]{2,1,0:T(2,128)(2,1)}), bf16[128,2,576]{2,1,0:T(2,128)(2,1)S(1)}, u32[]{:S(2)}, u32[]{:S(2)}) async-start(bf16[128,2,576]{2,1,0:T(2,128)(2,1)} %reshape.1306), calls=%async_computation | async-start | bytes 655360 | tf_op jit(solution)/shard_map/all_to_all | solution.py:124
  30.1 3.4 collective-permute-start
  33.4 2.5 collective-permute-start.1
  40.2 2.1 collective-permute-done
  46.3 7.0 %gather_fusion = bf16[2176,8,128]{2,1,0:T(8,128)(2,1)} fusion(bf16[129,8,128]{2,1,0:T(8,128)(2,1)S(1)} %pad_maximum_fusion.6, s32[3072]{0:T(1024)S(1)} %pad_clamp_fusion), kind=kCustom, calls=%fused_computation | custom fusion | bytes 8921600 | tf_op jit(solution)/shard_map/gather | solution.py:207
  53.3 14.0 %all-to-all-start.1 = ((bf16[128,136,128]{2,1,0:T(8,128)(2,1)}), bf16[128,136,128]{2,1,0:T(8,128)(2,1)}, u32[]{:S(2)}, u32[]{:S(2)}) async-start(bf16[128,136,128]{2,1,0:T(8,128)(2,1)} %bitcast.302), calls=%async_computation.1 | async-start | bytes 8912896 | tf_op jit(solution)/shard_map/all_to_all | solution.py:124
  67.6 3.1 gather_fusion.1
  70.7 99.0 %all-to-all-done.1 = bf16[128,136,128]{2,1,0:T(8,128)(2,1)} async-done(((bf16[128,136,128]{2,1,0:T(8,128)(2,1)}), bf16[128,136,128]{2,1,0:T(8,128)(2,1)}, u32[]{:S(2)}, u32[]{:S(2)}) %all-to-all-start.1) | async-done | bytes 4456480 | tf_op jit(solution)/shard_map/all_to_all | solution.py:124
  169.7 8.3 %all-to-all-start.2 = ((bf16[128,128,128]{2,1,0:T(8,128)(2,1)}), bf16[128,128,128]{2,1,0:T(8,128)(2,1)}, u32[]{:S(2)}, u32[]{:S(2)}) async-start(bf16[128,128,128]{2,1,0:T(8,128)(2,1)} %bitcast.303), calls=%async_computation.2 | async-start | bytes 8388608 | tf_op jit(solution)/shard_map/all_to_all | solution.py:124
  189.1 4.7 slice.389
  193.8 7.0 %copy.276 = bf16[128,136,128]{0,2,1:T(8,128)(2,1)} copy(bf16[128,136,128]{2,1,0:T(8,128)(2,1)} %all-to-all-done.1) | data formatting | bytes 8912896 | tf_op jit(solution)/shard_map/optimization_barrier | solution.py:212
  202.1 2.9 gather_fusion.2
  211.9 2.0 fusion.5
  213.9 3.3 bitcast_convert_fusion
  218.7 4.7 copy.303
  223.4 49.2 %all-to-all-done.2 = bf16[128,128,128]{2,1,0:T(8,128)(2,1)} async-done(((bf16[128,128,128]{2,1,0:T(8,128)(2,1)}), bf16[128,128,128]{2,1,0:T(8,128)(2,1)}, u32[]{:S(2)}, u32[]{:S(2)}) %all-to-all-start.2) | async-done | bytes 4194336 | tf_op jit(solution)/shard_map/all_to_all | solution.py:124
  272.7 7.8 %all-to-all-start.4 = ((bf16[128,128,128]{2,1,0:T(8,128)(2,1)}), bf16[128,128,128]{2,1,0:T(8,128)(2,1)}, u32[]{:S(2)}, u32[]{:S(2)}) async-start(bf16[128,128,128]{2,1,0:T(8,128)(2,1)} %bitcast.304), calls=%async_computation.4 | async-start | bytes 8388608 | tf_op jit(solution)/shard_map/all_to_all | solution.py:124
  280.5 5.3 %fusion.20 = f32[4,4,128,4,64]{2,4,3,1,0:T(8,128)} fusion(bf16[4,320,4,128,1]{3,1,4,2,0:T(8,128)(2,1)} %bitcast.326, f32[4,4,320,64,4]{2,3,4,1,0:T(8,128)} %copy-done, f32[4,4,4,64]{3,2,1,0:T(4,128)S(1)} %add.333, f32[4,4,4,64]{3,2,1,0:T(4,128)S(1)} %max.8, pred[4,320]{1,0:T(4,128)(4,1)S(1)} %broadcast_in_dim.274), kind=kOutput, calls=%fused_computation.45 | convolution fusion | flops 342097920 | bytes 8684800 | tf_op jit(solution)/shard_map/rhgtk,rkhd->rthgd/dot_general | solution.py:271
  285.8 6.0 %fusion.18 = f32[4,4,320,128,1]{3,2,4,1,0:T(8,128)} fusion(bf16[4,64,4,4,128]{4,3,2,1,0:T(4,128)(2,1)S(1)} %copy-done.17, f32[4,4,320,64,4]{2,3,4,1,0:T(8,128)} %copy-done, f32[4,4,4,64]{3,2,1,0:T(4,128)S(1)} %add.333, f32[4,4,4,64]{3,2,1,0:T(4,128)S(1)} %max.8, pred[4,320]{1,0:T(4,128)(4,1)S(1)} %broadcast_in_dim.274), kind=kOutput, calls=%fused_computation.43 | convolution fusion | flops 342097920 | bytes 8946944 | tf_op jit(solution)/shard_map/rhgtk,rthgd->rkhd/dot_general | solution.py:287
  291.8 2.9 gather_fusion.3
  294.7 5.0 multiply_reduce_fusion
  299.8 5.0 fusion.2
  305.8 2.3 copy-done.2
  308.3 2.3 fusion.12
  311.6 2.8 fusion.85
  314.4 3.1 copy.322
  317.6 3.2 copy.321
  320.7 2.9 fusion.91
  325.6 2.1 copy_dynamic-update-slice_fusion
  327.8 2.4 copy-done.4
  331.3 2.0 reshape.1223
  333.3 2.3 copy.294
  335.6 2.2 reshape.1224
  340.1 2.9 copy.289
  344.5 2.4 pad_maximum_fusion
  346.9 25.9 %all-to-all-done.4 = bf16[128,128,128]{2,1,0:T(8,128)(2,1)} async-done(((bf16[128,128,128]{2,1,0:T(8,128)(2,1)}), bf16[128,128,128]{2,1,0:T(8,128)(2,1)}, u32[]{:S(2)}, u32[]{:S(2)}) %all-to-all-start.4) | async-done | bytes 4194336 | tf_op jit(solution)/shard_map/all_to_all | solution.py:124
  372.8 7.7 %all-to-all-start.3 = ((bf16[128,144,128]{2,1,0:T(8,128)(2,1)}), bf16[128,144,128]{2,1,0:T(8,128)(2,1)}, u32[]{:S(2)}, u32[]{:S(2)}) async-start(bf16[128,144,128]{2,1,0:T(8,128)(2,1)} %pad_maximum_fusion), calls=%async_computation.3 | async-start | bytes 9437184 | tf_op jit(solution)/shard_map/all_to_all | solution.py:124
  385.4 2.2 slice_bitcast_fusion.2
  388.9 3.0 collective-permute-start.2
  391.9 4.6 fusion.26
  398.9 2.9 collective-permute-start.3
  401.8 2.5 copy.309
  404.3 72.5 %collective-permute-done.2 = bf16[2,64,4,128]{3,2,1,0:T(4,128)(2,1)} collective-permute-done((bf16[2,64,4,128]{3,2,1,0:T(4,128)(2,1)}, bf16[2,64,4,128]{3,2,1,0:T(4,128)(2,1)}, u32[]{:S(2)}, u32[]{:S(2)}) %collective-permute-start.2) | collective-permute-done | bytes 131104 | tf_op jit(solution)/shard_map/ppermute | solution.py:40
  478.9 5.3 %all-to-all-done.3 = bf16[128,144,128]{2,1,0:T(8,128)(2,1)} async-done(((bf16[128,144,128]{2,1,0:T(8,128)(2,1)}), bf16[128,144,128]{2,1,0:T(8,128)(2,1)}, u32[]{:S(2)}, u32[]{:S(2)}) %all-to-all-start.3) | async-done | bytes 4718624 | tf_op jit(solution)/shard_map/all_to_all | solution.py:124
  485.5 2.5 slice.458
  488.0 2.4 fusion.23
  491.4 8.4 %all-to-all-start.5 = ((f32[128,2,512]{2,1,0:T(2,128)}), f32[128,2,512]{2,1,0:T(2,128)S(1)}, u32[]{:S(2)}, u32[]{:S(2)}) async-start(f32[128,2,512]{2,1,0:T(2,128)} %broadcast_select_fusion), calls=%async_computation.5 | async-start | bytes 1048576 | tf_op jit(solution)/shard_map/all_to_all | solution.py:124
  502.3 13.4 %all-to-all-done.5 = f32[128,2,512]{2,1,0:T(2,128)S(1)} async-done(((f32[128,2,512]{2,1,0:T(2,128)}), f32[128,2,512]{2,1,0:T(2,128)S(1)}, u32[]{:S(2)}, u32[]{:S(2)}) %all-to-all-start.5) | async-done | bytes 524320 | tf_op jit(solution)/shard_map/all_to_all | solution.py:124
  (204 shorter events, 63.7 us)
Async XLA Ops:
  0.6 28.5 %copy-start.22 = (s32[3,256]{1,0:T(4,128)S(1)}, s32[3,256]{1,0:T(4,128)}, u32[]{:S(2)}) copy-start(s32[3,256]{1,0:T(4,128)} %param.22) | copy-start | bytes 9220
  0.6 28.5 %copy-start.21 = (bf16[256,512]{1,0:T(8,128)(2,1)S(1)}, bf16[256,512]{1,0:T(8,128)(2,1)}, u32[]{:S(2)}) copy-start(bf16[256,512]{1,0:T(8,128)(2,1)} %param.20) | copy-start | bytes 786436
  9.4 20.4 %copy-start.11 = (bf16[256,512]{1,0:T(8,128)(2,1)S(1)}, bf16[256,512]{1,0:T(8,128)(2,1)}, u32[]{:S(2)}) copy-start(bf16[256,512]{1,0:T(8,128)(2,1)} %param.21) | copy-start | bytes 786436
  14.1 31.0 %all-to-all-start = ((bf16[128,2,576]{2,1,0:T(2,128)(2,1)}), bf16[128,2,576]{2,1,0:T(2,128)(2,1)S(1)}, u32[]{:S(2)}, u32[]{:S(2)}) async-start(bf16[128,2,576]{2,1,0:T(2,128)(2,1)} %reshape.1306), calls=%async_computation | async-start | bytes 655360 | tf_op jit(solution)/shard_map/all_to_all | solution.py:124
  30.1 12.2 %collective-permute-start = (bf16[2,64,512]{1,2,0:T(8,128)(2,1)S(1)}, bf16[2,64,512]{1,2,0:T(8,128)(2,1)S(1)}, u32[]{:S(2)}, u32[]{:S(2)}) collective-permute-start(bf16[2,64,512]{1,2,0:T(8,128)(2,1)S(1)} %get-tuple-element.149), channel_id=1, source_target_pairs={{0,2},{2,4},{4,6},{6,8},{8,10},{10,12},{12,14},{14,16},{16,18},{18... | collective-permute-start | bytes 393224 | tf_op jit(solution)/shard_map/ppermute | solution.py:26
  33.4 9.9 %collective-permute-start.1 = (bf16[2,64,512]{1,2,0:T(8,128)(2,1)S(1)}, bf16[2,64,512]{1,2,0:T(8,128)(2,1)S(1)}, u32[]{:S(2)}, u32[]{:S(2)}) collective-permute-start(bf16[2,64,512]{1,2,0:T(8,128)(2,1)S(1)} %get-tuple-element.150), channel_id=1, source_target_pairs={{2,0},{4,2},{6,4},{8,6},{10,8},{12,10},{14,12},{16,14},{18,16},{20... | collective-permute-start | bytes 393224 | tf_op jit(solution)/shard_map/ppermute | solution.py:27
  53.3 116.4 %all-to-all-start.1 = ((bf16[128,136,128]{2,1,0:T(8,128)(2,1)}), bf16[128,136,128]{2,1,0:T(8,128)(2,1)}, u32[]{:S(2)}, u32[]{:S(2)}) async-start(bf16[128,136,128]{2,1,0:T(8,128)(2,1)} %bitcast.302), calls=%async_computation.1 | async-start | bytes 8912896 | tf_op jit(solution)/shard_map/all_to_all | solution.py:124
  169.7 8.6 %copy-start.13 = (bf16[256,2048]{1,0:T(8,128)(2,1)S(1)}, bf16[256,2048]{1,0:T(8,128)(2,1)}, u32[]{:S(2)}) copy-start(bf16[256,2048]{1,0:T(8,128)(2,1)} %param.25) | copy-start | bytes 3145732
  169.7 10.1 %copy-start.14 = (bf16[256,2048]{1,0:T(8,128)(2,1)S(1)}, bf16[256,2048]{1,0:T(8,128)(2,1)}, u32[]{:S(2)}) copy-start(bf16[256,2048]{1,0:T(8,128)(2,1)} %param.19) | copy-start | bytes 3145732
  169.7 102.9 %all-to-all-start.2 = ((bf16[128,128,128]{2,1,0:T(8,128)(2,1)}), bf16[128,128,128]{2,1,0:T(8,128)(2,1)}, u32[]{:S(2)}, u32[]{:S(2)}) async-start(bf16[128,128,128]{2,1,0:T(8,128)(2,1)} %bitcast.303), calls=%async_computation.2 | async-start | bytes 8388608 | tf_op jit(solution)/shard_map/all_to_all | solution.py:124
  205.0 3.4 copy-start.5
  209.3 4.7 copy-start.1
  210.4 3.5 copy-start
  211.9 2.0 copy-start.16
  272.7 100.1 %all-to-all-start.4 = ((bf16[128,128,128]{2,1,0:T(8,128)(2,1)}), bf16[128,128,128]{2,1,0:T(8,128)(2,1)}, u32[]{:S(2)}, u32[]{:S(2)}) async-start(bf16[128,128,128]{2,1,0:T(8,128)(2,1)} %bitcast.304), calls=%async_computation.4 | async-start | bytes 8388608 | tf_op jit(solution)/shard_map/all_to_all | solution.py:124
  280.5 5.3 %copy-start.17 = (bf16[4,64,4,4,128]{4,3,2,1,0:T(4,128)(2,1)S(1)}, bf16[4,64,4,4,128]{4,3,2,1,0:T(4,128)(2,1)}, u32[]{:S(2)}) copy-start(bf16[4,64,4,4,128]{4,3,2,1,0:T(4,128)(2,1)} %reshape.1220) | copy-start | bytes 3145732
  294.7 5.1 copy-start.19
  294.7 5.1 copy-start.12
  294.7 5.1 copy-start.18
  304.8 5.8 %copy-start.3 = (bf16[4,4,4,64,320]{4,3,2,1,0:T(8,128)(2,1)}, bf16[4,4,4,64,320]{4,3,2,1,0:T(8,128)(2,1)S(1)}, u32[]{:S(2)}) copy-start(bf16[4,4,4,64,320]{4,3,2,1,0:T(8,128)(2,1)S(1)} %fusion.2) | copy-start | bytes 7864324
  304.8 3.3 copy-start.2
  304.8 3.5 copy-start.20
  308.3 2.3 copy-start.6
  323.7 2.0 copy-start.9
  327.7 2.4 copy-start.4
  340.0 2.9 copy-start.7
  340.1 2.9 copy-start.8
  343.0 1.4 copy-start.10
  346.9 37.6 %copy-start.24 = (s32[4]{0:T(128)S(1)}, s32[4]{0:T(128)}, u32[]{:S(2)}) copy-start(s32[4]{0:T(128)} %constant.267.clone.1) | copy-start | bytes 52
  372.8 111.4 %all-to-all-start.3 = ((bf16[128,144,128]{2,1,0:T(8,128)(2,1)}), bf16[128,144,128]{2,1,0:T(8,128)(2,1)}, u32[]{:S(2)}, u32[]{:S(2)}) async-start(bf16[128,144,128]{2,1,0:T(8,128)(2,1)} %pad_maximum_fusion), calls=%async_computation.3 | async-start | bytes 9437184 | tf_op jit(solution)/shard_map/all_to_all | solution.py:124
  387.5 8.9 %copy-start.15 = (bf16[4,64,4,4,128]{4,1,3,2,0:T(8,128)(2,1)S(1)}, bf16[4,64,4,4,128]{4,1,3,2,0:T(8,128)(2,1)}, u32[]{:S(2)}) copy-start(bf16[4,64,4,4,128]{4,1,3,2,0:T(8,128)(2,1)} %get-tuple-element.193) | copy-start | bytes 3145732
  388.9 87.9 %collective-permute-start.2 = (bf16[2,64,4,128]{3,2,1,0:T(4,128)(2,1)}, bf16[2,64,4,128]{3,2,1,0:T(4,128)(2,1)}, u32[]{:S(2)}, u32[]{:S(2)}) collective-permute-start(bf16[2,64,4,128]{3,2,1,0:T(4,128)(2,1)} %get-tuple-element.135), channel_id=1, source_target_pairs={{2,0},{4,2},{6,4},{8,6},{10,8},{12,10},{14,12},{16,14},{18,16},{20... | collective-permute-start | bytes 393224 | tf_op jit(solution)/shard_map/ppermute | solution.py:40
  398.9 79.0 %collective-permute-start.3 = (bf16[2,64,4,128]{3,2,1,0:T(4,128)(2,1)}, bf16[2,64,4,128]{3,2,1,0:T(4,128)(2,1)}, u32[]{:S(2)}, u32[]{:S(2)}) collective-permute-start(bf16[2,64,4,128]{3,2,1,0:T(4,128)(2,1)} %get-tuple-element.134), channel_id=1, source_target_pairs={{0,2},{2,4},{4,6},{6,8},{8,10},{10,12},{12,14},{14,16},{16,18},{18... | collective-permute-start | bytes 393224 | tf_op jit(solution)/shard_map/ppermute | solution.py:40
  491.4 24.4 %all-to-all-start.5 = ((f32[128,2,512]{2,1,0:T(2,128)}), f32[128,2,512]{2,1,0:T(2,128)S(1)}, u32[]{:S(2)}, u32[]{:S(2)}) async-start(f32[128,2,512]{2,1,0:T(2,128)} %broadcast_select_fusion), calls=%async_computation.5 | async-start | bytes 1048576 | tf_op jit(solution)/shard_map/all_to_all | solution.py:124
  501.2 15.1 %copy-start.23 = (pred[2]{0:T(512)(128)(4,1)S(1)}, pred[2]{0:T(512)(128)(4,1)}, u32[]{:S(2)}) copy-start(pred[2]{0:T(512)(128)(4,1)} %get-tuple-element.114) | copy-start | bytes 10

commit v6 on v5

--- a/solution.py
+++ b/solution.py
@@ -308,7 +308,9 @@
     to_owner = jnp.where(
         jnp.arange(seq_count)[:, None, None] == glob_owner[None, :, None], piece_sum[None], 0.0
     )
-    glob_grad = exchange(to_owner).transpose(1, 0, 2).reshape(GLOB, 2, BLK, kv_dev, HD)
+    to_owner = to_owner.reshape(seq_count, glob_rows, HD)
+    glob_grad = exchange(to_owner).reshape(seq_count, GLOB, piece)
+    glob_grad = glob_grad.transpose(1, 0, 2).reshape(GLOB, 2, BLK, kv_dev, HD)
 
     window_acc = jnp.pad(near_grad[:, :, 0], ((0, 0), (0, 2), (0, 0), (0, 0), (0, 0)))
     window_acc = window_acc + jnp.pad(near_grad[:, :, 1], ((0, 0), (1, 1), (0, 0), (0, 0), (0, 0)))

time: 533 us -> 533 us (level)
  no operation moved by 1% of the time
where the time goes in v6:
time: 533 us; the launch traced here: 523 us
  waiting for transfers between devices  269 us (50%)
  local copies, waits for them, and re-layouts  94.6 us (18%)
  starting transfers between devices  72.9 us (14%)
  matrix products  44 us (8%)
  other arithmetic  29.9 us (6%)
  between operations  12.8 us (2%)
    all_to_all x6, waiting for transfers between devices, exchange(): return lax.all_to_all(array, 'seq', 0, 0, tiled=True)  193 us
    ppermute x2, waiting for transfers between devices, shifted(): return lax.ppermute(array, axis, pairs)  72.3 us
    all_to_all x6, starting transfers between devices, exchange(): return lax.all_to_all(array, 'seq', 0, 0, tiled=True)  61.3 us
    unnamed x67, local copies, waits for them, and re-layouts  20.9 us
  transfers between devices with their start and end apart: 10, of which 9 were waited for; matrix products, arithmetic and copies ran while one was open for 25% of the time, Pallas kernels for 0%

profile of v6, /device:TPU:32, one launch (start us, length us, event | category | flops | bytes accessed | tf_op | source)
XLA Modules:
  0.0 523.1 jit_solution(7348128261301687688)
XLA Ops:
  14.1 15.0 %all-to-all-start = ((bf16[128,2,576]{2,1,0:T(2,128)(2,1)}), bf16[128,2,576]{2,1,0:T(2,128)(2,1)S(1)}, u32[]{:S(2)}, u32[]{:S(2)}) async-start(bf16[128,2,576]{2,1,0:T(2,128)(2,1)} %reshape.1313), calls=%async_computation | async-start | bytes 655360 | tf_op jit(solution)/shard_map/all_to_all | solution.py:124
  30.1 3.4 collective-permute-start
  33.5 2.5 collective-permute-start.1
  40.2 2.1 collective-permute-done
  46.4 7.0 %gather_fusion = bf16[2176,8,128]{2,1,0:T(8,128)(2,1)} fusion(bf16[129,8,128]{2,1,0:T(8,128)(2,1)S(1)} %pad_maximum_fusion.6, s32[3072]{0:T(1024)S(1)} %pad_clamp_fusion), kind=kCustom, calls=%fused_computation | custom fusion | bytes 8921600 | tf_op jit(solution)/shard_map/gather | solution.py:207
  53.4 14.0 %all-to-all-start.1 = ((bf16[128,136,128]{2,1,0:T(8,128)(2,1)}), bf16[128,136,128]{2,1,0:T(8,128)(2,1)}, u32[]{:S(2)}, u32[]{:S(2)}) async-start(bf16[128,136,128]{2,1,0:T(8,128)(2,1)} %bitcast.303), calls=%async_computation.1 | async-start | bytes 8912896 | tf_op jit(solution)/shard_map/all_to_all | solution.py:124
  67.7 3.1 gather_fusion.1
  70.8 99.0 %all-to-all-done.1 = bf16[128,136,128]{2,1,0:T(8,128)(2,1)} async-done(((bf16[128,136,128]{2,1,0:T(8,128)(2,1)}), bf16[128,136,128]{2,1,0:T(8,128)(2,1)}, u32[]{:S(2)}, u32[]{:S(2)}) %all-to-all-start.1) | async-done | bytes 4456480 | tf_op jit(solution)/shard_map/all_to_all | solution.py:124
  169.8 8.3 %all-to-all-start.2 = ((bf16[128,128,128]{2,1,0:T(8,128)(2,1)}), bf16[128,128,128]{2,1,0:T(8,128)(2,1)}, u32[]{:S(2)}, u32[]{:S(2)}) async-start(bf16[128,128,128]{2,1,0:T(8,128)(2,1)} %bitcast.304), calls=%async_computation.2 | async-start | bytes 8388608 | tf_op jit(solution)/shard_map/all_to_all | solution.py:124
  189.2 4.7 slice.389
  193.9 7.0 %copy.284 = bf16[128,136,128]{0,2,1:T(8,128)(2,1)} copy(bf16[128,136,128]{2,1,0:T(8,128)(2,1)} %all-to-all-done.1) | data formatting | bytes 8912896 | tf_op jit(solution)/shard_map/optimization_barrier | solution.py:212
  202.2 2.9 gather_fusion.2
  212.0 2.0 fusion.5
  214.0 3.3 bitcast_convert_fusion
  218.7 4.7 copy.311
  223.5 49.2 %all-to-all-done.2 = bf16[128,128,128]{2,1,0:T(8,128)(2,1)} async-done(((bf16[128,128,128]{2,1,0:T(8,128)(2,1)}), bf16[128,128,128]{2,1,0:T(8,128)(2,1)}, u32[]{:S(2)}, u32[]{:S(2)}) %all-to-all-start.2) | async-done | bytes 4194336 | tf_op jit(solution)/shard_map/all_to_all | solution.py:124
  272.7 7.8 %all-to-all-start.4 = ((bf16[128,128,128]{2,1,0:T(8,128)(2,1)}), bf16[128,128,128]{2,1,0:T(8,128)(2,1)}, u32[]{:S(2)}, u32[]{:S(2)}) async-start(bf16[128,128,128]{2,1,0:T(8,128)(2,1)} %bitcast.305), calls=%async_computation.4 | async-start | bytes 8388608 | tf_op jit(solution)/shard_map/all_to_all | solution.py:124
  280.5 5.3 %fusion.20 = f32[4,4,128,4,64]{2,4,3,1,0:T(8,128)} fusion(bf16[4,320,4,128,1]{3,1,4,2,0:T(8,128)(2,1)} %bitcast.327, f32[4,4,320,64,4]{2,3,4,1,0:T(8,128)} %copy-done, f32[4,4,4,64]{3,2,1,0:T(4,128)S(1)} %add.333, f32[4,4,4,64]{3,2,1,0:T(4,128)S(1)} %max.8, pred[4,320]{1,0:T(4,128)(4,1)S(1)} %broadcast_in_dim.276), kind=kOutput, calls=%fused_computation.45 | convolution fusion | flops 342097920 | bytes 8684800 | tf_op jit(solution)/shard_map/rhgtk,rkhd->rthgd/dot_general | solution.py:271
  285.8 6.0 %fusion.18 = f32[4,4,320,128,1]{3,2,4,1,0:T(8,128)} fusion(bf16[4,64,4,4,128]{4,3,2,1,0:T(4,128)(2,1)S(1)} %copy-done.17, f32[4,4,320,64,4]{2,3,4,1,0:T(8,128)} %copy-done, f32[4,4,4,64]{3,2,1,0:T(4,128)S(1)} %add.333, f32[4,4,4,64]{3,2,1,0:T(4,128)S(1)} %max.8, pred[4,320]{1,0:T(4,128)(4,1)S(1)} %broadcast_in_dim.276), kind=kOutput, calls=%fused_computation.43 | convolution fusion | flops 342097920 | bytes 8946944 | tf_op jit(solution)/shard_map/rhgtk,rthgd->rkhd/dot_general | solution.py:287
  291.9 2.9 gather_fusion.3
  294.8 5.0 multiply_reduce_fusion
  299.8 5.0 fusion.2
  305.9 2.3 copy-done.2
  308.4 2.3 fusion.12
  311.7 2.8 fusion.85
  314.5 3.1 copy.331
  317.6 3.2 copy.330
  320.8 2.9 fusion.91
  325.7 2.1 copy_dynamic-update-slice_fusion
  327.8 2.4 copy-done.4
  331.4 2.0 reshape.1230
  333.4 2.3 copy.302
  335.7 2.2 reshape.1231
  340.1 2.9 copy.297
  344.6 2.4 pad_maximum_fusion
  346.9 25.9 %all-to-all-done.4 = bf16[128,128,128]{2,1,0:T(8,128)(2,1)} async-done(((bf16[128,128,128]{2,1,0:T(8,128)(2,1)}), bf16[128,128,128]{2,1,0:T(8,128)(2,1)}, u32[]{:S(2)}, u32[]{:S(2)}) %all-to-all-start.4) | async-done | bytes 4194336 | tf_op jit(solution)/shard_map/all_to_all | solution.py:124
  372.8 7.7 %all-to-all-start.3 = ((bf16[128,144,128]{2,1,0:T(8,128)(2,1)}), bf16[128,144,128]{2,1,0:T(8,128)(2,1)}, u32[]{:S(2)}, u32[]{:S(2)}) async-start(bf16[128,144,128]{2,1,0:T(8,128)(2,1)} %pad_maximum_fusion), calls=%async_computation.3 | async-start | bytes 9437184 | tf_op jit(solution)/shard_map/all_to_all | solution.py:124
  385.6 2.2 slice_bitcast_fusion.2
  389.2 3.0 collective-permute-start.2
  392.1 4.6 fusion.26
  399.1 2.9 collective-permute-start.3
  402.1 2.5 copy.319
  404.6 72.3 %collective-permute-done.2 = bf16[2,64,4,128]{3,2,1,0:T(4,128)(2,1)} collective-permute-done((bf16[2,64,4,128]{3,2,1,0:T(4,128)(2,1)}, bf16[2,64,4,128]{3,2,1,0:T(4,128)(2,1)}, u32[]{:S(2)}, u32[]{:S(2)}) %collective-permute-start.2) | collective-permute-done | bytes 131104 | tf_op jit(solution)/shard_map/ppermute | solution.py:40
  478.9 5.3 %all-to-all-done.3 = bf16[128,144,128]{2,1,0:T(8,128)(2,1)} async-done(((bf16[128,144,128]{2,1,0:T(8,128)(2,1)}), bf16[128,144,128]{2,1,0:T(8,128)(2,1)}, u32[]{:S(2)}, u32[]{:S(2)}) %all-to-all-start.3) | async-done | bytes 4718624 | tf_op jit(solution)/shard_map/all_to_all | solution.py:124
  485.5 2.5 slice.458
  488.0 2.4 fusion.23
  491.4 8.4 %all-to-all-start.5 = ((f32[128,8,128]{2,1,0:T(8,128)}), f32[128,8,128]{2,1,0:T(8,128)S(1)}, u32[]{:S(2)}, u32[]{:S(2)}) async-start(f32[128,8,128]{2,1,0:T(8,128)} %broadcast_select_fusion.1), calls=%async_computation.5 | async-start | bytes 1048576 | tf_op jit(solution)/shard_map/all_to_all | solution.py:124
  502.4 13.4 %all-to-all-done.5 = f32[128,8,128]{2,1,0:T(8,128)S(1)} async-done(((f32[128,8,128]{2,1,0:T(8,128)}), f32[128,8,128]{2,1,0:T(8,128)S(1)}, u32[]{:S(2)}, u32[]{:S(2)}) %all-to-all-start.5) | async-done | bytes 524320 | tf_op jit(solution)/shard_map/all_to_all | solution.py:124
  (207 shorter events, 64.1 us)
Async XLA Ops:
  0.6 28.5 %copy-start.22 = (s32[3,256]{1,0:T(4,128)S(1)}, s32[3,256]{1,0:T(4,128)}, u32[]{:S(2)}) copy-start(s32[3,256]{1,0:T(4,128)} %param.22) | copy-start | bytes 9220
  0.6 28.5 %copy-start.21 = (bf16[256,512]{1,0:T(8,128)(2,1)S(1)}, bf16[256,512]{1,0:T(8,128)(2,1)}, u32[]{:S(2)}) copy-start(bf16[256,512]{1,0:T(8,128)(2,1)} %param.20) | copy-start | bytes 786436
  9.4 20.4 %copy-start.11 = (bf16[256,512]{1,0:T(8,128)(2,1)S(1)}, bf16[256,512]{1,0:T(8,128)(2,1)}, u32[]{:S(2)}) copy-start(bf16[256,512]{1,0:T(8,128)(2,1)} %param.21) | copy-start | bytes 786436
  14.1 31.0 %all-to-all-start = ((bf16[128,2,576]{2,1,0:T(2,128)(2,1)}), bf16[128,2,576]{2,1,0:T(2,128)(2,1)S(1)}, u32[]{:S(2)}, u32[]{:S(2)}) async-start(bf16[128,2,576]{2,1,0:T(2,128)(2,1)} %reshape.1313), calls=%async_computation | async-start | bytes 655360 | tf_op jit(solution)/shard_map/all_to_all | solution.py:124
  30.1 12.2 %collective-permute-start = (bf16[2,64,512]{1,2,0:T(8,128)(2,1)S(1)}, bf16[2,64,512]{1,2,0:T(8,128)(2,1)S(1)}, u32[]{:S(2)}, u32[]{:S(2)}) collective-permute-start(bf16[2,64,512]{1,2,0:T(8,128)(2,1)S(1)} %get-tuple-element.149), channel_id=1, source_target_pairs={{0,2},{2,4},{4,6},{6,8},{8,10},{10,12},{12,14},{14,16},{16,18},{18... | collective-permute-start | bytes 393224 | tf_op jit(solution)/shard_map/ppermute | solution.py:26
  33.5 9.9 %collective-permute-start.1 = (bf16[2,64,512]{1,2,0:T(8,128)(2,1)S(1)}, bf16[2,64,512]{1,2,0:T(8,128)(2,1)S(1)}, u32[]{:S(2)}, u32[]{:S(2)}) collective-permute-start(bf16[2,64,512]{1,2,0:T(8,128)(2,1)S(1)} %get-tuple-element.150), channel_id=1, source_target_pairs={{2,0},{4,2},{6,4},{8,6},{10,8},{12,10},{14,12},{16,14},{18,16},{20... | collective-permute-start | bytes 393224 | tf_op jit(solution)/shard_map/ppermute | solution.py:27
  53.4 116.4 %all-to-all-start.1 = ((bf16[128,136,128]{2,1,0:T(8,128)(2,1)}), bf16[128,136,128]{2,1,0:T(8,128)(2,1)}, u32[]{:S(2)}, u32[]{:S(2)}) async-start(bf16[128,136,128]{2,1,0:T(8,128)(2,1)} %bitcast.303), calls=%async_computation.1 | async-start | bytes 8912896 | tf_op jit(solution)/shard_map/all_to_all | solution.py:124
  169.8 8.6 %copy-start.13 = (bf16[256,2048]{1,0:T(8,128)(2,1)S(1)}, bf16[256,2048]{1,0:T(8,128)(2,1)}, u32[]{:S(2)}) copy-start(bf16[256,2048]{1,0:T(8,128)(2,1)} %param.25) | copy-start | bytes 3145732
  169.8 10.1 %copy-start.14 = (bf16[256,2048]{1,0:T(8,128)(2,1)S(1)}, bf16[256,2048]{1,0:T(8,128)(2,1)}, u32[]{:S(2)}) copy-start(bf16[256,2048]{1,0:T(8,128)(2,1)} %param.19) | copy-start | bytes 3145732
  169.8 102.9 %all-to-all-start.2 = ((bf16[128,128,128]{2,1,0:T(8,128)(2,1)}), bf16[128,128,128]{2,1,0:T(8,128)(2,1)}, u32[]{:S(2)}, u32[]{:S(2)}) async-start(bf16[128,128,128]{2,1,0:T(8,128)(2,1)} %bitcast.304), calls=%async_computation.2 | async-start | bytes 8388608 | tf_op jit(solution)/shard_map/all_to_all | solution.py:124
  205.1 3.4 copy-start.5
  209.3 4.7 copy-start.1
  210.4 3.5 copy-start
  212.0 2.0 copy-start.16
  272.7 100.1 %all-to-all-start.4 = ((bf16[128,128,128]{2,1,0:T(8,128)(2,1)}), bf16[128,128,128]{2,1,0:T(8,128)(2,1)}, u32[]{:S(2)}, u32[]{:S(2)}) async-start(bf16[128,128,128]{2,1,0:T(8,128)(2,1)} %bitcast.305), calls=%async_computation.4 | async-start | bytes 8388608 | tf_op jit(solution)/shard_map/all_to_all | solution.py:124
  280.5 5.3 %copy-start.17 = (bf16[4,64,4,4,128]{4,3,2,1,0:T(4,128)(2,1)S(1)}, bf16[4,64,4,4,128]{4,3,2,1,0:T(4,128)(2,1)}, u32[]{:S(2)}) copy-start(bf16[4,64,4,4,128]{4,3,2,1,0:T(4,128)(2,1)} %reshape.1227) | copy-start | bytes 3145732
  294.7 5.1 copy-start.19
  294.8 5.1 copy-start.12
  294.8 5.1 copy-start.18
  304.8 5.8 %copy-start.3 = (bf16[4,4,4,64,320]{4,3,2,1,0:T(8,128)(2,1)}, bf16[4,4,4,64,320]{4,3,2,1,0:T(8,128)(2,1)S(1)}, u32[]{:S(2)}) copy-start(bf16[4,4,4,64,320]{4,3,2,1,0:T(8,128)(2,1)S(1)} %fusion.2) | copy-start | bytes 7864324
  304.9 3.3 copy-start.2
  304.9 3.5 copy-start.20
  308.4 2.3 copy-start.6
  323.7 2.0 copy-start.9
  327.8 2.4 copy-start.4
  340.1 2.9 copy-start.7
  340.1 2.9 copy-start.8
  343.1 1.4 copy-start.10
  346.9 37.8 %copy-start.24 = (s32[4]{0:T(128)S(1)}, s32[4]{0:T(128)}, u32[]{:S(2)}) copy-start(s32[4]{0:T(128)} %constant.267.clone.1) | copy-start | bytes 52
  372.8 111.4 %all-to-all-start.3 = ((bf16[128,144,128]{2,1,0:T(8,128)(2,1)}), bf16[128,144,128]{2,1,0:T(8,128)(2,1)}, u32[]{:S(2)}, u32[]{:S(2)}) async-start(bf16[128,144,128]{2,1,0:T(8,128)(2,1)} %pad_maximum_fusion), calls=%async_computation.3 | async-start | bytes 9437184 | tf_op jit(solution)/shard_map/all_to_all | solution.py:124
  387.8 8.9 %copy-start.15 = (bf16[4,64,4,4,128]{4,1,3,2,0:T(8,128)(2,1)S(1)}, bf16[4,64,4,4,128]{4,1,3,2,0:T(8,128)(2,1)}, u32[]{:S(2)}) copy-start(bf16[4,64,4,4,128]{4,1,3,2,0:T(8,128)(2,1)} %get-tuple-element.193) | copy-start | bytes 3145732
  389.2 87.7 %collective-permute-start.2 = (bf16[2,64,4,128]{3,2,1,0:T(4,128)(2,1)}, bf16[2,64,4,128]{3,2,1,0:T(4,128)(2,1)}, u32[]{:S(2)}, u32[]{:S(2)}) collective-permute-start(bf16[2,64,4,128]{3,2,1,0:T(4,128)(2,1)} %get-tuple-element.135), channel_id=1, source_target_pairs={{2,0},{4,2},{6,4},{8,6},{10,8},{12,10},{14,12},{16,14},{18,16},{20... | collective-permute-start | bytes 393224 | tf_op jit(solution)/shard_map/ppermute | solution.py:40
  399.1 78.8 %collective-permute-start.3 = (bf16[2,64,4,128]{3,2,1,0:T(4,128)(2,1)}, bf16[2,64,4,128]{3,2,1,0:T(4,128)(2,1)}, u32[]{:S(2)}, u32[]{:S(2)}) collective-permute-start(bf16[2,64,4,128]{3,2,1,0:T(4,128)(2,1)} %get-tuple-element.134), channel_id=1, source_target_pairs={{0,2},{2,4},{4,6},{6,8},{8,10},{10,12},{12,14},{14,16},{16,18},{18... | collective-permute-start | bytes 393224 | tf_op jit(solution)/shard_map/ppermute | solution.py:40
  491.4 24.4 %all-to-all-start.5 = ((f32[128,8,128]{2,1,0:T(8,128)}), f32[128,8,128]{2,1,0:T(8,128)S(1)}, u32[]{:S(2)}, u32[]{:S(2)}) async-start(f32[128,8,128]{2,1,0:T(8,128)} %broadcast_select_fusion.1), calls=%async_computation.5 | async-start | bytes 1048576 | tf_op jit(solution)/shard_map/all_to_all | solution.py:124
  501.6 14.8 %copy-start.23 = (pred[2]{0:T(512)(128)(4,1)S(1)}, pred[2]{0:T(512)(128)(4,1)}, u32[]{:S(2)}) copy-start(pred[2]{0:T(512)(128)(4,1)} %get-tuple-element.114) | copy-start | bytes 10

commit v7 on v4

--- a/solution.py
+++ b/solution.py
@@ -163,25 +163,33 @@
     slot_ids = jnp.arange(slot_count, dtype=jnp.int32)
     earlier = (owners[:, None] == owners[None, :]) & (slot_ids[None, :] < slot_ids[:, None])
     slot_pos = owners * capacity + jnp.sum(earlier, axis=1)
-    request = jnp.zeros((seq_count * capacity,), jnp.int32).at[slot_pos].set(req_code)
-    request = request.reshape(seq_count, capacity)
+    request = jnp.sum(
+        jnp.where(
+            slot_pos[None, :] == jnp.arange(seq_count * capacity, dtype=jnp.int32)[:, None],
+            req_code[None, :],
+            0,
+        ),
+        axis=1,
+    ).reshape(seq_count, capacity)
     glob_owner = global_blocks // block_rows
     glob_local = global_blocks % block_rows
-    glob_scatter = []
-    glob_cos, glob_sin = [], []
-    for which_glob in range(GLOB):
-        start = glob_local[which_glob] * BLK
-        block_cos, block_sin = tables(lax.dynamic_slice_in_dim(positions, start, BLK, 1))
-        glob_cos.append(block_cos)
-        glob_sin.append(block_sin)
-        block_keys = lax.dynamic_slice_in_dim(key_states, start, BLK, 0)
-        block_keys = rotate(
-            block_keys.reshape(BLK, kv_dev, HD).astype(jnp.float32), block_cos, block_sin
-        ).astype(jnp.bfloat16)
-        block_values = lax.dynamic_slice_in_dim(value_states, start, BLK, 0).reshape(BLK, kv_dev, HD)
-        glob_piece = jnp.stack([block_keys, block_values])
-        glob_piece = jnp.where(my_index == glob_owner[which_glob], glob_piece, jnp.zeros_like(glob_piece))
-        glob_scatter.append(glob_piece.reshape(seq_count, piece))
+    glob_tokens = (glob_local[:, None] * BLK + jnp.arange(BLK, dtype=jnp.int32)[None, :]).reshape(GLOB * BLK)
+    both_cos, both_sin = tables(positions[:, glob_tokens])
+    glob_cos = [both_cos[g * BLK : (g + 1) * BLK] for g in range(GLOB)]
+    glob_sin = [both_sin[g * BLK : (g + 1) * BLK] for g in range(GLOB)]
+    glob_keys = rotate(
+        key_states[glob_tokens].reshape(GLOB * BLK, kv_dev, HD).astype(jnp.float32), both_cos, both_sin
+    ).astype(jnp.bfloat16)
+    glob_values = value_states[glob_tokens].reshape(GLOB * BLK, kv_dev, HD)
+    glob_both = jnp.stack([glob_keys, glob_values]).reshape(2, GLOB, BLK, kv_dev, HD)
+    glob_both = jnp.where(
+        (my_index == glob_owner)[None, :, None, None, None], glob_both, jnp.zeros_like(glob_both)
+    )
+    glob_scatter = [
+        glob_both.transpose(1, 0, 2, 3, 4).reshape(GLOB, seq_count, piece).transpose(1, 0, 2).reshape(
+            seq_count, GLOB * piece
+        )
+    ]
     first_out = jnp.concatenate(
         glob_scatter
         + [request.astype(jnp.bfloat16), jnp.zeros((seq_count, code_cols - capacity), jnp.bfloat16)],

time: 532 us -> 527 us (level)
  local copies, waits for them, and re-layouts: 84.3 us -> 91.2 us
    unnamed x65 -> x83, local copies, waits for them, and re-layouts: 20.9 us -> 21.9 us
where the time goes in v7:
time: 527 us; the launch traced here: 521 us
  waiting for transfers between devices  272 us (52%)
  local copies, waits for them, and re-layouts  91.2 us (17%)
  starting transfers between devices  72 us (14%)
  matrix products  46.6 us (9%)
  other arithmetic  28.8 us (5%)
  between operations  10.1 us (2%)
    all_to_all x6, waiting for transfers between devices, exchange(): return lax.all_to_all(array, 'seq', 0, 0, tiled=True)  199 us
    ppermute x2, waiting for transfers between devices, shifted(): return lax.ppermute(array, axis, pairs)  70.7 us
    all_to_all x6, starting transfers between devices, exchange(): return lax.all_to_all(array, 'seq', 0, 0, tiled=True)  59.8 us
    unnamed x83, local copies, waits for them, and re-layouts  21.9 us
  transfers between devices with their start and end apart: 10, of which 9 were waited for; matrix products, arithmetic and copies ran while one was open for 24% of the time, Pallas kernels for 0%

profile of v7, /device:TPU:32, one launch (start us, length us, event | category | flops | bytes accessed | tf_op | source)
XLA Modules:
  0.0 520.8 jit_solution(10437609390444873878)
XLA Ops:
  14.2 15.0 %all-to-all-start = ((bf16[128,2,576]{2,1,0:T(2,128)(2,1)}), bf16[128,2,576]{2,1,0:T(2,128)(2,1)S(1)}, u32[]{:S(2)}, u32[]{:S(2)}) async-start(bf16[128,2,576]{2,1,0:T(2,128)(2,1)} %reshape.1171), calls=%async_computation | async-start | bytes 655360 | tf_op jit(solution)/shard_map/all_to_all | solution.py:124
  30.2 3.4 collective-permute-start
  33.6 3.0 collective-permute-start.1
  47.3 2.7 copy.260
  50.1 2.6 pad_maximum_fusion.1
  52.7 14.3 %all-to-all-start.1 = ((bf16[128,136,128]{2,1,0:T(8,128)(2,1)}), bf16[128,136,128]{2,1,0:T(8,128)(2,1)}, u32[]{:S(2)}, u32[]{:S(2)}) async-start(bf16[128,136,128]{2,1,0:T(8,128)(2,1)} %pad_maximum_fusion.1), calls=%async_computation.1 | async-start | bytes 8912896 | tf_op jit(solution)/shard_map/all_to_all | solution.py:124
  68.5 4.7 copy.264
  73.2 96.1 %all-to-all-done.1 = bf16[128,136,128]{2,1,0:T(8,128)(2,1)} async-done(((bf16[128,136,128]{2,1,0:T(8,128)(2,1)}), bf16[128,136,128]{2,1,0:T(8,128)(2,1)}, u32[]{:S(2)}, u32[]{:S(2)}) %all-to-all-start.1) | async-done | bytes 4456480 | tf_op jit(solution)/shard_map/all_to_all | solution.py:124
  169.3 8.3 %all-to-all-start.2 = ((bf16[128,128,128]{2,1,0:T(8,128)(2,1)}), bf16[128,128,128]{2,1,0:T(8,128)(2,1)}, u32[]{:S(2)}, u32[]{:S(2)}) async-start(bf16[128,128,128]{2,1,0:T(8,128)(2,1)} %bitcast.284), calls=%async_computation.2 | async-start | bytes 8388608 | tf_op jit(solution)/shard_map/all_to_all | solution.py:124
  189.7 4.8 slice.369
  194.7 2.9 gather_fusion.3
  204.5 2.0 fusion.5
  206.6 3.3 bitcast_convert_fusion
  211.3 4.7 copy.292
  216.0 56.2 %all-to-all-done.2 = bf16[128,128,128]{2,1,0:T(8,128)(2,1)} async-done(((bf16[128,128,128]{2,1,0:T(8,128)(2,1)}), bf16[128,128,128]{2,1,0:T(8,128)(2,1)}, u32[]{:S(2)}, u32[]{:S(2)}) %all-to-all-start.2) | async-done | bytes 4194336 | tf_op jit(solution)/shard_map/all_to_all | solution.py:124
  272.2 7.8 %all-to-all-start.4 = ((bf16[128,128,128]{2,1,0:T(8,128)(2,1)}), bf16[128,128,128]{2,1,0:T(8,128)(2,1)}, u32[]{:S(2)}, u32[]{:S(2)}) async-start(bf16[128,128,128]{2,1,0:T(8,128)(2,1)} %bitcast.285), calls=%async_computation.4 | async-start | bytes 8388608 | tf_op jit(solution)/shard_map/all_to_all | solution.py:124
  280.0 5.3 %fusion.20 = f32[4,4,128,4,64]{2,4,3,1,0:T(8,128)} fusion(bf16[4,320,4,128,1]{3,1,4,2,0:T(8,128)(2,1)} %bitcast.308, f32[4,4,320,64,4]{2,3,4,1,0:T(8,128)} %copy-done, f32[4,4,4,64]{3,2,1,0:T(4,128)S(1)} %add.314, f32[4,4,4,64]{3,2,1,0:T(4,128)S(1)} %max.8, pred[4,320]{1,0:T(4,128)(4,1)S(1)} %broadcast_in_dim.267), kind=kOutput, calls=%fused_computation.48 | convolution fusion | flops 342097920 | bytes 8684800 | tf_op jit(solution)/shard_map/rhgtk,rkhd->rthgd/dot_general | solution.py:278
  285.3 6.0 %fusion.18 = f32[4,4,320,128,1]{3,2,4,1,0:T(8,128)} fusion(bf16[4,64,4,4,128]{4,3,2,1,0:T(4,128)(2,1)S(1)} %copy-done.18, f32[4,4,320,64,4]{2,3,4,1,0:T(8,128)} %copy-done, f32[4,4,4,64]{3,2,1,0:T(4,128)S(1)} %add.314, f32[4,4,4,64]{3,2,1,0:T(4,128)S(1)} %max.8, pred[4,320]{1,0:T(4,128)(4,1)S(1)} %broadcast_in_dim.267), kind=kOutput, calls=%fused_computation.46 | convolution fusion | flops 342097920 | bytes 8946944 | tf_op jit(solution)/shard_map/rhgtk,rthgd->rkhd/dot_general | solution.py:294
  291.3 2.9 gather_fusion.4
  294.2 5.0 multiply_reduce_fusion
  299.3 5.0 fusion.2
  305.3 2.3 copy-done.2
  307.8 2.3 fusion.12
  311.1 2.8 fusion.82
  313.9 3.1 copy.311
  317.1 3.2 copy.310
  320.2 2.9 fusion.90
  323.2 1.9 copy_dynamic-update-slice_fusion.1
  325.1 2.1 copy_dynamic-update-slice_fusion
  327.2 2.4 copy-done.4
  330.8 2.0 reshape.1089
  332.8 2.3 copy.283
  335.1 2.3 reshape.1090
  339.6 2.9 copy.278
  344.0 2.4 pad_maximum_fusion
  346.4 25.9 %all-to-all-done.4 = bf16[128,128,128]{2,1,0:T(8,128)(2,1)} async-done(((bf16[128,128,128]{2,1,0:T(8,128)(2,1)}), bf16[128,128,128]{2,1,0:T(8,128)(2,1)}, u32[]{:S(2)}, u32[]{:S(2)}) %all-to-all-start.4) | async-done | bytes 4194336 | tf_op jit(solution)/shard_map/all_to_all | solution.py:124
  372.3 7.7 %all-to-all-start.3 = ((bf16[128,144,128]{2,1,0:T(8,128)(2,1)}), bf16[128,144,128]{2,1,0:T(8,128)(2,1)}, u32[]{:S(2)}, u32[]{:S(2)}) async-start(bf16[128,144,128]{2,1,0:T(8,128)(2,1)} %pad_maximum_fusion), calls=%async_computation.3 | async-start | bytes 9437184 | tf_op jit(solution)/shard_map/all_to_all | solution.py:124
  386.6 2.1 slice_bitcast_fusion.2
  390.1 3.0 collective-permute-start.2
  393.1 4.6 fusion.26
  400.1 2.9 collective-permute-start.3
  403.1 2.5 copy.298
  405.6 70.7 %collective-permute-done.2 = bf16[2,64,4,128]{3,2,1,0:T(4,128)(2,1)S(1)} collective-permute-done((bf16[2,64,4,128]{3,2,1,0:T(4,128)(2,1)}, bf16[2,64,4,128]{3,2,1,0:T(4,128)(2,1)S(1)}, u32[]{:S(2)}, u32[]{:S(2)}) %collective-permute-start.2) | collective-permute-done | bytes 131104 | tf_op jit(solution)/shard_map/ppermute | solution.py:40
  476.5 7.2 %all-to-all-done.3 = bf16[128,144,128]{2,1,0:T(8,128)(2,1)} async-done(((bf16[128,144,128]{2,1,0:T(8,128)(2,1)}), bf16[128,144,128]{2,1,0:T(8,128)(2,1)}, u32[]{:S(2)}, u32[]{:S(2)}) %all-to-all-start.3) | async-done | bytes 4718624 | tf_op jit(solution)/shard_map/all_to_all | solution.py:124
  485.0 2.5 slice.446
  487.6 2.4 fusion.23
  491.0 6.6 %all-to-all-start.5 = ((f32[128,2,512]{2,1,0:T(2,128)}), f32[128,2,512]{2,1,0:T(2,128)S(1)}, u32[]{:S(2)}, u32[]{:S(2)}) async-start(f32[128,2,512]{2,1,0:T(2,128)} %broadcast_select_fusion), calls=%async_computation.5 | async-start | bytes 1048576 | tf_op jit(solution)/shard_map/all_to_all | solution.py:124
  500.1 13.5 %all-to-all-done.5 = f32[128,2,512]{2,1,0:T(2,128)S(1)} async-done(((f32[128,2,512]{2,1,0:T(2,128)}), f32[128,2,512]{2,1,0:T(2,128)S(1)}, u32[]{:S(2)}, u32[]{:S(2)}) %all-to-all-start.5) | async-done | bytes 524320 | tf_op jit(solution)/shard_map/all_to_all | solution.py:124
  (219 shorter events, 68.2 us)
Async XLA Ops:
  6.2 23.0 %copy-start.30 = (s32[3,256]{1,0:T(4,128)S(1)}, s32[3,256]{1,0:T(4,128)}, u32[]{:S(2)}) copy-start(s32[3,256]{1,0:T(4,128)} %param.22) | copy-start | bytes 9220
  6.2 23.0 %copy-start.8 = (bf16[256,512]{1,0:T(8,128)(2,1)S(1)}, bf16[256,512]{1,0:T(8,128)(2,1)}, u32[]{:S(2)}) copy-start(bf16[256,512]{1,0:T(8,128)(2,1)} %param.20) | copy-start | bytes 786436
  9.7 20.1 %copy-start.5 = (bf16[256,512]{1,0:T(8,128)(2,1)S(1)}, bf16[256,512]{1,0:T(8,128)(2,1)}, u32[]{:S(2)}) copy-start(bf16[256,512]{1,0:T(8,128)(2,1)} %param.21) | copy-start | bytes 786436
  14.2 31.0 %all-to-all-start = ((bf16[128,2,576]{2,1,0:T(2,128)(2,1)}), bf16[128,2,576]{2,1,0:T(2,128)(2,1)S(1)}, u32[]{:S(2)}, u32[]{:S(2)}) async-start(bf16[128,2,576]{2,1,0:T(2,128)(2,1)} %reshape.1171), calls=%async_computation | async-start | bytes 655360 | tf_op jit(solution)/shard_map/all_to_all | solution.py:124
  30.2 12.2 %collective-permute-start = (bf16[2,64,512]{1,2,0:T(8,128)(2,1)S(1)}, bf16[2,64,512]{1,2,0:T(8,128)(2,1)S(1)}, u32[]{:S(2)}, u32[]{:S(2)}) collective-permute-start(bf16[2,64,512]{1,2,0:T(8,128)(2,1)S(1)} %get-tuple-element.150), channel_id=1, source_target_pairs={{0,2},{2,4},{4,6},{6,8},{8,10},{10,12},{12,14},{14,16},{16,18},{18... | collective-permute-start | bytes 393224 | tf_op jit(solution)/shard_map/ppermute | solution.py:26
  33.6 9.9 %collective-permute-start.1 = (bf16[2,64,512]{1,2,0:T(8,128)(2,1)S(1)}, bf16[2,64,512]{1,2,0:T(8,128)(2,1)S(1)}, u32[]{:S(2)}, u32[]{:S(2)}) collective-permute-start(bf16[2,64,512]{1,2,0:T(8,128)(2,1)S(1)} %get-tuple-element.151), channel_id=1, source_target_pairs={{2,0},{4,2},{6,4},{8,6},{10,8},{12,10},{14,12},{16,14},{18,16},{20... | collective-permute-start | bytes 393224 | tf_op jit(solution)/shard_map/ppermute | solution.py:27
  45.9 347.2 %copy-start.26 = (s32[256]{0:T(256)}, s32[256]{0:T(256)S(1)}, u32[]{:S(2)}) copy-start(s32[256]{0:T(256)S(1)} %reshape.1107) | copy-start | bytes 3076
  52.7 116.5 %all-to-all-start.1 = ((bf16[128,136,128]{2,1,0:T(8,128)(2,1)}), bf16[128,136,128]{2,1,0:T(8,128)(2,1)}, u32[]{:S(2)}, u32[]{:S(2)}) async-start(bf16[128,136,128]{2,1,0:T(8,128)(2,1)} %pad_maximum_fusion.1), calls=%async_computation.1 | async-start | bytes 8912896 | tf_op jit(solution)/shard_map/all_to_all | solution.py:124
  169.3 8.7 %copy-start.14 = (bf16[256,2048]{1,0:T(8,128)(2,1)S(1)}, bf16[256,2048]{1,0:T(8,128)(2,1)}, u32[]{:S(2)}) copy-start(bf16[256,2048]{1,0:T(8,128)(2,1)} %param.25) | copy-start | bytes 3145732
  169.3 10.2 %copy-start.15 = (bf16[256,2048]{1,0:T(8,128)(2,1)S(1)}, bf16[256,2048]{1,0:T(8,128)(2,1)}, u32[]{:S(2)}) copy-start(bf16[256,2048]{1,0:T(8,128)(2,1)} %param.19) | copy-start | bytes 3145732
  169.3 102.9 %all-to-all-start.2 = ((bf16[128,128,128]{2,1,0:T(8,128)(2,1)}), bf16[128,128,128]{2,1,0:T(8,128)(2,1)}, u32[]{:S(2)}, u32[]{:S(2)}) async-start(bf16[128,128,128]{2,1,0:T(8,128)(2,1)} %bitcast.284), calls=%async_computation.2 | async-start | bytes 8388608 | tf_op jit(solution)/shard_map/all_to_all | solution.py:124
  197.6 3.4 copy-start.6
  201.9 4.7 copy-start.1
  203.0 3.5 copy-start
  204.5 2.0 copy-start.17
  272.2 100.1 %all-to-all-start.4 = ((bf16[128,128,128]{2,1,0:T(8,128)(2,1)}), bf16[128,128,128]{2,1,0:T(8,128)(2,1)}, u32[]{:S(2)}, u32[]{:S(2)}) async-start(bf16[128,128,128]{2,1,0:T(8,128)(2,1)} %bitcast.285), calls=%async_computation.4 | async-start | bytes 8388608 | tf_op jit(solution)/shard_map/all_to_all | solution.py:124
  280.0 5.3 %copy-start.18 = (bf16[4,64,4,4,128]{4,3,2,1,0:T(4,128)(2,1)S(1)}, bf16[4,64,4,4,128]{4,3,2,1,0:T(4,128)(2,1)}, u32[]{:S(2)}) copy-start(bf16[4,64,4,4,128]{4,3,2,1,0:T(4,128)(2,1)} %reshape.1086) | copy-start | bytes 3145732
  294.2 5.1 copy-start.20
  294.2 5.1 copy-start.13
  294.2 5.1 copy-start.19
  304.3 5.8 %copy-start.3 = (bf16[4,4,4,64,320]{4,3,2,1,0:T(8,128)(2,1)}, bf16[4,4,4,64,320]{4,3,2,1,0:T(8,128)(2,1)S(1)}, u32[]{:S(2)}) copy-start(bf16[4,4,4,64,320]{4,3,2,1,0:T(8,128)(2,1)S(1)} %fusion.2) | copy-start | bytes 7864324
  304.3 3.3 copy-start.2
  304.3 3.5 copy-start.21
  307.8 2.3 copy-start.7
  323.1 2.0 copy-start.11
  327.2 2.4 copy-start.4
  339.6 2.9 copy-start.9
  339.6 2.9 copy-start.10
  342.5 1.4 copy-start.12
  346.4 38.2 %copy-start.32 = (s32[4]{0:T(128)S(1)}, s32[4]{0:T(128)}, u32[]{:S(2)}) copy-start(s32[4]{0:T(128)} %constant.253.clone.1) | copy-start | bytes 52
  372.3 111.4 %all-to-all-start.3 = ((bf16[128,144,128]{2,1,0:T(8,128)(2,1)}), bf16[128,144,128]{2,1,0:T(8,128)(2,1)}, u32[]{:S(2)}, u32[]{:S(2)}) async-start(bf16[128,144,128]{2,1,0:T(8,128)(2,1)} %pad_maximum_fusion), calls=%async_computation.3 | async-start | bytes 9437184 | tf_op jit(solution)/shard_map/all_to_all | solution.py:124
  384.5 8.6 %copy-start.28 = (s32[4,4]{1,0:T(4,128)}, s32[4,4]{1,0:T(4,128)S(1)}, u32[]{:S(2)}) copy-start(s32[4,4]{1,0:T(4,128)S(1)} %multiply_add_fusion.4) | copy-start | bytes 196
  388.8 8.9 %copy-start.16 = (bf16[4,64,4,4,128]{4,1,3,2,0:T(8,128)(2,1)S(1)}, bf16[4,64,4,4,128]{4,1,3,2,0:T(8,128)(2,1)}, u32[]{:S(2)}) copy-start(bf16[4,64,4,4,128]{4,1,3,2,0:T(8,128)(2,1)} %get-tuple-element.180) | copy-start | bytes 3145732
  390.1 86.1 %collective-permute-start.2 = (bf16[2,64,4,128]{3,2,1,0:T(4,128)(2,1)}, bf16[2,64,4,128]{3,2,1,0:T(4,128)(2,1)S(1)}, u32[]{:S(2)}, u32[]{:S(2)}) collective-permute-start(bf16[2,64,4,128]{3,2,1,0:T(4,128)(2,1)} %get-tuple-element.136), channel_id=1, source_target_pairs={{2,0},{4,2},{6,4},{8,6},{10,8},{12,10},{14,12},{16,14},{18,16},{20... | collective-permute-start | bytes 393224 | tf_op jit(solution)/shard_map/ppermute | solution.py:40
  400.1 76.3 %collective-permute-start.3 = (bf16[2,64,4,128]{3,2,1,0:T(4,128)(2,1)}, bf16[2,64,4,128]{3,2,1,0:T(4,128)(2,1)S(1)}, u32[]{:S(2)}, u32[]{:S(2)}) collective-permute-start(bf16[2,64,4,128]{3,2,1,0:T(4,128)(2,1)} %get-tuple-element.135), channel_id=1, source_target_pairs={{0,2},{2,4},{4,6},{6,8},{8,10},{10,12},{12,14},{14,16},{16,18},{18... | collective-permute-start | bytes 393224 | tf_op jit(solution)/shard_map/ppermute | solution.py:40
  485.0 2.5 copy-start.27
  485.0 2.5 copy-start.29
  491.0 22.7 %all-to-all-start.5 = ((f32[128,2,512]{2,1,0:T(2,128)}), f32[128,2,512]{2,1,0:T(2,128)S(1)}, u32[]{:S(2)}, u32[]{:S(2)}) async-start(f32[128,2,512]{2,1,0:T(2,128)} %broadcast_select_fusion), calls=%async_computation.5 | async-start | bytes 1048576 | tf_op jit(solution)/shard_map/all_to_all | solution.py:124
  499.0 15.2 %copy-start.31 = (pred[2]{0:T(512)(128)(4,1)S(1)}, pred[2]{0:T(512)(128)(4,1)}, u32[]{:S(2)}) copy-start(pred[2]{0:T(512)(128)(4,1)} %get-tuple-element.113) | copy-start | bytes 10
  499.7 17.8 %copy-start.24 = (f32[64,64]{1,0:T(8,128)S(1)}, f32[64,64]{1,0:T(8,128)}, u32[]{:S(2)}) copy-start(f32[64,64]{1,0:T(8,128)} %get-tuple-element.158) | copy-start | bytes 49156
  499.7 17.8 %copy-start.25 = (f32[64,64]{1,0:T(8,128)S(1)}, f32[64,64]{1,0:T(8,128)}, u32[]{:S(2)}) copy-start(f32[64,64]{1,0:T(8,128)} %get-tuple-element.160) | copy-start | bytes 49156
  499.7 17.9 %copy-start.22 = (f32[64,64]{1,0:T(8,128)S(1)}, f32[64,64]{1,0:T(8,128)}, u32[]{:S(2)}) copy-start(f32[64,64]{1,0:T(8,128)} %get-tuple-element.159) | copy-start | bytes 49156
  499.7 17.9 %copy-start.23 = (f32[64,64]{1,0:T(8,128)S(1)}, f32[64,64]{1,0:T(8,128)}, u32[]{:S(2)}) copy-start(f32[64,64]{1,0:T(8,128)} %get-tuple-element.161) | copy-start | bytes 49156

commit v8 on v7

--- a/solution.py
+++ b/solution.py
@@ -122,12 +122,6 @@
 
 def exchange(array):
     return lax.all_to_all(array, "seq", 0, 0, tiled=True)
-
-
-def pick(ids, table):
-    return jnp.einsum(
-        "sq,qte->ste", onehot(ids, table.shape[0]), table, preferred_element_type=jnp.float32
-    )
 
 
 def local(queries, key_states, value_states, positions, random_blocks, global_blocks, out_grad):
@@ -207,12 +201,19 @@
 
     k_table = own_blocks[0].transpose(0, 2, 1, 3).reshape(table_rows, BLK, HD)
     v_table = own_blocks[1].transpose(0, 2, 1, 3).reshape(table_rows, BLK, HD)
-    answers_k = pick(asked_flat, k_table).astype(jnp.bfloat16).reshape(seq_count, capacity * BLK, HD)
-    answers_k = jnp.concatenate(
-        [answers_k, jnp.broadcast_to(my_pieces.reshape(1, glob_rows, HD), (seq_count, glob_rows, HD))],
+    slab_table = jnp.concatenate(
+        [k_table.reshape(table_rows * BLK // glob_rows, glob_rows, HD), my_pieces.reshape(1, glob_rows, HD)]
+    )
+    slab_ids = (asked_part[:, :, None] * (BLK // glob_rows) + jnp.arange(BLK // glob_rows)[None, None, :])
+    slab_ids = jnp.concatenate(
+        [
+            slab_ids.reshape(seq_count, capacity * BLK // glob_rows),
+            jnp.full((seq_count, 1), table_rows * BLK // glob_rows, jnp.int32),
+        ],
         axis=1,
     )
-    answers_v = pick(asked_flat, v_table).astype(jnp.bfloat16).reshape(seq_count, capacity * BLK, HD)
+    answers_k = slab_table[slab_ids].reshape(seq_count, capacity * BLK + glob_rows, HD)
+    answers_v = v_table[asked_flat].reshape(seq_count, capacity * BLK, HD)
     padded = extended(paired, (("seq", 1),), BLK)
     answers_k, padded = lax.optimization_barrier((answers_k, padded))
     fetched_k = exchange(answers_k)
@@ -315,7 +316,9 @@
     to_owner = jnp.where(
         jnp.arange(seq_count)[:, None, None] == glob_owner[None, :, None], piece_sum[None], 0.0
     )
-    glob_grad = exchange(to_owner).transpose(1, 0, 2).reshape(GLOB, 2, BLK, kv_dev, HD)
+    to_owner = to_owner.reshape(seq_count, glob_rows, HD)
+    glob_grad = exchange(to_owner).reshape(seq_count, GLOB, piece)
+    glob_grad = glob_grad.transpose(1, 0, 2).reshape(GLOB, 2, BLK, kv_dev, HD)
 
     window_acc = jnp.pad(near_grad[:, :, 0], ((0, 0), (0, 2), (0, 0), (0, 0), (0, 0)))
     window_acc = window_acc + jnp.pad(near_grad[:, :, 1], ((0, 0), (1, 1), (0, 0), (0, 0), (0, 0)))

time: 527 us -> 532 us (level)
  local copies, waits for them, and re-layouts: 91.2 us -> 102 us
    gather x0 -> x2, local copies, waits for them, and re-layouts: none -> 10.1 us  [the longest x1 7.01 us: local(): slab_table[slab_ids].reshape(seq_count, capacity * BLK + glob_rows, HD)]
    convert_element_type x2 -> x0, local copies, waits for them, and re-layouts: 7.37 us -> none  [the longest x1 4.67 us: local(): pick(asked_flat, v_table).astype(jnp.bfloat16)]
    optimization_barrier x0 -> x1, local copies, waits for them, and re-layouts: none -> 7.04 us  [local(): answers_v, fetched_k = lax.optimization_barrier((answers_v, fetched_k))]
    unnamed x83 -> x85, local copies, waits for them, and re-layouts: 21.9 us -> 21.9 us
  transfers between devices with their start and end apart: 10 -> 10, of which waited for: 9 -> 9; matrix products, arithmetic and copies ran while one was open for 24% -> 25% of each run, Pallas kernels for 0% -> 0%
where the time goes in v8:
time: 532 us; the launch traced here: 522 us
  waiting for transfers between devices  268 us (50%)
  local copies, waits for them, and re-layouts  102 us (19%)
  starting transfers between devices  70.9 us (13%)
  matrix products  44 us (8%)
  other arithmetic  26.9 us (5%)
  between operations  10.2 us (2%)
    all_to_all x6, waiting for transfers between devices, exchange(): return lax.all_to_all(array, 'seq', 0, 0, tiled=True)  195 us
    ppermute x2, waiting for transfers between devices, shifted(): return lax.ppermute(array, axis, pairs)  70.3 us
    all_to_all x6, starting transfers between devices, exchange(): return lax.all_to_all(array, 'seq', 0, 0, tiled=True)  59.2 us
    unnamed x85, local copies, waits for them, and re-layouts  21.9 us
  transfers between devices with their start and end apart: 10, of which 9 were waited for; matrix products, arithmetic and copies ran while one was open for 25% of the time, Pallas kernels for 0%

profile of v8, /device:TPU:32, one launch (start us, length us, event | category | flops | bytes accessed | tf_op | source)
XLA Modules:
  0.0 521.9 jit_solution(9225400828427957710)
XLA Ops:
  14.7 15.0 %all-to-all-start = ((bf16[128,2,576]{2,1,0:T(2,128)(2,1)}), bf16[128,2,576]{2,1,0:T(2,128)(2,1)S(1)}, u32[]{:S(2)}, u32[]{:S(2)}) async-start(bf16[128,2,576]{2,1,0:T(2,128)(2,1)} %reshape.1226), calls=%async_computation | async-start | bytes 655360 | tf_op jit(solution)/shard_map/all_to_all | solution.py:124
  30.7 3.4 collective-permute-start
  34.1 2.5 collective-permute-start.1
  46.9 7.0 %gather_fusion.3 = bf16[2176,8,128]{2,1,0:T(8,128)(2,1)} fusion(bf16[129,8,128]{2,1,0:T(8,128)(2,1)S(1)} %pad_maximum_fusion.6, s32[3072]{0:T(1024)S(1)} %pad_clamp_fusion), kind=kCustom, calls=%fused_computation.3 | custom fusion | bytes 8921600 | tf_op jit(solution)/shard_map/gather | solution.py:215
  53.9 14.0 %all-to-all-start.1 = ((bf16[128,136,128]{2,1,0:T(8,128)(2,1)}), bf16[128,136,128]{2,1,0:T(8,128)(2,1)}, u32[]{:S(2)}, u32[]{:S(2)}) async-start(bf16[128,136,128]{2,1,0:T(8,128)(2,1)} %bitcast.283), calls=%async_computation.1 | async-start | bytes 8912896 | tf_op jit(solution)/shard_map/all_to_all | solution.py:124
  68.3 3.1 gather_fusion.4
  71.3 99.0 %all-to-all-done.1 = bf16[128,136,128]{2,1,0:T(8,128)(2,1)} async-done(((bf16[128,136,128]{2,1,0:T(8,128)(2,1)}), bf16[128,136,128]{2,1,0:T(8,128)(2,1)}, u32[]{:S(2)}, u32[]{:S(2)}) %all-to-all-start.1) | async-done | bytes 4456480 | tf_op jit(solution)/shard_map/all_to_all | solution.py:124
  170.4 8.1 %all-to-all-start.2 = ((bf16[128,128,128]{2,1,0:T(8,128)(2,1)}), bf16[128,128,128]{2,1,0:T(8,128)(2,1)}, u32[]{:S(2)}, u32[]{:S(2)}) async-start(bf16[128,128,128]{2,1,0:T(8,128)(2,1)} %bitcast.284), calls=%async_computation.2 | async-start | bytes 8388608 | tf_op jit(solution)/shard_map/all_to_all | solution.py:124
  189.6 4.7 slice.375
  194.4 7.0 %copy.317 = bf16[128,136,128]{0,2,1:T(8,128)(2,1)} copy(bf16[128,136,128]{2,1,0:T(8,128)(2,1)} %all-to-all-done.1) | data formatting | bytes 8912896 | tf_op jit(solution)/shard_map/optimization_barrier | solution.py:220
  202.7 2.9 gather_fusion.5
  212.5 2.0 fusion.5
  214.5 3.4 bitcast_convert_fusion
  219.2 4.7 copy.345
  224.0 49.3 %all-to-all-done.2 = bf16[128,128,128]{2,1,0:T(8,128)(2,1)} async-done(((bf16[128,128,128]{2,1,0:T(8,128)(2,1)}), bf16[128,128,128]{2,1,0:T(8,128)(2,1)}, u32[]{:S(2)}, u32[]{:S(2)}) %all-to-all-start.2) | async-done | bytes 4194336 | tf_op jit(solution)/shard_map/all_to_all | solution.py:124
  273.3 7.8 %all-to-all-start.4 = ((bf16[128,128,128]{2,1,0:T(8,128)(2,1)}), bf16[128,128,128]{2,1,0:T(8,128)(2,1)}, u32[]{:S(2)}, u32[]{:S(2)}) async-start(bf16[128,128,128]{2,1,0:T(8,128)(2,1)} %bitcast.285), calls=%async_computation.4 | async-start | bytes 8388608 | tf_op jit(solution)/shard_map/all_to_all | solution.py:124
  281.1 5.3 %fusion.20 = f32[4,4,128,4,64]{2,4,3,1,0:T(8,128)} fusion(bf16[4,320,4,128,1]{3,1,4,2,0:T(8,128)(2,1)} %bitcast.307, f32[4,4,320,64,4]{2,3,4,1,0:T(8,128)} %copy-done, f32[4,4,4,64]{3,2,1,0:T(4,128)S(1)} %add.365, f32[4,4,4,64]{3,2,1,0:T(4,128)S(1)} %max.8, pred[4,320]{1,0:T(4,128)(4,1)S(1)} %broadcast_in_dim.269), kind=kOutput, calls=%fused_computation.47 | convolution fusion | flops 342097920 | bytes 8684800 | tf_op jit(solution)/shard_map/rhgtk,rkhd->rthgd/dot_general | solution.py:279
  286.3 6.0 %fusion.18 = f32[4,4,320,128,1]{3,2,4,1,0:T(8,128)} fusion(bf16[4,64,4,4,128]{4,3,2,1,0:T(4,128)(2,1)S(1)} %copy-done.18, f32[4,4,320,64,4]{2,3,4,1,0:T(8,128)} %copy-done, f32[4,4,4,64]{3,2,1,0:T(4,128)S(1)} %add.365, f32[4,4,4,64]{3,2,1,0:T(4,128)S(1)} %max.8, pred[4,320]{1,0:T(4,128)(4,1)S(1)} %broadcast_in_dim.269), kind=kOutput, calls=%fused_computation.45 | convolution fusion | flops 342097920 | bytes 8946944 | tf_op jit(solution)/shard_map/rhgtk,rthgd->rkhd/dot_general | solution.py:295
  292.3 2.9 gather_fusion.6
  295.3 5.0 multiply_reduce_fusion
  300.3 5.0 fusion.2
  306.4 2.3 copy-done.2
  308.9 2.3 fusion.12
  312.2 2.8 fusion.77
  315.0 3.1 copy.365
  318.1 3.2 copy.364
  321.3 2.9 fusion.85
  324.2 1.9 copy_dynamic-update-slice_fusion.1
  326.2 2.1 copy_dynamic-update-slice_fusion
  328.3 2.4 copy-done.4
  331.8 2.0 reshape.1127
  333.9 2.3 copy.336
  336.1 2.3 reshape.1128
  340.6 2.9 copy.331
  345.1 2.4 pad_maximum_fusion
  347.4 25.9 %all-to-all-done.4 = bf16[128,128,128]{2,1,0:T(8,128)(2,1)} async-done(((bf16[128,128,128]{2,1,0:T(8,128)(2,1)}), bf16[128,128,128]{2,1,0:T(8,128)(2,1)}, u32[]{:S(2)}, u32[]{:S(2)}) %all-to-all-start.4) | async-done | bytes 4194336 | tf_op jit(solution)/shard_map/all_to_all | solution.py:124
  373.4 7.7 %all-to-all-start.3 = ((bf16[128,144,128]{2,1,0:T(8,128)(2,1)}), bf16[128,144,128]{2,1,0:T(8,128)(2,1)}, u32[]{:S(2)}, u32[]{:S(2)}) async-start(bf16[128,144,128]{2,1,0:T(8,128)(2,1)} %pad_maximum_fusion), calls=%async_computation.3 | async-start | bytes 9437184 | tf_op jit(solution)/shard_map/all_to_all | solution.py:124
  388.0 2.2 slice_bitcast_fusion.2
  391.6 3.0 collective-permute-start.2
  394.6 4.6 fusion.26
  401.5 2.9 collective-permute-start.3
  404.5 2.5 copy.353
  407.0 70.3 %collective-permute-done.2 = bf16[2,64,4,128]{3,2,1,0:T(4,128)(2,1)S(1)} collective-permute-done((bf16[2,64,4,128]{3,2,1,0:T(4,128)(2,1)}, bf16[2,64,4,128]{3,2,1,0:T(4,128)(2,1)S(1)}, u32[]{:S(2)}, u32[]{:S(2)}) %collective-permute-start.2) | collective-permute-done | bytes 131104 | tf_op jit(solution)/shard_map/ppermute | solution.py:40
  477.6 7.2 %all-to-all-done.3 = bf16[128,144,128]{2,1,0:T(8,128)(2,1)} async-done(((bf16[128,144,128]{2,1,0:T(8,128)(2,1)}), bf16[128,144,128]{2,1,0:T(8,128)(2,1)}, u32[]{:S(2)}, u32[]{:S(2)}) %all-to-all-start.3) | async-done | bytes 4718624 | tf_op jit(solution)/shard_map/all_to_all | solution.py:124
  486.1 2.5 slice.457
  488.6 2.4 fusion.23
  492.0 6.6 %all-to-all-start.5 = ((f32[128,8,128]{2,1,0:T(8,128)}), f32[128,8,128]{2,1,0:T(8,128)S(1)}, u32[]{:S(2)}, u32[]{:S(2)}) async-start(f32[128,8,128]{2,1,0:T(8,128)} %broadcast_select_fusion.1), calls=%async_computation.5 | async-start | bytes 1048576 | tf_op jit(solution)/shard_map/all_to_all | solution.py:124
  501.1 13.5 %all-to-all-done.5 = f32[128,8,128]{2,1,0:T(8,128)S(1)} async-done(((f32[128,8,128]{2,1,0:T(8,128)}), f32[128,8,128]{2,1,0:T(8,128)S(1)}, u32[]{:S(2)}, u32[]{:S(2)}) %all-to-all-start.5) | async-done | bytes 524320 | tf_op jit(solution)/shard_map/all_to_all | solution.py:124
  (233 shorter events, 67.5 us)
Async XLA Ops:
  6.7 23.0 %copy-start.28 = (s32[3,256]{1,0:T(4,128)S(1)}, s32[3,256]{1,0:T(4,128)}, u32[]{:S(2)}) copy-start(s32[3,256]{1,0:T(4,128)} %param.22) | copy-start | bytes 9220
  6.7 23.1 %copy-start.8 = (bf16[256,512]{1,0:T(8,128)(2,1)S(1)}, bf16[256,512]{1,0:T(8,128)(2,1)}, u32[]{:S(2)}) copy-start(bf16[256,512]{1,0:T(8,128)(2,1)} %param.20) | copy-start | bytes 786436
  10.2 20.2 %copy-start.5 = (bf16[256,512]{1,0:T(8,128)(2,1)S(1)}, bf16[256,512]{1,0:T(8,128)(2,1)}, u32[]{:S(2)}) copy-start(bf16[256,512]{1,0:T(8,128)(2,1)} %param.21) | copy-start | bytes 786436
  14.7 31.0 %all-to-all-start = ((bf16[128,2,576]{2,1,0:T(2,128)(2,1)}), bf16[128,2,576]{2,1,0:T(2,128)(2,1)S(1)}, u32[]{:S(2)}, u32[]{:S(2)}) async-start(bf16[128,2,576]{2,1,0:T(2,128)(2,1)} %reshape.1226), calls=%async_computation | async-start | bytes 655360 | tf_op jit(solution)/shard_map/all_to_all | solution.py:124
  30.7 12.2 %collective-permute-start = (bf16[2,64,512]{1,2,0:T(8,128)(2,1)S(1)}, bf16[2,64,512]{1,2,0:T(8,128)(2,1)S(1)}, u32[]{:S(2)}, u32[]{:S(2)}) collective-permute-start(bf16[2,64,512]{1,2,0:T(8,128)(2,1)S(1)} %get-tuple-element.154), channel_id=1, source_target_pairs={{0,2},{2,4},{4,6},{6,8},{8,10},{10,12},{12,14},{14,16},{16,18},{18... | collective-permute-start | bytes 393224 | tf_op jit(solution)/shard_map/ppermute | solution.py:26
  34.1 9.9 %collective-permute-start.1 = (bf16[2,64,512]{1,2,0:T(8,128)(2,1)S(1)}, bf16[2,64,512]{1,2,0:T(8,128)(2,1)S(1)}, u32[]{:S(2)}, u32[]{:S(2)}) collective-permute-start(bf16[2,64,512]{1,2,0:T(8,128)(2,1)S(1)} %get-tuple-element.155), channel_id=1, source_target_pairs={{2,0},{4,2},{6,4},{8,6},{10,8},{12,10},{14,12},{16,14},{18,16},{20... | collective-permute-start | bytes 393224 | tf_op jit(solution)/shard_map/ppermute | solution.py:27
  53.9 116.4 %all-to-all-start.1 = ((bf16[128,136,128]{2,1,0:T(8,128)(2,1)}), bf16[128,136,128]{2,1,0:T(8,128)(2,1)}, u32[]{:S(2)}, u32[]{:S(2)}) async-start(bf16[128,136,128]{2,1,0:T(8,128)(2,1)} %bitcast.283), calls=%async_computation.1 | async-start | bytes 8912896 | tf_op jit(solution)/shard_map/all_to_all | solution.py:124
  170.4 8.5 %copy-start.14 = (bf16[256,2048]{1,0:T(8,128)(2,1)S(1)}, bf16[256,2048]{1,0:T(8,128)(2,1)}, u32[]{:S(2)}) copy-start(bf16[256,2048]{1,0:T(8,128)(2,1)} %param.25) | copy-start | bytes 3145732
  170.4 10.0 %copy-start.15 = (bf16[256,2048]{1,0:T(8,128)(2,1)S(1)}, bf16[256,2048]{1,0:T(8,128)(2,1)}, u32[]{:S(2)}) copy-start(bf16[256,2048]{1,0:T(8,128)(2,1)} %param.19) | copy-start | bytes 3145732
  170.4 102.9 %all-to-all-start.2 = ((bf16[128,128,128]{2,1,0:T(8,128)(2,1)}), bf16[128,128,128]{2,1,0:T(8,128)(2,1)}, u32[]{:S(2)}, u32[]{:S(2)}) async-start(bf16[128,128,128]{2,1,0:T(8,128)(2,1)} %bitcast.284), calls=%async_computation.2 | async-start | bytes 8388608 | tf_op jit(solution)/shard_map/all_to_all | solution.py:124
  205.6 3.4 copy-start.6
  209.8 4.7 copy-start.1
  210.9 3.5 copy-start
  212.5 2.0 copy-start.17
  273.3 100.1 %all-to-all-start.4 = ((bf16[128,128,128]{2,1,0:T(8,128)(2,1)}), bf16[128,128,128]{2,1,0:T(8,128)(2,1)}, u32[]{:S(2)}, u32[]{:S(2)}) async-start(bf16[128,128,128]{2,1,0:T(8,128)(2,1)} %bitcast.285), calls=%async_computation.4 | async-start | bytes 8388608 | tf_op jit(solution)/shard_map/all_to_all | solution.py:124
  281.1 5.3 %copy-start.18 = (bf16[4,64,4,4,128]{4,3,2,1,0:T(4,128)(2,1)S(1)}, bf16[4,64,4,4,128]{4,3,2,1,0:T(4,128)(2,1)}, u32[]{:S(2)}) copy-start(bf16[4,64,4,4,128]{4,3,2,1,0:T(4,128)(2,1)} %reshape.1124) | copy-start | bytes 3145732
  295.2 5.1 copy-start.20
  295.2 5.1 copy-start.13
  295.3 5.1 copy-start.19
  305.3 5.8 %copy-start.3 = (bf16[4,4,4,64,320]{4,3,2,1,0:T(8,128)(2,1)}, bf16[4,4,4,64,320]{4,3,2,1,0:T(8,128)(2,1)S(1)}, u32[]{:S(2)}) copy-start(bf16[4,4,4,64,320]{4,3,2,1,0:T(8,128)(2,1)S(1)} %fusion.2) | copy-start | bytes 7864324
  305.3 3.3 copy-start.2
  305.4 3.5 copy-start.21
  308.9 2.3 copy-start.7
  324.2 2.0 copy-start.11
  328.3 2.4 copy-start.4
  340.6 2.9 copy-start.9
  340.6 2.9 copy-start.10
  343.6 1.4 copy-start.12
  347.4 33.7 %copy-start.32 = (s32[2]{0:T(128)S(1)}, s32[2]{0:T(128)}, u32[]{:S(2)}) copy-start(s32[2]{0:T(128)} %get-tuple-element.124) | copy-start | bytes 28
  347.4 38.4 %copy-start.33 = (s32[4]{0:T(128)S(1)}, s32[4]{0:T(128)}, u32[]{:S(2)}) copy-start(s32[4]{0:T(128)} %constant.262.clone.1) | copy-start | bytes 52
  373.4 111.4 %all-to-all-start.3 = ((bf16[128,144,128]{2,1,0:T(8,128)(2,1)}), bf16[128,144,128]{2,1,0:T(8,128)(2,1)}, u32[]{:S(2)}, u32[]{:S(2)}) async-start(bf16[128,144,128]{2,1,0:T(8,128)(2,1)} %pad_maximum_fusion), calls=%async_computation.3 | async-start | bytes 9437184 | tf_op jit(solution)/shard_map/all_to_all | solution.py:124
  385.8 8.7 %copy-start.26 = (s32[4,4]{1,0:T(4,128)}, s32[4,4]{1,0:T(4,128)S(1)}, u32[]{:S(2)}) copy-start(s32[4,4]{1,0:T(4,128)S(1)} %multiply_add_fusion.4) | copy-start | bytes 196
  388.0 6.5 %copy-start.29 = (s32[256]{0:T(256)}, s32[256]{0:T(256)S(1)}, u32[]{:S(2)}) copy-start(s32[256]{0:T(256)S(1)} %eq.148) | copy-start | bytes 3076
  390.2 8.9 %copy-start.16 = (bf16[4,64,4,4,128]{4,1,3,2,0:T(8,128)(2,1)S(1)}, bf16[4,64,4,4,128]{4,1,3,2,0:T(8,128)(2,1)}, u32[]{:S(2)}) copy-start(bf16[4,64,4,4,128]{4,1,3,2,0:T(8,128)(2,1)} %get-tuple-element.184) | copy-start | bytes 3145732
  391.6 85.7 %collective-permute-start.2 = (bf16[2,64,4,128]{3,2,1,0:T(4,128)(2,1)}, bf16[2,64,4,128]{3,2,1,0:T(4,128)(2,1)S(1)}, u32[]{:S(2)}, u32[]{:S(2)}) collective-permute-start(bf16[2,64,4,128]{3,2,1,0:T(4,128)(2,1)} %get-tuple-element.140), channel_id=1, source_target_pairs={{2,0},{4,2},{6,4},{8,6},{10,8},{12,10},{14,12},{16,14},{18,16},{20... | collective-permute-start | bytes 393224 | tf_op jit(solution)/shard_map/ppermute | solution.py:40
  401.5 75.9 %collective-permute-start.3 = (bf16[2,64,4,128]{3,2,1,0:T(4,128)(2,1)}, bf16[2,64,4,128]{3,2,1,0:T(4,128)(2,1)S(1)}, u32[]{:S(2)}, u32[]{:S(2)}) collective-permute-start(bf16[2,64,4,128]{3,2,1,0:T(4,128)(2,1)} %get-tuple-element.139), channel_id=1, source_target_pairs={{0,2},{2,4},{4,6},{6,8},{8,10},{10,12},{12,14},{14,16},{16,18},{18... | collective-permute-start | bytes 393224 | tf_op jit(solution)/shard_map/ppermute | solution.py:40
  486.1 2.5 copy-start.27
  486.1 2.5 copy-start.30
  492.0 22.7 %all-to-all-start.5 = ((f32[128,8,128]{2,1,0:T(8,128)}), f32[128,8,128]{2,1,0:T(8,128)S(1)}, u32[]{:S(2)}, u32[]{:S(2)}) async-start(f32[128,8,128]{2,1,0:T(8,128)} %broadcast_select_fusion.1), calls=%async_computation.5 | async-start | bytes 1048576 | tf_op jit(solution)/shard_map/all_to_all | solution.py:124
  500.3 15.0 %copy-start.31 = (pred[2]{0:T(512)(128)(4,1)S(1)}, pred[2]{0:T(512)(128)(4,1)}, u32[]{:S(2)}) copy-start(pred[2]{0:T(512)(128)(4,1)} %get-tuple-element.117) | copy-start | bytes 10
  500.9 17.8 %copy-start.24 = (f32[64,64]{1,0:T(8,128)S(1)}, f32[64,64]{1,0:T(8,128)}, u32[]{:S(2)}) copy-start(f32[64,64]{1,0:T(8,128)} %get-tuple-element.162) | copy-start | bytes 49156
  500.9 17.8 %copy-start.25 = (f32[64,64]{1,0:T(8,128)S(1)}, f32[64,64]{1,0:T(8,128)}, u32[]{:S(2)}) copy-start(f32[64,64]{1,0:T(8,128)} %get-tuple-element.164) | copy-start | bytes 49156
  500.9 18.0 %copy-start.22 = (f32[64,64]{1,0:T(8,128)S(1)}, f32[64,64]{1,0:T(8,128)}, u32[]{:S(2)}) copy-start(f32[64,64]{1,0:T(8,128)} %get-tuple-element.163) | copy-start | bytes 49156
  500.9 18.0 %copy-start.23 = (f32[64,64]{1,0:T(8,128)S(1)}, f32[64,64]{1,0:T(8,128)}, u32[]{:S(2)}) copy-start(f32[64,64]{1,0:T(8,128)} %get-tuple-element.165) | copy-start | bytes 49156
